TPU v7x, 32 devices: a whole 2x2x4 slice. The times are simulated.
32 devices in a mesh: rec: 2 (over core), space: 16 (over z, y, x).
Axes of the slice: x: 2, y: 2, z: 4, core: 2. Of those that a mesh axis runs over, the one named last changes fastest.
Arguments:
- footprints: bfloat16 [32, 120, 8400], P(('rec', 'space')), may hold values from 0 to 1
- time_cov: bfloat16 [120, 120], replicated, may hold values from -1 to 3
- lat_cov: bfloat16 [70, 70], replicated, may hold values from -1 to 3
- lon_cov: bfloat16 [120, 120], replicated, may hold values from -1 to 3
Outputs:
- gram: float32 [32, 32], P(('rec', 'space'))
All inputs are finite; a program needn't handle non-finite values.
Results may differ from a plain program's by a relative error of at most 0.0003.
Values may be sent and summed in bfloat16 or wider, within the bound.
No kernel may reach another device: no remote copies, remote signals or barrier semaphores. Data moves between devices by JAX's collectives and lax.ppermute only.
A program may use at most 64 MiB of HBM per device.

v0:
```python
import jax
import jax.numpy as jnp
from jax import lax
from jax.sharding import PartitionSpec as P


def weigh_footprints(footprints, time_cov, lat_cov, lon_cov):
    receptors_here, time_count, cell_count = footprints.shape
    lat_count = lat_cov.shape[0]
    lon_count = lon_cov.shape[0]
    along_lon = jnp.dot(
        footprints.reshape(receptors_here * time_count * lat_count, lon_count),
        lon_cov,
        preferred_element_type=jnp.float32,
    ).astype(jnp.bfloat16)
    along_lat = jnp.einsum(
        "rab,ac->rcb",
        along_lon.reshape(receptors_here * time_count, lat_count, lon_count),
        lat_cov,
        preferred_element_type=jnp.float32,
    ).astype(jnp.bfloat16)
    return jnp.einsum(
        "rtc,ts->rsc",
        along_lat.reshape(receptors_here, time_count, cell_count),
        time_cov,
        preferred_element_type=jnp.float32,
    ).astype(jnp.bfloat16)


def flatten_padded(values, devices):
    receptors_here = values.shape[0]
    flat = values.reshape(receptors_here, -1)
    length = flat.shape[1]
    per_device = -(-length // devices)
    per_device = -(-per_device // 128) * 128
    return jnp.pad(flat, ((0, 0), (0, per_device * devices - length)))


def regroup(values):
    moved = (
        lax.all_to_all(
            lax.all_to_all(values[0], "space", split_axis=1, concat_axis=0, tiled=True),
            "rec",
            split_axis=1,
            concat_axis=0,
            tiled=True,
        ),
        lax.all_to_all(
            lax.all_to_all(values[1], "space", split_axis=1, concat_axis=0, tiled=True),
            "rec",
            split_axis=1,
            concat_axis=0,
            tiled=True,
        ),
    )
    return moved


def local(footprints, time_cov, lat_cov, lon_cov):
    rec_count = lax.axis_size("rec")
    space_count = lax.axis_size("space")
    devices = rec_count * space_count
    plain = flatten_padded(footprints, devices)
    weighted = flatten_padded(weigh_footprints(footprints, time_cov, lat_cov, lon_cov), devices)
    weighted_all, plain_all = regroup((weighted, plain))
    partial_value = lax.dot_general(
        weighted_all, plain_all, (((1,), (1,)), ((), ())), preferred_element_type=jnp.float32
    )
    return lax.psum_scatter(partial_value, ("rec", "space"), scatter_dimension=0, tiled=True)


def solution(mesh):
    in_specs = (P(("rec", "space"), None, None), P(), P(), P())
    out_specs = P(("rec", "space"), None)
    return jax.shard_map(local, mesh=mesh, in_specs=in_specs, out_specs=out_specs, check_vma=False)
```

profile of v0, /device:TPU:0, one launch (start us, length us, event | category | flops | bytes accessed | tf_op | source)
XLA Modules:
  0.0 254.2 jit_solution(8349191223248169489)
XLA Ops:
  0.0 5.8 %reshape.41 = bf16[8400,120]{1,0:T(8,128)(2,1)S(1)} reshape(bf16[1,120,8400]{2,1,0:T(8,128)(2,1)} %param.4) | data formatting | bytes 4032000 | tf_op jit(solution)/shard_map/reshape | solution.py:12
  7.9 4.1 %copy.15 = bf16[8400,120]{1,0:T(8,128)(2,1)} copy(bf16[8400,120]{0,1:T(8,128)(2,1)} %convolution_convert_fusion.1) | data formatting | bytes 4032000 | tf_op jit(solution)/shard_map/convert_element_type | solution.py:15
  12.0 2.8 %reshape.42 = bf16[120,70,120]{2,1,0:T(8,128)(2,1)S(1)} reshape(bf16[8400,120]{1,0:T(8,128)(2,1)} %copy.15) | data formatting | bytes 4032000 | tf_op jit(solution)/shard_map/reshape | solution.py:18
  14.8 2.2 convert_bitcast_fusion
  17.0 3.6 %copy.17 = bf16[120,70,120]{0,2,1:T(8,128)(2,1)S(1)} copy(bf16[120,70,120]{2,1,0:T(8,128)(2,1)} %convert_bitcast_fusion) | data formatting | bytes 4032000 | tf_op jit(solution)/shard_map/convert_element_type | solution.py:21
  22.7 4.7 %reshape.49 = bf16[1008000]{0:T(1024)(128)(2,1)S(1)} reshape(bf16[120,8400]{1,0:T(8,128)(2,1)} %fusion) | data formatting | bytes 4032000
  27.4 23.2 %reshape.44 = bf16[1,1008000]{1,0:T(2,128)(2,1)S(1)} reshape(bf16[1008000]{0:T(1024)(128)(2,1)S(1)} %reshape.49) | data formatting | bytes 4032000 | tf_op jit(solution)/shard_map/reshape | solution.py:32
  50.6 5.9 %pad.7 = bf16[1,1011712]{1,0:T(2,128)(2,1)} pad(bf16[1,1008000]{1,0:T(2,128)(2,1)S(1)} %reshape.44, bf16[]{:T(256)} %constant.2.clone.1), padding=0_0x0_3712 | pad | bytes 4039426 | tf_op jit(solution)/shard_map/jit(_pad)/pad | solution.py:36
  57.0 12.8 %reduce.4 = bf16[16,63232]{1,0:T(8,128)(2,1)S(1)} reduce(bf16[16,1,63232]{2,1,0:T(2,128)(2,1)} %bitcast.37, bf16[]{:T(256)} %broadcast.6), dimensions={1}, to_apply=%bitcast.22.reduce_sub_computation | reduce | bytes 4046850
  71.4 8.5 %all-to-all-start = ((bf16[16,2,31616]{2,1,0:T(2,128)(2,1)}), bf16[16,2,31616]{2,1,0:T(2,128)(2,1)}, u32[]{:S(2)}, u32[]{:S(2)}) async-start(bf16[16,2,31616]{2,1,0:T(2,128)(2,1)} %reshape.53), calls=%async_computation | async-start | bytes 4046848 | tf_op jit(solution)/shard_map/all_to_all | solution.py:42
  79.9 5.0 %reshape.51 = bf16[1008000]{0:T(1024)(128)(2,1)} reshape(bf16[1,120,8400]{2,1,0:T(8,128)(2,1)S(1)} %copy-done.2) | data formatting | bytes 4032000
  84.9 20.0 %reshape.45 = bf16[1,1008000]{1,0:T(2,128)(2,1)S(1)} reshape(bf16[1008000]{0:T(1024)(128)(2,1)} %reshape.51) | data formatting | bytes 4032000 | tf_op jit(solution)/shard_map/reshape | solution.py:32
  104.8 5.9 %pad.8 = bf16[1,1011712]{1,0:T(2,128)(2,1)} pad(bf16[1,1008000]{1,0:T(2,128)(2,1)S(1)} %reshape.45, bf16[]{:T(256)} %constant.2.clone.1), padding=0_0x0_3712 | pad | bytes 4039426 | tf_op jit(solution)/shard_map/jit(_pad)/pad | solution.py:36
  110.7 12.8 %reduce.5 = bf16[16,63232]{1,0:T(8,128)(2,1)S(1)} reduce(bf16[16,1,63232]{2,1,0:T(2,128)(2,1)} %bitcast.38, bf16[]{:T(256)} %broadcast.6), dimensions={1}, to_apply=%bitcast.24.reduce_sub_computation | reduce | bytes 4046850
  125.2 6.8 %all-to-all-start.2 = ((bf16[16,2,31616]{2,1,0:T(2,128)(2,1)}), bf16[16,2,31616]{2,1,0:T(2,128)(2,1)S(1)}, u32[]{:S(2)}, u32[]{:S(2)}) async-start(bf16[16,2,31616]{2,1,0:T(2,128)(2,1)} %reshape.55), calls=%async_computation.2 | async-start | bytes 4046848 | tf_op jit(solution)/shard_map/all_to_all | solution.py:49
  132.0 12.4 %reshape.54 = bf16[16,1,63232]{2,1,0:T(2,128)(2,1)} reshape(bf16[16,2,31616]{2,1,0:T(2,128)(2,1)} %all-to-all-done) | data formatting | bytes 4046848
  144.4 13.2 %bitcast_reduce_fusion.1 = bf16[16,63232]{1,0:T(8,128)(2,1)S(1)} fusion(bf16[16,1,63232]{2,1,0:T(2,128)(2,1)} %reshape.54), kind=kLoop, calls=%fused_computation.9 | loop fusion | bytes 4046848 | tf_op jit(solution)/shard_map/all_to_all | solution.py:42
  159.0 14.5 %all-to-all-done.2 = bf16[16,2,31616]{2,1,0:T(2,128)(2,1)S(1)} async-done(((bf16[16,2,31616]{2,1,0:T(2,128)(2,1)}), bf16[16,2,31616]{2,1,0:T(2,128)(2,1)S(1)}, u32[]{:S(2)}, u32[]{:S(2)}) %all-to-all-start.2) | async-done | bytes 2023456 | tf_op jit(solution)/shard_map/all_to_all | solution.py:49
  173.6 5.0 %all-to-all-start.1 = ((bf16[16,2,31616]{2,0,1:T(8,128)(2,1)}), bf16[16,2,31616]{2,0,1:T(8,128)(2,1)}, u32[]{:S(2)}, u32[]{:S(2)}) async-start(bf16[16,2,31616]{2,0,1:T(8,128)(2,1)} %bitcast.42), calls=%async_computation.1 | async-start | bytes 4046848 | tf_op jit(solution)/shard_map/all_to_all | solution.py:41
  178.6 9.0 %reshape.56 = bf16[16,1,63232]{2,1,0:T(2,128)(2,1)} reshape(bf16[16,2,31616]{2,1,0:T(2,128)(2,1)S(1)} %all-to-all-done.2) | data formatting | bytes 4046848
  187.6 13.2 %bitcast_reduce_fusion = bf16[16,63232]{1,0:T(8,128)(2,1)S(1)} fusion(bf16[16,1,63232]{2,1,0:T(2,128)(2,1)} %reshape.56), kind=kLoop, calls=%fused_computation.8 | loop fusion | bytes 4046848 | tf_op jit(solution)/shard_map/all_to_all | solution.py:49
  200.9 5.4 %all_to_all.64 = bf16[16,2,31616]{2,0,1:T(8,128)(2,1)S(1)} all-to-all(bf16[16,2,31616]{2,0,1:T(8,128)(2,1)S(1)} %bitcast.43), channel_id=1, replica_groups=mesh['rec'=2,'space'=16] {'rec'}, dimensions={1} | all-to-all | bytes 4046848 | tf_op jit(solution)/shard_map/all_to_all | solution.py:48
  206.3 2.3 fusion.2
  208.7 45.1 %all-reduce.2 = f32[32,32]{1,0:T(8,128)S(1)} all-reduce(f32[32,32]{1,0:T(8,128)S(1)} %fusion.2), channel_id=2, replica_groups=mesh['rec'=2,'space'=16] {'rec','space'}, use_global_device_ids=true, to_apply=%region_0.1.clone | all-reduce | flops 1024 | bytes 8192
  (20 shorter events, 10.1 us)
Async XLA Ops:
  0.0 5.8 %copy-start = (bf16[120,120]{1,0:T(8,128)(2,1)S(1)}, bf16[120,120]{1,0:T(8,128)(2,1)}, u32[]{:S(2)}) copy-start(bf16[120,120]{1,0:T(8,128)(2,1)} %param.7) | copy-start | bytes 86404
  12.0 2.8 %copy-start.4 = (bf16[70,70]{1,0:T(8,128)(2,1)S(1)}, bf16[70,70]{1,0:T(8,128)(2,1)}, u32[]{:S(2)}) copy-start(bf16[70,70]{1,0:T(8,128)(2,1)} %param.6) | copy-start | bytes 29404
  17.0 3.6 %copy-start.3 = (bf16[120,120]{1,0:T(8,128)(2,1)S(1)}, bf16[120,120]{1,0:T(8,128)(2,1)}, u32[]{:S(2)}) copy-start(bf16[120,120]{1,0:T(8,128)(2,1)} %param.5) | copy-start | bytes 86404
  71.4 8.5 %copy-start.2 = (bf16[1,120,8400]{2,1,0:T(8,128)(2,1)S(1)}, bf16[1,120,8400]{2,1,0:T(8,128)(2,1)}, u32[]{:S(2)}) copy-start(bf16[1,120,8400]{2,1,0:T(8,128)(2,1)} %param.4) | copy-start | bytes 6048004
  71.4 53.8 %all-to-all-start = ((bf16[16,2,31616]{2,1,0:T(2,128)(2,1)}), bf16[16,2,31616]{2,1,0:T(2,128)(2,1)}, u32[]{:S(2)}, u32[]{:S(2)}) async-start(bf16[16,2,31616]{2,1,0:T(2,128)(2,1)} %reshape.53), calls=%async_computation | async-start | bytes 4046848 | tf_op jit(solution)/shard_map/all_to_all | solution.py:42
  125.2 48.4 %all-to-all-start.2 = ((bf16[16,2,31616]{2,1,0:T(2,128)(2,1)}), bf16[16,2,31616]{2,1,0:T(2,128)(2,1)S(1)}, u32[]{:S(2)}, u32[]{:S(2)}) async-start(bf16[16,2,31616]{2,1,0:T(2,128)(2,1)} %reshape.55), calls=%async_computation.2 | async-start | bytes 4046848 | tf_op jit(solution)/shard_map/all_to_all | solution.py:49
  173.6 27.4 %all-to-all-start.1 = ((bf16[16,2,31616]{2,0,1:T(8,128)(2,1)}), bf16[16,2,31616]{2,0,1:T(8,128)(2,1)}, u32[]{:S(2)}, u32[]{:S(2)}) async-start(bf16[16,2,31616]{2,0,1:T(8,128)(2,1)} %bitcast.42), calls=%async_computation.1 | async-start | bytes 4046848 | tf_op jit(solution)/shard_map/all_to_all | solution.py:41
  206.3 47.9 %copy-start.1 = (bf16[120,120]{1,0:T(8,128)(2,1)S(1)}, bf16[120,120]{1,0:T(8,128)(2,1)}, u32[]{:S(2)}) copy-start(bf16[120,120]{1,0:T(8,128)(2,1)} %param.7) | copy-start | bytes 86404
where the time goes:
time: 255 us; the launch traced here: 254 us
  local copies, waits for them, and re-layouts  134 us (53%)
  blocking collectives  50.4 us (20%)
  other arithmetic  25.6 us (10%)
  starting transfers between devices  20.4 us (8%)
  waiting for transfers between devices  14.5 us (6%)
  matrix products  8.68 us (3%)
    unnamed x1, blocking collectives  45.1 us
    reshape x2, local copies, waits for them, and re-layouts, flatten_padded(): flat = values.reshape(receptors_here, -1)  43.2 us
    unnamed x18, local copies, waits for them, and re-layouts  35.3 us
    unnamed x2, other arithmetic  25.6 us
    all_to_all x1, waiting for transfers between devices, regroup(): lax.all_to_all(values[1], 'space', split_axis=1, concat_axis=0, tiled=True)  14.5 us
    all_to_all x1, local copies, waits for them, and re-layouts, regroup(): lax.all_to_all(values[0], 'space', split_axis=1, concat_axis=0, tiled=True)  13.2 us
    all_to_all x1, local copies, waits for them, and re-layouts, regroup(): lax.all_to_all(values[1], 'space', split_axis=1, concat_axis=0, tiled=True)  13.2 us
    pad x2, local copies, waits for them, and re-layouts, flatten_padded(): return jnp.pad(flat, ((0, 0), (0, per_device * devices - length)))  11.7 us
  transfers between devices with their start and end apart: 3, of which 1 were waited for; matrix products, arithmetic and copies ran while one was open for 37% of the time, Pallas kernels for 0%

commit v1 on v0

v1 whole, which is shorter than its diff:
```python
import jax
import jax.numpy as jnp
from jax import lax
from jax.sharding import PartitionSpec as P

ROW_TILE = 16
LANE = 128


def weigh_footprints(footprints, time_cov, lat_cov, lon_cov):
    receptors_here, time_count, cell_count = footprints.shape
    lat_count = lat_cov.shape[0]
    lon_count = lon_cov.shape[0]
    along_lon = jnp.dot(
        footprints.reshape(receptors_here * time_count * lat_count, lon_count),
        lon_cov,
        preferred_element_type=jnp.float32,
    ).astype(jnp.bfloat16)
    along_lat = jnp.einsum(
        "rab,ac->rcb",
        along_lon.reshape(receptors_here * time_count, lat_count, lon_count),
        lat_cov,
        preferred_element_type=jnp.float32,
    ).astype(jnp.bfloat16)
    return jnp.einsum(
        "rtc,ts->rsc",
        along_lat.reshape(receptors_here, time_count, cell_count),
        time_cov,
        preferred_element_type=jnp.float32,
    ).astype(jnp.bfloat16)


def chunk_geometry(time_count, cell_count, chunks):
    row_tiles = -(-time_count // ROW_TILE)
    col_tiles = -(-cell_count // LANE)
    if chunks % row_tiles == 0:
        per_row = chunks // row_tiles
        col_tiles = -(-col_tiles // per_row) * per_row
    else:
        assert row_tiles % chunks == 0
        per_row = 1
    return row_tiles, col_tiles, per_row


def to_chunks(values, chunks):
    time_count, cell_count = values.shape
    row_tiles, col_tiles, per_row = chunk_geometry(time_count, cell_count, chunks)
    rows = row_tiles * ROW_TILE
    cols = col_tiles * LANE
    padded = jnp.pad(values, ((0, rows - time_count), (0, cols - cell_count)))
    if per_row > 1:
        blocks = padded.reshape(row_tiles, ROW_TILE, per_row, cols // per_row)
        return blocks.transpose(0, 2, 1, 3).reshape(chunks, ROW_TILE, cols // per_row)
    return padded.reshape(chunks, rows // chunks, cols)


def local(footprints, time_cov, lat_cov, lon_cov):
    space_count = lax.axis_size("space")
    rec_index = lax.axis_index("rec")
    plain = to_chunks(footprints[0], space_count)
    plain_here = lax.all_to_all(plain, "space", split_axis=0, concat_axis=0, tiled=True)
    weighted = to_chunks(weigh_footprints(footprints, time_cov, lat_cov, lon_cov)[0], space_count)
    weighted_here = lax.all_to_all(weighted, "space", split_axis=0, concat_axis=0, tiled=True)
    rec_count = lax.axis_size("rec")
    contract = (((1, 2), (1, 2)), ((), ()))
    if rec_count == 1:
        partial_value = lax.dot_general(weighted_here, plain_here, contract, preferred_element_type=jnp.float32)
    else:
        gathered = lax.all_gather(plain_here, "rec", axis=0, tiled=True)
        partial_value = lax.dot_general(weighted_here, gathered, contract, preferred_element_type=jnp.float32)
    return lax.psum_scatter(partial_value, "space", scatter_dimension=0, tiled=True)


def solution(mesh):
    in_specs = (P(("rec", "space"), None, None), P(), P(), P())
    out_specs = P(("rec", "space"), None)
    return jax.shard_map(local, mesh=mesh, in_specs=in_specs, out_specs=out_specs, check_vma=False)
```

time: 255 us -> 188 us (0.74)
  local copies, waits for them, and re-layouts: 134 us -> 34.8 us
  waiting for transfers between devices: 14.5 us -> 66.6 us
  other arithmetic: 25.6 us -> 0 us
  between operations: 0.17 us -> 13.5 us
  blocking collectives: 50.4 us -> 45.4 us
    all_to_all x3 -> x2, waiting for transfers between devices: 14.5 us -> 66.6 us  [the longest x1 43 us: local(): lax.all_to_all(weighted, 'space', split_axis=0, concat_axis=0, tiled=True)]
    reshape x2 -> x3, local copies, waits for them, and re-layouts: 43.2 us -> 7.46 us  [to_chunks(): blocks = padded.reshape(row_tiles, ROW_TILE, per_row, cols // per_row)]
    unnamed x18 -> x10, local copies, waits for them, and re-layouts: 35.3 us -> 2.59 us
    unnamed x2 -> x0, other arithmetic: 25.6 us -> none
    all_to_all x4 -> x1, local copies, waits for them, and re-layouts: 27.9 us -> 3.31 us  [local(): lax.all_to_all(plain, 'space', split_axis=0, concat_axis=0, tiled=True)]
    pad x2, local copies, waits for them, and re-layouts: 11.7 us -> 1.85 us  [to_chunks(): padded = jnp.pad(values, ((0, rows - time_count), (0, cols - cell_count)))]
    all_to_all x1 -> x0, blocking collectives: 5.35 us -> none  [regroup(): lax.all_to_all(lax.all_to_all(values[1], 'space', split_axis=1, concat_ax...]
    transpose x0 -> x1, local copies, waits for them, and re-layouts: none -> 3.23 us  [to_chunks(): blocks.transpose(0, 2, 1, 3).reshape(chunks, ROW_TILE, cols // per_row)]
  transfers between devices with their start and end apart: 3 -> 3, of which waited for: 1 -> 2; matrix products, arithmetic and copies ran while one was open for 37% -> 15% of each run, Pallas kernels for 0% -> 0%
where the time goes in v1:
time: 188 us; the launch traced here: 187 us
  waiting for transfers between devices  66.6 us (35%)
  blocking collectives  45.4 us (24%)
  local copies, waits for them, and re-layouts  34.8 us (19%)
  starting transfers between devices  18.7 us (10%)
  between operations  13.5 us (7%)
  matrix products  8.51 us (5%)
    unnamed x1, blocking collectives  45.4 us
    all_to_all x1, waiting for transfers between devices, local(): lax.all_to_all(weighted, 'space', split_axis=0, concat_axis=0, tiled=True)  43 us
    all_to_all x1, waiting for transfers between devices, local(): lax.all_to_all(plain, 'space', split_axis=0, concat_axis=0, tiled=True)  23.6 us
    all_to_all x1, starting transfers between devices, local(): lax.all_to_all(weighted, 'space', split_axis=0, concat_axis=0, tiled=True)  10.3 us
    all_to_all x1, starting transfers between devices, local(): lax.all_to_all(plain, 'space', split_axis=0, concat_axis=0, tiled=True)  8.36 us
    reshape x3, local copies, waits for them, and re-layouts, to_chunks(): blocks = padded.reshape(row_tiles, ROW_TILE, per_row, cols // per_row)  7.46 us
    reshape x1, local copies, waits for them, and re-layouts, weigh_footprints(): footprints.reshape(receptors_here * time_count * lat_count, lon_count)  5.83 us
    convert_element_type x1, local copies, waits for them, and re-layouts, weigh_footprints(): along_lon = jnp.dot(footprints.reshape(receptors_here * time_count * lat_...  4.09 us
  transfers between devices with their start and end apart: 3, of which 2 were waited for; matrix products, arithmetic and copies ran while one was open for 15% of the time, Pallas kernels for 0%

profile of v1, /device:TPU:0, one launch (start us, length us, event | category | flops | bytes accessed | tf_op | source)
XLA Modules:
  0.0 187.5 jit_solution(5962604896555334931)
XLA Ops:
  6.5 1.7 pad.8
  8.3 2.1 %reshape.32 = bf16[8,16,2,4224]{3,2,1,0:T(2,128)(2,1)} reshape(bf16[128,8448]{1,0:T(8,128)(2,1)S(1)} %pad.8) | data formatting | bytes 4325376 | tf_op jit(solution)/shard_map/reshape | solution.py:52
  10.4 3.2 %copy.18 = bf16[8,16,2,4224]{3,1,2,0:T(8,128)(2,1)} copy(bf16[8,16,2,4224]{3,2,1,0:T(2,128)(2,1)} %reshape.32) | data formatting | bytes 4325376 | tf_op jit(solution)/shard_map/reshape | solution.py:52
  13.6 8.4 %all-to-all-start.1 = ((bf16[16,16,4224]{2,1,0:T(8,128)(2,1)}), bf16[16,16,4224]{2,1,0:T(8,128)(2,1)}, u32[]{:S(2)}, u32[]{:S(2)}) async-start(bf16[16,16,4224]{2,1,0:T(8,128)(2,1)} %bitcast.8), calls=%async_computation.1 | async-start | bytes 4325376 | tf_op jit(solution)/shard_map/all_to_all | solution.py:61
  21.9 0.0 all-gather.2.cloned.1.call-start
  22.0 5.8 %reshape.27 = bf16[8400,120]{1,0:T(8,128)(2,1)S(1)} reshape(bf16[1,120,8400]{2,1,0:T(8,128)(2,1)} %param.4) | data formatting | bytes 4032000 | tf_op jit(solution)/shard_map/reshape | solution.py:15
  27.8 2.1 %convolution_convert_fusion.1 = bf16[8400,120]{0,1:T(8,128)(2,1)} fusion(bf16[8400,120]{1,0:T(8,128)(2,1)S(1)} %reshape.27, bf16[120,120]{1,0:T(8,128)(2,1)S(1)} %copy-done), kind=kOutput, calls=%fused_computation.1 | convolution fusion | flops 242928000 | bytes 4060800 | tf_op jit(solution)/shard_map/dot_general | solution.py:14
  30.0 4.1 %copy.14 = bf16[8400,120]{1,0:T(8,128)(2,1)} copy(bf16[8400,120]{0,1:T(8,128)(2,1)} %convolution_convert_fusion.1) | data formatting | bytes 4032000 | tf_op jit(solution)/shard_map/convert_element_type | solution.py:18
  34.1 2.8 %reshape.28 = bf16[120,70,120]{2,1,0:T(8,128)(2,1)S(1)} reshape(bf16[8400,120]{1,0:T(8,128)(2,1)} %copy.14) | data formatting | bytes 4032000 | tf_op jit(solution)/shard_map/reshape | solution.py:21
  36.9 2.1 %convert_bitcast_fusion = bf16[120,70,120]{2,1,0:T(8,128)(2,1)} fusion(bf16[120,70,120]{2,1,0:T(8,128)(2,1)S(1)} %reshape.28, bf16[70,70]{1,0:T(8,128)(2,1)S(1)} %copy-done.2), kind=kOutput, calls=%fused_computation.3 | convolution fusion | flops 142128000 | bytes 4041800 | tf_op jit(solution)/shard_map/rab,ac->rcb/dot_general | solution.py:19
  39.0 3.6 %copy.16 = bf16[120,70,120]{0,2,1:T(8,128)(2,1)S(1)} copy(bf16[120,70,120]{2,1,0:T(8,128)(2,1)} %convert_bitcast_fusion) | data formatting | bytes 4032000 | tf_op jit(solution)/shard_map/convert_element_type | solution.py:24
  42.6 23.6 %all-to-all-done.1 = bf16[16,16,4224]{2,1,0:T(8,128)(2,1)} async-done(((bf16[16,16,4224]{2,1,0:T(8,128)(2,1)}), bf16[16,16,4224]{2,1,0:T(8,128)(2,1)}, u32[]{:S(2)}, u32[]{:S(2)}) %all-to-all-start.1) | async-done | bytes 2162720 | tf_op jit(solution)/shard_map/all_to_all | solution.py:61
  66.2 3.3 %copy.19 = bf16[16,16,4224]{2,0,1:T(8,128)(2,1)} copy(bf16[16,16,4224]{2,1,0:T(8,128)(2,1)} %all-to-all-done.1) | data formatting | bytes 4325376 | tf_op jit(solution)/shard_map/all_to_all | solution.py:61
  69.5 0.7 copy-done.1
  70.3 0.8 fusion
  71.1 0.1 pad.7
  71.2 2.1 %reshape.30 = bf16[8,16,2,4224]{3,2,1,0:T(2,128)(2,1)} reshape(bf16[128,8448]{1,0:T(8,128)(2,1)S(1)} %pad.7) | data formatting | bytes 4325376 | tf_op jit(solution)/shard_map/reshape | solution.py:52
  73.3 3.2 %copy.17 = bf16[8,2,16,4224]{3,2,1,0:T(8,128)(2,1)} copy(bf16[8,2,16,4224]{3,1,2,0:T(2,128)(2,1)} %bitcast.24) | data formatting | bytes 4325376 | tf_op jit(solution)/shard_map/transpose | solution.py:53
  76.6 10.3 %all-to-all-start = ((bf16[16,16,4224]{2,1,0:T(8,128)(2,1)}), bf16[16,16,4224]{2,1,0:T(8,128)(2,1)S(1)}, u32[]{:S(2)}, u32[]{:S(2)}) async-start(bf16[16,16,4224]{2,1,0:T(8,128)(2,1)} %bitcast.23), calls=%async_computation | async-start | bytes 4325376 | tf_op jit(solution)/shard_map/all_to_all | solution.py:63
  86.9 0.7 dynamic-slice
  87.6 43.0 %all-to-all-done = bf16[16,16,4224]{2,1,0:T(8,128)(2,1)S(1)} async-done(((bf16[16,16,4224]{2,1,0:T(8,128)(2,1)}), bf16[16,16,4224]{2,1,0:T(8,128)(2,1)S(1)}, u32[]{:S(2)}, u32[]{:S(2)}) %all-to-all-start) | async-done | bytes 2162720 | tf_op jit(solution)/shard_map/all_to_all | solution.py:63
  130.6 3.5 %fusion.3 = f32[16,32]{1,0:T(8,128)S(1)} fusion(bf16[32,16,4224]{2,0,1:T(8,128)(2,1)} %all-gather.2.cloned.1.call-done, bf16[16,16,4224]{2,1,0:T(8,128)(2,1)S(1)} %all-to-all-done), kind=kOutput, calls=%fused_computation.6 | convolution fusion | flops 69206016 | bytes 6490112 | tf_op jit(solution)/shard_map/dot_general | solution.py:70
  134.0 45.4 %all-reduce.2 = f32[16,32]{1,0:T(8,128)S(1)} all-reduce(f32[16,32]{1,0:T(8,128)S(1)} %fusion.3), channel_id=2, replica_groups=mesh['rec'=2,'space'=16] {'space'}, use_global_device_ids=true, to_apply=%region_0.1.clone | all-reduce | flops 512 | bytes 4096
  179.4 1.2 constant_dynamic-slice_fusion
  (9 shorter events, 0.0 us)
Async XLA Ops:
  6.5 21.3 %copy-start = (bf16[120,120]{1,0:T(8,128)(2,1)S(1)}, bf16[120,120]{1,0:T(8,128)(2,1)}, u32[]{:S(2)}) copy-start(bf16[120,120]{1,0:T(8,128)(2,1)} %param.7) | copy-start | bytes 86404
  13.6 52.6 %all-to-all-start.1 = ((bf16[16,16,4224]{2,1,0:T(8,128)(2,1)}), bf16[16,16,4224]{2,1,0:T(8,128)(2,1)}, u32[]{:S(2)}, u32[]{:S(2)}) async-start(bf16[16,16,4224]{2,1,0:T(8,128)(2,1)} %bitcast.8), calls=%async_computation.1 | async-start | bytes 4325376 | tf_op jit(solution)/shard_map/all_to_all | solution.py:61
  21.9 108.6 %all-gather.2.cloned.1.call-start = ((), (), s32[]{:S(2)}) async-start(), calls=%async_computation.2 | async-start | bytes 6488064 | tf_op jit(solution)/shard_map/all_gather | solution.py:69
  34.1 2.8 %copy-start.2 = (bf16[70,70]{1,0:T(8,128)(2,1)S(1)}, bf16[70,70]{1,0:T(8,128)(2,1)}, u32[]{:S(2)}) copy-start(bf16[70,70]{1,0:T(8,128)(2,1)} %param.6) | copy-start | bytes 29404
  69.5 0.8 copy-start.1
  76.6 10.4 %copy-start.3 = (u32[32]{0:T(128)S(1)}, u32[32]{0:T(128)}, u32[]{:S(2)}) copy-start(u32[32]{0:T(128)} %constant.10) | copy-start | bytes 388
  76.6 54.0 %all-to-all-start = ((bf16[16,16,4224]{2,1,0:T(8,128)(2,1)}), bf16[16,16,4224]{2,1,0:T(8,128)(2,1)S(1)}, u32[]{:S(2)}, u32[]{:S(2)}) async-start(bf16[16,16,4224]{2,1,0:T(8,128)(2,1)} %bitcast.23), calls=%async_computation | async-start | bytes 4325376 | tf_op jit(solution)/shard_map/all_to_all | solution.py:63
Sparse Core Ops, SparseCore 0:
  69.7 18.4 all-gather.1

commit v2 on v1

v2 whole, which is shorter than its diff:
```python
import jax
import jax.numpy as jnp
from jax import lax
from jax.sharding import PartitionSpec as P

ROW_TILE = 16
LANE = 128


def chunk_geometry(time_count, cell_count, chunks):
    row_tiles = -(-time_count // ROW_TILE)
    col_tiles = -(-cell_count // LANE)
    assert chunks % row_tiles == 0
    per_row = chunks // row_tiles
    col_tiles = -(-col_tiles // per_row) * per_row
    return row_tiles, col_tiles * LANE, per_row


def plain_chunks(values, chunks):
    time_count, cell_count = values.shape
    row_tiles, cols, per_row = chunk_geometry(time_count, cell_count, chunks)
    padded = jnp.pad(values, ((0, row_tiles * ROW_TILE - time_count), (0, cols - cell_count)))
    width = cols // per_row
    blocks = padded.reshape(row_tiles, ROW_TILE, per_row, width)
    return blocks.transpose(0, 2, 1, 3).reshape(chunks, ROW_TILE, width)


def weighted_chunks(footprint, time_cov, lat_cov, lon_cov, chunks):
    time_count, cell_count = footprint.shape
    lat_count = lat_cov.shape[0]
    lon_count = lon_cov.shape[0]
    row_tiles, cols, per_row = chunk_geometry(time_count, cell_count, chunks)
    along_lon = jnp.dot(
        footprint.reshape(time_count * lat_count, lon_count),
        lon_cov,
        preferred_element_type=jnp.float32,
    ).astype(jnp.bfloat16)
    along_lat = jnp.einsum(
        "tab,ac->tcb",
        along_lon.reshape(time_count, lat_count, lon_count),
        lat_cov,
        preferred_element_type=jnp.float32,
    ).astype(jnp.bfloat16)
    along_lat = jnp.pad(along_lat.reshape(time_count, cell_count), ((0, 0), (0, cols - cell_count)))
    width = cols // per_row
    time_padded = jnp.pad(time_cov, ((0, 0), (0, row_tiles * ROW_TILE - time_count)))
    weighted = jnp.einsum(
        "trq,thc->rhqc",
        time_padded.reshape(time_count, row_tiles, ROW_TILE),
        along_lat.reshape(time_count, per_row, width),
        preferred_element_type=jnp.float32,
    ).astype(jnp.bfloat16)
    return weighted.reshape(chunks, ROW_TILE, width)


def local(footprints, time_cov, lat_cov, lon_cov):
    space_count = lax.axis_size("space")
    rec_count = lax.axis_size("rec")
    rec_index = lax.axis_index("rec")
    plain = plain_chunks(footprints[0], space_count)
    plain_here = lax.all_to_all(plain, "space", split_axis=0, concat_axis=0, tiled=True)
    weighted = weighted_chunks(footprints[0], time_cov, lat_cov, lon_cov, space_count)
    weighted_here = lax.all_to_all(weighted, "space", split_axis=0, concat_axis=0, tiled=True)
    contract = (((1, 2), (1, 2)), ((), ()))
    group = plain_here.shape[0]
    partial_value = jnp.zeros((group, group * rec_count), jnp.float32)
    for shift in range(rec_count):
        if shift == 0:
            other = plain_here
        else:
            perm = [(i, (i + shift) % rec_count) for i in range(rec_count)]
            other = lax.ppermute(plain_here, "rec", perm)
        block = lax.dot_general(weighted_here, other, contract, preferred_element_type=jnp.float32)
        source = (rec_index + rec_count - shift) % rec_count
        partial_value = lax.dynamic_update_slice(partial_value, block, (0, source * group))
    spread = lax.all_to_all(partial_value, "space", split_axis=0, concat_axis=0, tiled=True)
    return jnp.sum(spread, axis=0, keepdims=True)


def solution(mesh):
    in_specs = (P(("rec", "space"), None, None), P(), P(), P())
    out_specs = P(("rec", "space"), None)
    return jax.shard_map(local, mesh=mesh, in_specs=in_specs, out_specs=out_specs, check_vma=False)
```

time: 188 us -> 140 us (0.74)
  blocking collectives: 45.4 us -> 17.1 us
  between operations: 13.5 us -> 0.13 us
  waiting for transfers between devices: 66.6 us -> 58.9 us
  matrix products: 8.51 us -> 10.5 us
    unnamed x1 -> x0, blocking collectives: 45.4 us -> none
    all_to_all x0 -> x1, blocking collectives: none -> 17.1 us  [local(): lax.all_to_all(partial_value, 'space', split_axis=0, concat_axis=0, tiled...]
    reshape x5 -> x3, local copies, waits for them, and re-layouts: 16.1 us -> 8.09 us  [the longest x2 5.3 us: plain_chunks(): blocks = padded.reshape(row_tiles, ROW_TILE, per_row, width)]
    another operation x0 -> x1, local copies, waits for them, and re-layouts: none -> 5.83 us  [weighted_chunks(): footprint.reshape(time_count * lat_count, lon_count)]
    all_to_all x1, waiting for transfers between devices: 23.6 us -> 18.6 us  [local(): lax.all_to_all(plain, 'space', split_axis=0, concat_axis=0, tiled=True)]
    transpose x1 -> x0, local copies, waits for them, and re-layouts: 3.23 us -> none  [to_chunks(): blocks.transpose(0, 2, 1, 3).reshape(chunks, ROW_TILE, cols // per_row)]
    dynamic_update_slice x0 -> x2, local copies, waits for them, and re-layouts: none -> 2.83 us  [local(): lax.dynamic_update_slice(partial_value, block, (0, source * group))]
    all_to_all x1, waiting for transfers between devices: 43 us -> 40.3 us  [local(): lax.all_to_all(weighted, 'space', split_axis=0, concat_axis=0, tiled=True)]
  transfers between devices with their start and end apart: 3 -> 3, of which waited for: 2 -> 2; matrix products, arithmetic and copies ran while one was open for 15% -> 23% of each run, Pallas kernels for 0% -> 0%
where the time goes in v2:
time: 140 us; the launch traced here: 139 us
  waiting for transfers between devices  58.9 us (42%)
  local copies, waits for them, and re-layouts  33.8 us (24%)
  starting transfers between devices  18.6 us (13%)
  blocking collectives  17.1 us (12%)
  matrix products  10.5 us (8%)
    all_to_all x1, waiting for transfers between devices, local(): lax.all_to_all(weighted, 'space', split_axis=0, concat_axis=0, tiled=True)  40.3 us
    all_to_all x1, waiting for transfers between devices, local(): lax.all_to_all(plain, 'space', split_axis=0, concat_axis=0, tiled=True)  18.6 us
    all_to_all x1, blocking collectives, local(): lax.all_to_all(partial_value, 'space', split_axis=0, concat_axis=0, tiled...  17.1 us
    all_to_all x1, starting transfers between devices, local(): lax.all_to_all(weighted, 'space', split_axis=0, concat_axis=0, tiled=True)  10.2 us
    all_to_all x1, starting transfers between devices, local(): lax.all_to_all(plain, 'space', split_axis=0, concat_axis=0, tiled=True)  8.36 us
    another operation x1, local copies, waits for them, and re-layouts, weighted_chunks(): footprint.reshape(time_count * lat_count, lon_count)  5.83 us
    dot_general x2, matrix products, local(): lax.dot_general(weighted_here, other, contract, preferred_element_type=jn...  5.51 us
    reshape x2, local copies, waits for them, and re-layouts, plain_chunks(): blocks = padded.reshape(row_tiles, ROW_TILE, per_row, width)  5.3 us
  transfers between devices with their start and end apart: 3, of which 2 were waited for; matrix products, arithmetic and copies ran while one was open for 23% of the time, Pallas kernels for 0%

profile of v2, /device:TPU:0, one launch (start us, length us, event | category | flops | bytes accessed | tf_op | source)
XLA Modules:
  0.0 139.5 jit_solution(3298507960157099547)
XLA Ops:
  0.0 1.7 %pad.14 = bf16[128,8448]{1,0:T(8,128)(2,1)S(1)} pad(bf16[120,8400]{1,0:T(8,128)(2,1)} %bitcast.38, bf16[]{:T(256)} %constant.30.clone.1), padding=0_8x0_48 | pad | bytes 4178690 | tf_op jit(solution)/shard_map/jit(_pad)/pad | solution.py:22
  1.7 2.1 %reshape.32 = bf16[8,16,2,4224]{3,2,1,0:T(2,128)(2,1)} reshape(bf16[128,8448]{1,0:T(8,128)(2,1)S(1)} %pad.14) | data formatting | bytes 4325376 | tf_op jit(solution)/shard_map/reshape | solution.py:24
  3.9 3.2 %copy.25 = bf16[8,16,2,4224]{3,1,2,0:T(8,128)(2,1)} copy(bf16[8,16,2,4224]{3,2,1,0:T(2,128)(2,1)} %reshape.32) | data formatting | bytes 4325376 | tf_op jit(solution)/shard_map/reshape | solution.py:24
  7.0 8.4 %all-to-all-start.1 = ((bf16[16,16,4224]{2,1,0:T(8,128)(2,1)}), bf16[16,16,4224]{2,1,0:T(8,128)(2,1)}, u32[]{:S(2)}, u32[]{:S(2)}) async-start(bf16[16,16,4224]{2,1,0:T(8,128)(2,1)} %bitcast.11), calls=%async_computation.1 | async-start | bytes 4325376 | tf_op jit(solution)/shard_map/all_to_all | solution.py:61
  15.4 5.8 %reshape_squeeze.3 = bf16[8400,120]{1,0:T(8,128)(2,1)S(1)} reshape(bf16[1,120,8400]{2,1,0:T(8,128)(2,1)} %param.4) | data formatting | bytes 4032000 | tf_op jit(solution)/shard_map/reshape;squeeze | solution.py:34
  21.2 2.1 %convolution_convert_fusion = bf16[8400,120]{0,1:T(8,128)(2,1)} fusion(bf16[8400,120]{1,0:T(8,128)(2,1)S(1)} %reshape_squeeze.3, bf16[120,120]{1,0:T(8,128)(2,1)S(1)} %copy-done), kind=kOutput, calls=%fused_computation | convolution fusion | flops 242928000 | bytes 4060800 | tf_op jit(solution)/shard_map/dot_general | solution.py:33
  23.3 4.1 %copy.18 = bf16[8400,120]{1,0:T(8,128)(2,1)} copy(bf16[8400,120]{0,1:T(8,128)(2,1)} %convolution_convert_fusion) | data formatting | bytes 4032000 | tf_op jit(solution)/shard_map/convert_element_type | solution.py:37
  27.4 2.8 %reshape.27 = bf16[120,70,120]{2,1,0:T(8,128)(2,1)S(1)} reshape(bf16[8400,120]{1,0:T(8,128)(2,1)} %copy.18) | data formatting | bytes 4032000 | tf_op jit(solution)/shard_map/reshape | solution.py:40
  30.3 2.2 %convert_bitcast_fusion = bf16[120,70,120]{2,1,0:T(8,128)(2,1)} fusion(bf16[120,70,120]{2,1,0:T(8,128)(2,1)S(1)} %reshape.27, bf16[70,70]{1,0:T(8,128)(2,1)S(1)} %copy-done.2), kind=kOutput, calls=%fused_computation.3 | convolution fusion | flops 142128000 | bytes 4041800 | tf_op jit(solution)/shard_map/tab,ac->tcb/dot_general | solution.py:38
  32.4 4.4 %copy.20 = bf16[120,70,120]{0,2,1:T(8,128)(2,1)} copy(bf16[120,70,120]{2,1,0:T(8,128)(2,1)} %convert_bitcast_fusion) | data formatting | bytes 4032000 | tf_op jit(solution)/shard_map/convert_element_type | solution.py:43
  36.9 1.8 %pad.12 = bf16[120,8448]{0,1:T(8,128)(2,1)S(1)} pad(bf16[120,8400]{0,1:T(8,128)(2,1)} %bitcast.37, bf16[]{:T(256)} %constant.30.clone.1), padding=0_0x0_48 | pad | bytes 4043522 | tf_op jit(solution)/shard_map/jit(_pad)/pad | solution.py:44
  38.7 0.1 copy.39
  38.8 0.7 fusion
  39.6 1.5 %copy.24 = bf16[8,2,16,4224]{3,2,1,0:T(8,128)(2,1)} copy(bf16[8,2,16,4224]{3,2,0,1:T(8,128)(2,1)S(1)} %fusion) | data formatting | bytes 4325376 | tf_op jit(solution)/shard_map/convert_element_type | solution.py:52
  41.1 18.6 %all-to-all-done.1 = bf16[16,16,4224]{2,1,0:T(8,128)(2,1)} async-done(((bf16[16,16,4224]{2,1,0:T(8,128)(2,1)}), bf16[16,16,4224]{2,1,0:T(8,128)(2,1)}, u32[]{:S(2)}, u32[]{:S(2)}) %all-to-all-start.1) | async-done | bytes 2162720 | tf_op jit(solution)/shard_map/all_to_all | solution.py:61
  59.6 10.2 %all-to-all-start = ((bf16[16,16,4224]{2,1,0:T(8,128)(2,1)}), bf16[16,16,4224]{2,1,0:T(8,128)(2,1)S(1)}, u32[]{:S(2)}, u32[]{:S(2)}) async-start(bf16[16,16,4224]{2,1,0:T(8,128)(2,1)} %bitcast.8), calls=%async_computation | async-start | bytes 4325376 | tf_op jit(solution)/shard_map/all_to_all | solution.py:63
  69.8 3.3 %copy.27 = bf16[16,16,4224]{2,0,1:T(8,128)(2,1)} copy(bf16[16,16,4224]{2,1,0:T(8,128)(2,1)} %all-to-all-done.1) | data formatting | bytes 4325376 | tf_op jit(solution)/shard_map/all_to_all | solution.py:61
  73.1 40.3 %all-to-all-done = bf16[16,16,4224]{2,1,0:T(8,128)(2,1)S(1)} async-done(((bf16[16,16,4224]{2,1,0:T(8,128)(2,1)}), bf16[16,16,4224]{2,1,0:T(8,128)(2,1)S(1)}, u32[]{:S(2)}, u32[]{:S(2)}) %all-to-all-start) | async-done | bytes 2162720 | tf_op jit(solution)/shard_map/all_to_all | solution.py:63
  113.5 2.8 %fusion.3 = f32[16,16,1]{1,0,2:T(8,128)S(1)} fusion(bf16[16,16,4224]{2,1,0:T(8,128)(2,1)S(1)} %all-to-all-done, bf16[16,16,4224]{2,1,0:T(8,128)(2,1)} %all-to-all-done.1), kind=kOutput, calls=%fused_computation.6 | convolution fusion | flops 34603008 | bytes 4326400 | tf_op jit(solution)/shard_map/dot_general | solution.py:73
  116.4 0.4 dynamic_update_slice.8
  116.7 2.7 %fusion.1 = f32[16,16,1]{1,0,2:T(8,128)S(1)} fusion(bf16[16,16,4224]{2,0,1:T(8,128)(2,1)} %collective-permute-done, bf16[16,16,4224]{2,1,0:T(8,128)(2,1)S(1)} %all-to-all-done), kind=kOutput, calls=%fused_computation.4 | convolution fusion | flops 34603008 | bytes 4326400 | tf_op jit(solution)/shard_map/dot_general | solution.py:73
  119.4 2.5 %dynamic_update_slice.9 = f32[16,1,32]{2,1,0:T(1,128)S(1)} dynamic-update-slice(f32[16,1,32]{2,1,0:T(1,128)S(1)} %dynamic_update_slice.8, f32[16,1,16]{2,1,0:T(1,128)S(1)} %bitcast.40, s32[]{:T(128)} %constant.31.clone.1, s32[]{:T(128)} %constant.31.clone.1, s32[]{:T(128)S(6)} %select_n.20) | dynamic-update-slice | bytes 2052 | tf_op jit(solution)/shard_map/dynamic_update_slice | solution.py:75
  121.9 17.1 %all_to_all.25 = f32[16,1,32]{2,1,0:T(1,128)S(1)} all-to-all(f32[16,1,32]{2,1,0:T(1,128)S(1)} %dynamic_update_slice.9), channel_id=1, replica_groups=mesh['rec'=2,'space'=16] {'space'}, dimensions={0} | all-to-all | bytes 4096 | tf_op jit(solution)/shard_map/all_to_all | solution.py:76
  139.0 0.5 reduce_sum.9
  (10 shorter events, 0.0 us)
Async XLA Ops:
  0.0 21.2 %copy-start = (bf16[120,120]{1,0:T(8,128)(2,1)S(1)}, bf16[120,120]{1,0:T(8,128)(2,1)}, u32[]{:S(2)}) copy-start(bf16[120,120]{1,0:T(8,128)(2,1)} %param.7) | copy-start | bytes 86404
  7.0 52.6 %all-to-all-start.1 = ((bf16[16,16,4224]{2,1,0:T(8,128)(2,1)}), bf16[16,16,4224]{2,1,0:T(8,128)(2,1)}, u32[]{:S(2)}, u32[]{:S(2)}) async-start(bf16[16,16,4224]{2,1,0:T(8,128)(2,1)} %bitcast.11), calls=%async_computation.1 | async-start | bytes 4325376 | tf_op jit(solution)/shard_map/all_to_all | solution.py:61
  27.4 2.8 %copy-start.2 = (bf16[70,70]{1,0:T(8,128)(2,1)S(1)}, bf16[70,70]{1,0:T(8,128)(2,1)}, u32[]{:S(2)}) copy-start(bf16[70,70]{1,0:T(8,128)(2,1)} %param.6) | copy-start | bytes 29404
  36.9 1.8 %copy-start.1 = (bf16[120,120]{1,0:T(8,128)(2,1)S(1)}, bf16[120,120]{1,0:T(8,128)(2,1)}, u32[]{:S(2)}) copy-start(bf16[120,120]{1,0:T(8,128)(2,1)} %param.5) | copy-start | bytes 86404
  59.6 53.9 %all-to-all-start = ((bf16[16,16,4224]{2,1,0:T(8,128)(2,1)}), bf16[16,16,4224]{2,1,0:T(8,128)(2,1)S(1)}, u32[]{:S(2)}, u32[]{:S(2)}) async-start(bf16[16,16,4224]{2,1,0:T(8,128)(2,1)} %bitcast.8), calls=%async_computation | async-start | bytes 4325376 | tf_op jit(solution)/shard_map/all_to_all | solution.py:63
  73.1 43.6 %collective-permute-start = (bf16[16,16,4224]{2,0,1:T(8,128)(2,1)}, bf16[16,16,4224]{2,0,1:T(8,128)(2,1)}, u32[]{:S(2)}, u32[]{:S(2)}) collective-permute-start(bf16[16,16,4224]{2,0,1:T(8,128)(2,1)} %copy.27), channel_id=1, source_target_pairs={{0,16},{16,0},{1,17},{17,1},{2,18},{18,2},{3,19},{19,3},{4,20},{20... | collective-permute-start | bytes 6488072 | tf_op jit(solution)/shard_map/ppermute | solution.py:72

commit v3 on v2

--- a/solution.py
+++ b/solution.py
@@ -21,8 +21,12 @@
     row_tiles, cols, per_row = chunk_geometry(time_count, cell_count, chunks)
     padded = jnp.pad(values, ((0, row_tiles * ROW_TILE - time_count), (0, cols - cell_count)))
     width = cols // per_row
-    blocks = padded.reshape(row_tiles, ROW_TILE, per_row, width)
-    return blocks.transpose(0, 2, 1, 3).reshape(chunks, ROW_TILE, width)
+    pieces = [
+        padded[row * ROW_TILE:(row + 1) * ROW_TILE, part * width:(part + 1) * width]
+        for row in range(row_tiles)
+        for part in range(per_row)
+    ]
+    return jnp.concatenate(pieces, axis=0).reshape(chunks, ROW_TILE, width)
 
 
 def weighted_chunks(footprint, time_cov, lat_cov, lon_cov, chunks):
@@ -63,16 +67,18 @@
     weighted_here = lax.all_to_all(weighted, "space", split_axis=0, concat_axis=0, tiled=True)
     contract = (((1, 2), (1, 2)), ((), ()))
     group = plain_here.shape[0]
-    partial_value = jnp.zeros((group, group * rec_count), jnp.float32)
-    for shift in range(rec_count):
-        if shift == 0:
-            other = plain_here
-        else:
-            perm = [(i, (i + shift) % rec_count) for i in range(rec_count)]
-            other = lax.ppermute(plain_here, "rec", perm)
-        block = lax.dot_general(weighted_here, other, contract, preferred_element_type=jnp.float32)
-        source = (rec_index + rec_count - shift) % rec_count
-        partial_value = lax.dynamic_update_slice(partial_value, block, (0, source * group))
+    received = [plain_here]
+    for shift in range(1, rec_count):
+        perm = [(i, (i + shift) % rec_count) for i in range(rec_count)]
+        received.append(lax.ppermute(plain_here, "rec", perm))
+    ordered = []
+    for g in range(rec_count):
+        choice = received[0]
+        for shift in range(1, rec_count):
+            choice = jnp.where((rec_index + rec_count - shift) % rec_count == g, received[shift], choice)
+        ordered.append(choice)
+    everyone = jnp.concatenate(ordered, axis=0)
+    partial_value = lax.dot_general(weighted_here, everyone, contract, preferred_element_type=jnp.float32)
     spread = lax.all_to_all(partial_value, "space", split_axis=0, concat_axis=0, tiled=True)
     return jnp.sum(spread, axis=0, keepdims=True)
 

time: 140 us -> 132 us (0.943)
  local copies, waits for them, and re-layouts: 33.8 us -> 23.4 us
  other arithmetic: 0.54 us -> 5.72 us
  matrix products: 10.5 us -> 8.75 us
    all_to_all x1, waiting for transfers between devices: 40.3 us -> 30.5 us  [local(): lax.all_to_all(weighted, 'space', split_axis=0, concat_axis=0, tiled=True)]
    reshape x2 -> x0, local copies, waits for them, and re-layouts: 5.3 us -> none  [plain_chunks(): blocks = padded.reshape(row_tiles, ROW_TILE, per_row, width)]
    select_n x0 -> x1, other arithmetic: none -> 5.18 us  [local(): jnp.where((rec_index + rec_count - shift) % rec_count == g, received[shif...]
    ppermute x1, waiting for transfers between devices: 0.01 us -> 4.59 us  [local(): received.append(lax.ppermute(plain_here, 'rec', perm))]
    all_to_all x1, waiting for transfers between devices: 18.6 us -> 22.5 us  [local(): lax.all_to_all(plain, 'space', split_axis=0, concat_axis=0, tiled=True)]
    unnamed x7 -> x26, local copies, waits for them, and re-layouts: 0.12 us -> 3.69 us
    dynamic_update_slice x2 -> x0, local copies, waits for them, and re-layouts: 2.83 us -> none  [local(): lax.dynamic_update_slice(partial_value, block, (0, source * group))]
    dot_general x2 -> x1, matrix products: 5.51 us -> 3.49 us  [local(): lax.dot_general(weighted_here, everyone, contract, preferred_element_type...]
  transfers between devices with their start and end apart: 3 -> 3, of which waited for: 2 -> 3; matrix products, arithmetic and copies ran while one was open for 23% -> 23% of each run, Pallas kernels for 0% -> 0%
where the time goes in v3:
time: 132 us; the launch traced here: 131 us
  waiting for transfers between devices  57.6 us (44%)
  local copies, waits for them, and re-layouts  23.4 us (18%)
  starting transfers between devices  18.6 us (14%)
  blocking collectives  17.1 us (13%)
  matrix products  8.75 us (7%)
  other arithmetic  5.72 us (4%)
    all_to_all x1, waiting for transfers between devices, local(): lax.all_to_all(weighted, 'space', split_axis=0, concat_axis=0, tiled=True)  30.5 us
    all_to_all x1, waiting for transfers between devices, local(): lax.all_to_all(plain, 'space', split_axis=0, concat_axis=0, tiled=True)  22.5 us
    all_to_all x1, blocking collectives, local(): lax.all_to_all(partial_value, 'space', split_axis=0, concat_axis=0, tiled...  17.1 us
    all_to_all x1, starting transfers between devices, local(): lax.all_to_all(weighted, 'space', split_axis=0, concat_axis=0, tiled=True)  10.2 us
    all_to_all x1, starting transfers between devices, local(): lax.all_to_all(plain, 'space', split_axis=0, concat_axis=0, tiled=True)  8.36 us
    another operation x1, local copies, waits for them, and re-layouts, weighted_chunks(): footprint.reshape(time_count * lat_count, lon_count)  5.51 us
    select_n x1, other arithmetic, local(): jnp.where((rec_index + rec_count - shift) % rec_count == g, received[shif...  5.18 us
    ppermute x1, waiting for transfers between devices, local(): received.append(lax.ppermute(plain_here, 'rec', perm))  4.59 us
  transfers between devices with their start and end apart: 3, of which 3 were waited for; matrix products, arithmetic and copies ran while one was open for 23% of the time, Pallas kernels for 0%

profile of v3, /device:TPU:0, one launch (start us, length us, event | category | flops | bytes accessed | tf_op | source)
XLA Modules:
  0.0 131.2 jit_solution(13720652095957861837)
XLA Ops:
  0.0 1.1 slice_dynamic-update-slice_fusion.6
  1.1 0.9 fusion.6
  2.3 1.3 %copy-done.2 = bf16[256,4224]{1,0:T(8,128)(2,1)} copy-done((bf16[256,4224]{1,0:T(8,128)(2,1)}, bf16[256,4224]{1,0:T(8,128)(2,1)S(1)}, u32[]{:S(2)}) %copy-start.2) | copy-done | bytes 2162712
  3.6 8.4 %all-to-all-start.1 = ((bf16[16,16,4224]{2,1,0:T(8,128)(2,1)}), bf16[16,16,4224]{2,1,0:T(8,128)(2,1)}, u32[]{:S(2)}, u32[]{:S(2)}) async-start(bf16[16,16,4224]{2,1,0:T(8,128)(2,1)} %bitcast.47), calls=%async_computation.1 | async-start | bytes 4325376 | tf_op jit(solution)/shard_map/all_to_all | solution.py:65
  12.0 5.5 %reshape_squeeze.3 = bf16[8400,120]{1,0:T(8,128)(2,1)} reshape(bf16[1,120,8400]{2,1,0:T(8,128)(2,1)S(1)} %copy-done.1) | data formatting | bytes 4032000 | tf_op jit(solution)/shard_map/reshape;squeeze | solution.py:38
  17.5 2.4 %convolution_convert_fusion = bf16[8400,120]{0,1:T(8,128)(2,1)S(1)} fusion(bf16[8400,120]{1,0:T(8,128)(2,1)} %reshape_squeeze.3, bf16[120,120]{1,0:T(8,128)(2,1)S(1)} %copy-done), kind=kOutput, calls=%fused_computation | convolution fusion | flops 242928000 | bytes 4060800 | tf_op jit(solution)/shard_map/dot_general | solution.py:37
  19.9 2.4 %copy.17 = bf16[8400,120]{1,0:T(8,128)(2,1)} copy(bf16[8400,120]{0,1:T(8,128)(2,1)S(1)} %convolution_convert_fusion) | data formatting | bytes 4032000 | tf_op jit(solution)/shard_map/convert_element_type | solution.py:41
  22.3 2.8 %reshape.20 = bf16[120,70,120]{2,1,0:T(8,128)(2,1)S(1)} reshape(bf16[8400,120]{1,0:T(8,128)(2,1)} %copy.17) | data formatting | bytes 4032000 | tf_op jit(solution)/shard_map/reshape | solution.py:44
  25.2 2.1 %convert_bitcast_fusion = bf16[120,70,120]{2,1,0:T(8,128)(2,1)} fusion(bf16[120,70,120]{2,1,0:T(8,128)(2,1)S(1)} %reshape.20, bf16[70,70]{1,0:T(8,128)(2,1)S(1)} %copy-done.4), kind=kOutput, calls=%fused_computation.7 | convolution fusion | flops 142128000 | bytes 4041800 | tf_op jit(solution)/shard_map/tab,ac->tcb/dot_general | solution.py:42
  27.3 3.6 %copy.19 = bf16[120,70,120]{0,2,1:T(8,128)(2,1)S(1)} copy(bf16[120,70,120]{2,1,0:T(8,128)(2,1)} %convert_bitcast_fusion) | data formatting | bytes 4032000 | tf_op jit(solution)/shard_map/convert_element_type | solution.py:47
  30.9 0.1 copy.36
  31.0 0.5 pad.12
  31.6 0.7 fusion
  32.3 1.5 %copy.23 = bf16[8,2,16,4224]{3,2,1,0:T(8,128)(2,1)} copy(bf16[8,2,16,4224]{3,2,0,1:T(8,128)(2,1)S(1)} %fusion) | data formatting | bytes 4325376 | tf_op jit(solution)/shard_map/convert_element_type | solution.py:56
  33.8 22.5 %all-to-all-done.1 = bf16[16,16,4224]{2,1,0:T(8,128)(2,1)} async-done(((bf16[16,16,4224]{2,1,0:T(8,128)(2,1)}), bf16[16,16,4224]{2,1,0:T(8,128)(2,1)}, u32[]{:S(2)}, u32[]{:S(2)}) %all-to-all-start.1) | async-done | bytes 2162720 | tf_op jit(solution)/shard_map/all_to_all | solution.py:65
  56.3 10.2 %all-to-all-start = ((bf16[16,16,4224]{2,1,0:T(8,128)(2,1)}), bf16[16,16,4224]{2,1,0:T(8,128)(2,1)S(1)}, u32[]{:S(2)}, u32[]{:S(2)}) async-start(bf16[16,16,4224]{2,1,0:T(8,128)(2,1)} %bitcast.8), calls=%async_computation | async-start | bytes 4325376 | tf_op jit(solution)/shard_map/all_to_all | solution.py:67
  66.5 3.4 %copy.24 = bf16[16,16,4224]{2,0,1:T(8,128)(2,1)} copy(bf16[16,16,4224]{2,1,0:T(8,128)(2,1)} %all-to-all-done.1) | data formatting | bytes 4325376 | tf_op jit(solution)/shard_map/all_to_all | solution.py:65
  69.8 0.0 collective-permute-start
  69.8 4.6 %collective-permute-done = bf16[16,16,4224]{2,0,1:T(8,128)(2,1)} collective-permute-done((bf16[16,16,4224]{2,0,1:T(8,128)(2,1)}, bf16[16,16,4224]{2,0,1:T(8,128)(2,1)}, u32[]{:S(2)}, u32[]{:S(2)}) %collective-permute-start) | collective-permute-done | bytes 2162720 | tf_op jit(solution)/shard_map/ppermute | solution.py:73
  74.4 5.2 %broadcast_select_fusion.1 = (bf16[16,16,4224]{2,0,1:T(8,128)(2,1)}, bf16[16,16,4224]{2,0,1:T(8,128)(2,1)}) fusion(bf16[16,16,4224]{2,0,1:T(8,128)(2,1)} %collective-permute-done, pred[]{:T(512)S(6)} %eq.9, bf16[16,16,4224]{2,1,0:T(8,128)(2,1)} %all-to-all-done.1, pred[]{:T(512)S(6)} %eq.10), kind=kLoop, calls=%fused_computation.10 | loop fusion | flops 2162688 | bytes 8650754 | tf_op jit(solution)/shard_map/jit(_where)/select_n | solution.py:78
  79.6 30.5 %all-to-all-done = bf16[16,16,4224]{2,1,0:T(8,128)(2,1)S(1)} async-done(((bf16[16,16,4224]{2,1,0:T(8,128)(2,1)}), bf16[16,16,4224]{2,1,0:T(8,128)(2,1)S(1)}, u32[]{:S(2)}, u32[]{:S(2)}) %all-to-all-start) | async-done | bytes 2162720 | tf_op jit(solution)/shard_map/all_to_all | solution.py:67
  110.1 3.5 %fusion.1 = f32[16,32,1]{1,0,2:T(8,128)S(1)} fusion(bf16[16,16,4224]{2,0,1:T(8,128)(2,1)} %get-tuple-element.6, bf16[16,16,4224]{2,0,1:T(8,128)(2,1)} %get-tuple-element.5, bf16[16,16,4224]{2,1,0:T(8,128)(2,1)S(1)} %all-to-all-done), kind=kOutput, calls=%fused_computation.3 | convolution fusion | flops 77856768 | bytes 6490112 | tf_op jit(solution)/shard_map/dot_general | solution.py:81
  113.6 17.1 %all_to_all.19 = f32[16,1,32]{2,1,0:T(1,128)S(1)} all-to-all(f32[16,1,32]{2,1,0:T(1,128)S(1)} %bitcast.49), channel_id=1, replica_groups=mesh['rec'=2,'space'=16] {'space'}, dimensions={0} | all-to-all | bytes 4096 | tf_op jit(solution)/shard_map/all_to_all | solution.py:82
  130.7 0.5 reduce_sum.9
  (24 shorter events, 0.3 us)
Async XLA Ops:
  0.0 17.5 %copy-start = (bf16[120,120]{1,0:T(8,128)(2,1)S(1)}, bf16[120,120]{1,0:T(8,128)(2,1)}, u32[]{:S(2)}) copy-start(bf16[120,120]{1,0:T(8,128)(2,1)} %param.7) | copy-start | bytes 86404
  0.0 2.0 %copy-start.1 = (bf16[1,120,8400]{2,1,0:T(8,128)(2,1)S(1)}, bf16[1,120,8400]{2,1,0:T(8,128)(2,1)}, u32[]{:S(2)}) copy-start(bf16[1,120,8400]{2,1,0:T(8,128)(2,1)} %param.4) | copy-start | bytes 6048004
  2.3 1.4 %copy-start.2 = (bf16[256,4224]{1,0:T(8,128)(2,1)}, bf16[256,4224]{1,0:T(8,128)(2,1)S(1)}, u32[]{:S(2)}) copy-start(bf16[256,4224]{1,0:T(8,128)(2,1)S(1)} %fusion.14) | copy-start | bytes 6488068
  3.6 52.6 %all-to-all-start.1 = ((bf16[16,16,4224]{2,1,0:T(8,128)(2,1)}), bf16[16,16,4224]{2,1,0:T(8,128)(2,1)}, u32[]{:S(2)}, u32[]{:S(2)}) async-start(bf16[16,16,4224]{2,1,0:T(8,128)(2,1)} %bitcast.47), calls=%async_computation.1 | async-start | bytes 4325376 | tf_op jit(solution)/shard_map/all_to_all | solution.py:65
  22.3 2.8 %copy-start.4 = (bf16[70,70]{1,0:T(8,128)(2,1)S(1)}, bf16[70,70]{1,0:T(8,128)(2,1)}, u32[]{:S(2)}) copy-start(bf16[70,70]{1,0:T(8,128)(2,1)} %param.6) | copy-start | bytes 29404
  27.3 3.6 %copy-start.3 = (bf16[120,120]{1,0:T(8,128)(2,1)S(1)}, bf16[120,120]{1,0:T(8,128)(2,1)}, u32[]{:S(2)}) copy-start(bf16[120,120]{1,0:T(8,128)(2,1)} %param.5) | copy-start | bytes 86404
  56.3 53.9 %all-to-all-start = ((bf16[16,16,4224]{2,1,0:T(8,128)(2,1)}), bf16[16,16,4224]{2,1,0:T(8,128)(2,1)S(1)}, u32[]{:S(2)}, u32[]{:S(2)}) async-start(bf16[16,16,4224]{2,1,0:T(8,128)(2,1)} %bitcast.8), calls=%async_computation | async-start | bytes 4325376 | tf_op jit(solution)/shard_map/all_to_all | solution.py:67
  69.8 4.6 %collective-permute-start = (bf16[16,16,4224]{2,0,1:T(8,128)(2,1)}, bf16[16,16,4224]{2,0,1:T(8,128)(2,1)}, u32[]{:S(2)}, u32[]{:S(2)}) collective-permute-start(bf16[16,16,4224]{2,0,1:T(8,128)(2,1)} %copy.24), channel_id=1, source_target_pairs={{0,16},{16,0},{1,17},{17,1},{2,18},{18,2},{3,19},{19,3},{4,20},{20... | collective-permute-start | bytes 6488072 | tf_op jit(solution)/shard_map/ppermute | solution.py:73

commit v4 on v3

v4 whole, which is shorter than its diff:
```python
import jax
import jax.numpy as jnp
from jax import lax
from jax.sharding import PartitionSpec as P

ROW_TILE = 16
LANE = 128


def dense_chunks(values, chunks):
    time_count, cell_count = values.shape
    col_tiles = cell_count // LANE
    per = col_tiles // chunks
    main_cols = per * chunks * LANE
    main = values[:, :main_cols].reshape(time_count, chunks, per, LANE)
    main = main.transpose(1, 2, 0, 3).reshape(chunks, per * time_count, LANE)
    rest_tiles = -(-(cell_count - main_cols) // LANE)
    rest_rows = rest_tiles * time_count
    share = -(-rest_rows // chunks)
    rest = jnp.pad(values[:, main_cols:], ((0, 0), (0, rest_tiles * LANE - (cell_count - main_cols))))
    rest = rest.reshape(time_count, rest_tiles, LANE).transpose(1, 0, 2).reshape(rest_rows, LANE)
    rest = jnp.pad(rest, ((0, share * chunks - rest_rows), (0, 0))).reshape(chunks, share, LANE)
    rows = per * time_count + share
    padded_rows = -(-rows // ROW_TILE) * ROW_TILE
    pieces = [main, rest]
    if padded_rows > rows:
        pieces.append(jnp.zeros((chunks, padded_rows - rows, LANE), values.dtype))
    return jnp.concatenate(pieces, axis=1)


def weighted_full(footprint, time_cov, lat_cov, lon_cov):
    time_count, cell_count = footprint.shape
    lat_count = lat_cov.shape[0]
    lon_count = lon_cov.shape[0]
    along_lon = jnp.dot(
        footprint.reshape(time_count * lat_count, lon_count),
        lon_cov,
        preferred_element_type=jnp.float32,
    ).astype(jnp.bfloat16)
    along_lat = jnp.einsum(
        "tab,ac->tcb",
        along_lon.reshape(time_count, lat_count, lon_count),
        lat_cov,
        preferred_element_type=jnp.float32,
    ).astype(jnp.bfloat16)
    return jnp.dot(
        time_cov.T, along_lat.reshape(time_count, cell_count), preferred_element_type=jnp.float32
    ).astype(jnp.bfloat16)


def local(footprints, time_cov, lat_cov, lon_cov):
    space_count = lax.axis_size("space")
    rec_count = lax.axis_size("rec")
    rec_index = lax.axis_index("rec")
    plain = dense_chunks(footprints[0], space_count)
    plain, footprint = lax.optimization_barrier((plain, footprints[0]))
    plain_here = lax.all_to_all(plain, "space", split_axis=0, concat_axis=0, tiled=True)
    weighted = dense_chunks(weighted_full(footprint, time_cov, lat_cov, lon_cov), space_count)
    weighted_here = lax.all_to_all(weighted, "space", split_axis=0, concat_axis=0, tiled=True)
    contract = (((1, 2), (1, 2)), ((), ()))
    group = plain_here.shape[0]
    received = [plain_here]
    for shift in range(1, rec_count):
        perm = [(i, (i + shift) % rec_count) for i in range(rec_count)]
        received.append(lax.ppermute(plain_here, "rec", perm))
    ordered = []
    for g in range(rec_count):
        choice = received[0]
        for shift in range(1, rec_count):
            choice = jnp.where((rec_index + rec_count - shift) % rec_count == g, received[shift], choice)
        ordered.append(choice)
    everyone = jnp.concatenate(ordered, axis=0)
    partial_value = lax.dot_general(weighted_here, everyone, contract, preferred_element_type=jnp.float32)
    spread = lax.all_to_all(partial_value, "space", split_axis=0, concat_axis=0, tiled=True)
    return jnp.sum(spread, axis=0, keepdims=True)


def solution(mesh):
    in_specs = (P(("rec", "space"), None, None), P(), P(), P())
    out_specs = P(("rec", "space"), None)
    return jax.shard_map(local, mesh=mesh, in_specs=in_specs, out_specs=out_specs, check_vma=False)
```

time: 132 us -> 133 us (level)
  waiting for transfers between devices: 57.6 us -> 35.6 us
  local copies, waits for them, and re-layouts: 23.4 us -> 40.1 us
  matrix products: 8.75 us -> 13.8 us
  other arithmetic: 5.72 us -> 9.64 us
  starting transfers between devices: 18.6 us -> 16.7 us
    all_to_all x1, waiting for transfers between devices: 22.5 us -> 0.01 us  [local(): lax.all_to_all(plain, 'space', split_axis=0, concat_axis=0, tiled=True)]
    reshape x1 -> x7, local copies, waits for them, and re-layouts: 2.8 us -> 21.5 us  [the longest x3 10.8 us: dense_chunks(): main = values[:, :main_cols].reshape(time_count, chunks, per, LANE)]
    another operation x1 -> x0, local copies, waits for them, and re-layouts: 5.51 us -> none  [weighted_chunks(): footprint.reshape(time_count * lat_count, lon_count)]
    concatenate x0 -> x2, other arithmetic: none -> 5.14 us  [dense_chunks(): return jnp.concatenate(pieces, axis=1)]
    dot_general x3, matrix products: 5.27 us -> 9.84 us  [the longest x1 3.74 us: weighted_full(): jnp.einsum('tab,ac->tcb', along_lon.reshape(time_count, lat_count, lon_co...]
    transpose x0 -> x3, local copies, waits for them, and re-layouts: none -> 4.1 us  [the longest x1 4.07 us: dense_chunks(): main = main.transpose(1, 2, 0, 3).reshape(chunks, per * time_count, LANE)]
    slice x0 -> x4, local copies, waits for them, and re-layouts: none -> 4.03 us  [the longest x2 3.18 us: dense_chunks(): main = values[:, :main_cols].reshape(time_count, chunks, per, LANE)]
    unnamed x26 -> x6, local copies, waits for them, and re-layouts: 3.69 us -> 0.01 us
  transfers between devices with their start and end apart: 3 -> 3, of which waited for: 3 -> 2; matrix products, arithmetic and copies ran while one was open for 23% -> 37% of each run, Pallas kernels for 0% -> 0%
where the time goes in v4:
time: 133 us; the launch traced here: 132 us
  local copies, waits for them, and re-layouts  40.1 us (30%)
  waiting for transfers between devices  35.6 us (27%)
  starting transfers between devices  16.7 us (13%)
  blocking collectives  16.5 us (12%)
  matrix products  13.8 us (10%)
  other arithmetic  9.64 us (7%)
    all_to_all x1, waiting for transfers between devices, local(): lax.all_to_all(weighted, 'space', split_axis=0, concat_axis=0, tiled=True)  31.2 us
    all_to_all x1, blocking collectives, local(): lax.all_to_all(partial_value, 'space', split_axis=0, concat_axis=0, tiled...  16.5 us
    reshape x3, local copies, waits for them, and re-layouts, dense_chunks(): main = values[:, :main_cols].reshape(time_count, chunks, per, LANE)  10.8 us
    all_to_all x1, starting transfers between devices, local(): lax.all_to_all(weighted, 'space', split_axis=0, concat_axis=0, tiled=True)  8.4 us
    all_to_all x1, starting transfers between devices, local(): lax.all_to_all(plain, 'space', split_axis=0, concat_axis=0, tiled=True)  8.32 us
    reshape x1, local copies, waits for them, and re-layouts, weighted_full(): footprint.reshape(time_count * lat_count, lon_count)  6.6 us
    concatenate x2, other arithmetic, dense_chunks(): return jnp.concatenate(pieces, axis=1)  5.14 us
    ppermute x1, waiting for transfers between devices, local(): received.append(lax.ppermute(plain_here, 'rec', perm))  4.41 us
  transfers between devices with their start and end apart: 3, of which 2 were waited for; matrix products, arithmetic and copies ran while one was open for 37% of the time, Pallas kernels for 0%

profile of v4, /device:TPU:0, one launch (start us, length us, event | category | flops | bytes accessed | tf_op | source)
XLA Modules:
  0.0 132.5 jit_solution(4152531875079779360)
XLA Ops:
  0.0 0.8 slice.17
  0.8 1.7 %slice.16 = bf16[120,8192]{1,0:T(8,128)(2,1)S(1)} slice(bf16[120,8400]{1,0:T(8,128)(2,1)} %bitcast.41), slice={[0:120], [0:8192]} | slice | bytes 3932160 | tf_op jit(solution)/shard_map/slice | solution.py:15
  2.6 2.7 %reshape.39 = bf16[120,16,4,128]{3,2,1,0:T(4,128)(2,1)} reshape(bf16[120,8192]{1,0:T(8,128)(2,1)S(1)} %slice.16) | data formatting | bytes 3932160 | tf_op jit(solution)/shard_map/reshape | solution.py:15
  5.3 2.8 %copy.18 = bf16[120,16,4,128]{3,0,2,1:T(8,128)(2,1)S(1)} copy(bf16[120,16,4,128]{3,2,1,0:T(4,128)(2,1)} %reshape.39) | data formatting | bytes 3932160 | tf_op jit(solution)/shard_map/reshape | solution.py:15
  8.2 1.8 %maximum_maximum_fusion = bf16[16,496,128]{2,1,0:T(8,128)(2,1)} fusion(bf16[16,15,128]{2,1,0:T(8,128)(2,1)S(1)} %reshape.42, bf16[16,480,128]{2,1,0:T(8,128)(2,1)S(1)} %bitcast.44, bf16[496]{0:T(512)(128)(2,1)S(1)} %pad.16.clone), kind=kLoop, calls=%fused_computation.8 | loop fusion | flops 6094848 | bytes 4060128 | tf_op jit(solution)/shard_map/concatenate | solution.py:28
  10.0 8.3 %all-to-all-start.1 = ((bf16[16,496,128]{2,1,0:T(8,128)(2,1)}), bf16[16,496,128]{2,1,0:T(8,128)(2,1)S(1)}, u32[]{:S(2)}, u32[]{:S(2)}) async-start(bf16[16,496,128]{2,1,0:T(8,128)(2,1)} %maximum_maximum_fusion), calls=%async_computation.1 | async-start | bytes 4063232 | tf_op jit(solution)/shard_map/all_to_all | solution.py:57
  18.3 6.6 %reshape.43 = bf16[8400,120]{1,0:T(8,128)(2,1)} reshape(bf16[120,8400]{1,0:T(8,128)(2,1)} %bitcast.42) | data formatting | bytes 4032000 | tf_op jit(solution)/shard_map/reshape | solution.py:36
  24.9 3.7 %convolution_convert_fusion.1 = bf16[8400,120]{0,1:T(8,128)(2,1)} fusion(bf16[8400,120]{1,0:T(8,128)(2,1)} %reshape.43, bf16[120,120]{1,0:T(8,128)(2,1)S(1)} %copy-done), kind=kOutput, calls=%fused_computation.1 | convolution fusion | flops 242928000 | bytes 4060800 | tf_op jit(solution)/shard_map/dot_general | solution.py:35
  28.6 4.1 %copy.20 = bf16[8400,120]{1,0:T(8,128)(2,1)} copy(bf16[8400,120]{0,1:T(8,128)(2,1)} %convolution_convert_fusion.1) | data formatting | bytes 4032000 | tf_op jit(solution)/shard_map/convert_element_type | solution.py:39
  32.7 4.1 %reshape.44 = bf16[120,70,120]{2,1,0:T(8,128)(2,1)} reshape(bf16[8400,120]{1,0:T(8,128)(2,1)} %copy.20) | data formatting | bytes 4032000 | tf_op jit(solution)/shard_map/reshape | solution.py:42
  36.8 3.7 %convert_bitcast_fusion = bf16[120,70,120]{2,1,0:T(8,128)(2,1)} fusion(bf16[120,70,120]{2,1,0:T(8,128)(2,1)} %reshape.44, bf16[70,70]{1,0:T(8,128)(2,1)S(1)} %copy-done.2), kind=kOutput, calls=%fused_computation.7 | convolution fusion | flops 142128000 | bytes 4041800 | tf_op jit(solution)/shard_map/tab,ac->tcb/dot_general | solution.py:40
  40.6 4.4 %copy.22 = bf16[120,70,120]{0,2,1:T(8,128)(2,1)} copy(bf16[120,70,120]{2,1,0:T(8,128)(2,1)} %convert_bitcast_fusion) | data formatting | bytes 4032000 | tf_op jit(solution)/shard_map/convert_element_type | solution.py:45
  45.0 2.4 %fusion = bf16[120,8400]{1,0:T(8,128)(2,1)S(1)} fusion(bf16[120,8400]{0,1:T(8,128)(2,1)} %bitcast.39, bf16[120,120]{1,0:T(8,128)(2,1)S(1)} %copy-done.1), kind=kOutput, calls=%fused_computation.2 | convolution fusion | flops 242928000 | bytes 4060800 | tf_op jit(solution)/shard_map/dot_general | solution.py:46
  47.4 1.5 %slice.18 = bf16[120,8192]{1,0:T(8,128)(2,1)} slice(bf16[120,8400]{1,0:T(8,128)(2,1)S(1)} %fusion), slice={[0:120], [0:8192]} | slice | bytes 3932160 | tf_op jit(solution)/shard_map/slice | solution.py:15
  48.8 5.3 %reshape.46 = bf16[120,16,4,128]{3,2,1,0:T(4,128)(2,1)} reshape(bf16[120,8192]{1,0:T(8,128)(2,1)} %slice.18) | data formatting | bytes 3932160 | tf_op jit(solution)/shard_map/reshape | solution.py:15
  54.1 4.1 %copy.23 = bf16[16,4,120,128]{3,2,1,0:T(8,128)(2,1)} copy(bf16[16,4,120,128]{3,1,0,2:T(4,128)(2,1)} %bitcast.45) | data formatting | bytes 3932160 | tf_op jit(solution)/shard_map/transpose | solution.py:16
  58.3 3.3 %maximum_maximum_fusion.1 = bf16[16,496,128]{2,1,0:T(8,128)(2,1)} fusion(bf16[16,15,128]{2,1,0:T(8,128)(2,1)S(1)} %reshape.49, bf16[16,480,128]{2,1,0:T(8,128)(2,1)} %bitcast.43, bf16[496]{0:T(512)(128)(2,1)S(1)} %pad.16.clone), kind=kLoop, calls=%fused_computation.9 | loop fusion | flops 6094848 | bytes 4060128 | tf_op jit(solution)/shard_map/concatenate | solution.py:28
  61.6 8.4 %all-to-all-start = ((bf16[16,496,128]{2,1,0:T(8,128)(2,1)}), bf16[16,496,128]{2,1,0:T(8,128)(2,1)}, u32[]{:S(2)}, u32[]{:S(2)}) async-start(bf16[16,496,128]{2,1,0:T(8,128)(2,1)} %maximum_maximum_fusion.1), calls=%async_computation | async-start | bytes 4063232 | tf_op jit(solution)/shard_map/all_to_all | solution.py:59
  70.0 1.8 %copy.25 = bf16[16,496,128]{2,0,1:T(8,128)(2,1)} copy(bf16[16,496,128]{2,1,0:T(8,128)(2,1)S(1)} %all-to-all-done.1) | data formatting | bytes 4063232 | tf_op jit(solution)/shard_map/all_to_all | solution.py:57
  71.9 4.4 %collective-permute-done = bf16[16,496,128]{2,0,1:T(8,128)(2,1)} collective-permute-done((bf16[16,496,128]{2,0,1:T(8,128)(2,1)}, bf16[16,496,128]{2,0,1:T(8,128)(2,1)}, u32[]{:S(2)}, u32[]{:S(2)}) %collective-permute-start) | collective-permute-done | bytes 2031648 | tf_op jit(solution)/shard_map/ppermute | solution.py:65
  76.3 4.0 %broadcast_select_fusion.1 = (bf16[16,496,128]{2,0,1:T(8,128)(2,1)}, bf16[16,496,128]{2,0,1:T(8,128)(2,1)}) fusion(bf16[16,496,128]{2,0,1:T(8,128)(2,1)} %collective-permute-done, pred[]{:T(512)S(6)} %eq.9, bf16[16,496,128]{2,1,0:T(8,128)(2,1)S(1)} %all-to-all-done.1, pred[]{:T(512)S(6)} %eq.10), kind=kLoop, calls=%fused_computation.12 | loop fusion | flops 2031616 | bytes 8126466 | tf_op jit(solution)/shard_map/jit(_where)/select_n | solution.py:70
  80.2 31.2 %all-to-all-done = bf16[16,496,128]{2,1,0:T(8,128)(2,1)} async-done(((bf16[16,496,128]{2,1,0:T(8,128)(2,1)}), bf16[16,496,128]{2,1,0:T(8,128)(2,1)}, u32[]{:S(2)}, u32[]{:S(2)}) %all-to-all-start) | async-done | bytes 2031648 | tf_op jit(solution)/shard_map/all_to_all | solution.py:59
  111.4 3.9 %fusion.1 = f32[16,32,1]{1,0,2:T(8,128)S(1)} fusion(bf16[16,496,128]{2,0,1:T(8,128)(2,1)} %get-tuple-element.10, bf16[16,496,128]{2,0,1:T(8,128)(2,1)} %get-tuple-element.9, bf16[16,496,128]{2,1,0:T(8,128)(2,1)} %all-to-all-done), kind=kOutput, calls=%fused_computation.3 | convolution fusion | flops 73138176 | bytes 6096896 | tf_op jit(solution)/shard_map/dot_general | solution.py:73
  115.4 16.5 %all_to_all.19 = f32[16,1,32]{2,1,0:T(1,128)S(1)} all-to-all(f32[16,1,32]{2,1,0:T(1,128)S(1)} %bitcast.46), channel_id=1, replica_groups=mesh['rec'=2,'space'=16] {'space'}, dimensions={0} | all-to-all | bytes 4096 | tf_op jit(solution)/shard_map/all_to_all | solution.py:74
  (15 shorter events, 0.7 us)
Async XLA Ops:
  0.0 24.9 %copy-start = (bf16[120,120]{1,0:T(8,128)(2,1)S(1)}, bf16[120,120]{1,0:T(8,128)(2,1)}, u32[]{:S(2)}) copy-start(bf16[120,120]{1,0:T(8,128)(2,1)} %param.7) | copy-start | bytes 86404
  10.0 51.6 %all-to-all-start.1 = ((bf16[16,496,128]{2,1,0:T(8,128)(2,1)}), bf16[16,496,128]{2,1,0:T(8,128)(2,1)S(1)}, u32[]{:S(2)}, u32[]{:S(2)}) async-start(bf16[16,496,128]{2,1,0:T(8,128)(2,1)} %maximum_maximum_fusion), calls=%async_computation.1 | async-start | bytes 4063232 | tf_op jit(solution)/shard_map/all_to_all | solution.py:57
  32.7 4.1 %copy-start.2 = (bf16[70,70]{1,0:T(8,128)(2,1)S(1)}, bf16[70,70]{1,0:T(8,128)(2,1)}, u32[]{:S(2)}) copy-start(bf16[70,70]{1,0:T(8,128)(2,1)} %param.6) | copy-start | bytes 29404
  40.6 4.4 %copy-start.1 = (bf16[120,120]{1,0:T(8,128)(2,1)S(1)}, bf16[120,120]{1,0:T(8,128)(2,1)}, u32[]{:S(2)}) copy-start(bf16[120,120]{1,0:T(8,128)(2,1)} %param.5) | copy-start | bytes 86404
  61.6 49.8 %all-to-all-start = ((bf16[16,496,128]{2,1,0:T(8,128)(2,1)}), bf16[16,496,128]{2,1,0:T(8,128)(2,1)}, u32[]{:S(2)}, u32[]{:S(2)}) async-start(bf16[16,496,128]{2,1,0:T(8,128)(2,1)} %maximum_maximum_fusion.1), calls=%async_computation | async-start | bytes 4063232 | tf_op jit(solution)/shard_map/all_to_all | solution.py:59
  71.9 4.4 %collective-permute-start = (bf16[16,496,128]{2,0,1:T(8,128)(2,1)}, bf16[16,496,128]{2,0,1:T(8,128)(2,1)}, u32[]{:S(2)}, u32[]{:S(2)}) collective-permute-start(bf16[16,496,128]{2,0,1:T(8,128)(2,1)} %copy.25), channel_id=1, source_target_pairs={{0,16},{16,0},{1,17},{17,1},{2,18},{18,2},{3,19},{19,3},{4,20},{20... | collective-permute-start | bytes 6094856 | tf_op jit(solution)/shard_map/ppermute | solution.py:65

commit v5 on v4

--- a/solution.py
+++ b/solution.py
@@ -7,31 +7,55 @@
 LANE = 128
 
 
-def dense_chunks(values, chunks):
-    time_count, cell_count = values.shape
+def layout_of(time_count, cell_count, chunks):
     col_tiles = cell_count // LANE
     per = col_tiles // chunks
     main_cols = per * chunks * LANE
-    main = values[:, :main_cols].reshape(time_count, chunks, per, LANE)
-    main = main.transpose(1, 2, 0, 3).reshape(chunks, per * time_count, LANE)
-    rest_tiles = -(-(cell_count - main_cols) // LANE)
-    rest_rows = rest_tiles * time_count
+    full_rows = (time_count // ROW_TILE) * ROW_TILE
+    rest_rows = (time_count - full_rows) * (main_cols // LANE)
+    rest_rows += time_count * (-(-(cell_count - main_cols) // LANE))
     share = -(-rest_rows // chunks)
-    rest = jnp.pad(values[:, main_cols:], ((0, 0), (0, rest_tiles * LANE - (cell_count - main_cols))))
-    rest = rest.reshape(time_count, rest_tiles, LANE).transpose(1, 0, 2).reshape(rest_rows, LANE)
-    rest = jnp.pad(rest, ((0, share * chunks - rest_rows), (0, 0))).reshape(chunks, share, LANE)
-    rows = per * time_count + share
+    rows = per * full_rows + share
     padded_rows = -(-rows // ROW_TILE) * ROW_TILE
+    return per, main_cols, full_rows, share, padded_rows - rows
+
+
+def rest_chunks(low, right, chunks, share):
+    parts = []
+    if low.shape[0]:
+        height = low.shape[0]
+        parts.append(low.reshape(height, -1, LANE).transpose(1, 0, 2).reshape(-1, LANE))
+    if right.shape[1]:
+        height, width = right.shape
+        tiles = -(-width // LANE)
+        right = jnp.pad(right, ((0, 0), (0, tiles * LANE - width)))
+        parts.append(right.reshape(height, tiles, LANE).transpose(1, 0, 2).reshape(-1, LANE))
+    rest = jnp.concatenate(parts, axis=0)
+    rest = jnp.pad(rest, ((0, share * chunks - rest.shape[0]), (0, 0)))
+    return rest.reshape(chunks, share, LANE)
+
+
+def assemble(main, rest, extra, chunks, dtype):
     pieces = [main, rest]
-    if padded_rows > rows:
-        pieces.append(jnp.zeros((chunks, padded_rows - rows, LANE), values.dtype))
+    if extra:
+        pieces.append(jnp.zeros((chunks, extra, LANE), dtype))
     return jnp.concatenate(pieces, axis=1)
 
 
-def weighted_full(footprint, time_cov, lat_cov, lon_cov):
+def dense_chunks(values, chunks):
+    time_count, cell_count = values.shape
+    per, main_cols, full_rows, share, extra = layout_of(time_count, cell_count, chunks)
+    main = jnp.stack([values[:full_rows, j * LANE:(j + 1) * LANE] for j in range(chunks * per)])
+    main = main.reshape(chunks, per * full_rows, LANE)
+    rest = rest_chunks(values[full_rows:, :main_cols], values[:, main_cols:], chunks, share)
+    return assemble(main, rest, extra, chunks, values.dtype)
+
+
+def weighted_dense_chunks(footprint, time_cov, lat_cov, lon_cov, chunks):
     time_count, cell_count = footprint.shape
     lat_count = lat_cov.shape[0]
     lon_count = lon_cov.shape[0]
+    per, main_cols, full_rows, share, extra = layout_of(time_count, cell_count, chunks)
     along_lon = jnp.dot(
         footprint.reshape(time_count * lat_count, lon_count),
         lon_cov,
@@ -43,9 +67,14 @@
         lat_cov,
         preferred_element_type=jnp.float32,
     ).astype(jnp.bfloat16)
-    return jnp.dot(
-        time_cov.T, along_lat.reshape(time_count, cell_count), preferred_element_type=jnp.float32
-    ).astype(jnp.bfloat16)
+    along_lat = along_lat.reshape(time_count, cell_count)
+    main = along_lat[:, :main_cols].reshape(time_count, chunks * per, LANE)
+    main = jnp.einsum("ts,tjl->jsl", time_cov[:, :full_rows], main, preferred_element_type=jnp.float32)
+    main = main.astype(jnp.bfloat16).reshape(chunks, per * full_rows, LANE)
+    low = jnp.dot(time_cov[:, full_rows:].T, along_lat[:, :main_cols], preferred_element_type=jnp.float32)
+    right = jnp.dot(time_cov.T, along_lat[:, main_cols:], preferred_element_type=jnp.float32)
+    rest = rest_chunks(low.astype(jnp.bfloat16), right.astype(jnp.bfloat16), chunks, share)
+    return assemble(main, rest, extra, chunks, jnp.bfloat16)
 
 
 def local(footprints, time_cov, lat_cov, lon_cov):
@@ -55,7 +84,7 @@
     plain = dense_chunks(footprints[0], space_count)
     plain, footprint = lax.optimization_barrier((plain, footprints[0]))
     plain_here = lax.all_to_all(plain, "space", split_axis=0, concat_axis=0, tiled=True)
-    weighted = dense_chunks(weighted_full(footprint, time_cov, lat_cov, lon_cov), space_count)
+    weighted = weighted_dense_chunks(footprint, time_cov, lat_cov, lon_cov, space_count)
     weighted_here = lax.all_to_all(weighted, "space", split_axis=0, concat_axis=0, tiled=True)
     contract = (((1, 2), (1, 2)), ((), ()))
     group = plain_here.shape[0]

time: 133 us -> 177 us (1.33)
  local copies, waits for them, and re-layouts: 40.1 us -> 72.1 us
  waiting for transfers between devices: 35.6 us -> 48 us
  matrix products: 13.8 us -> 10.8 us
    unnamed x6 -> x71, local copies, waits for them, and re-layouts: 0.01 us -> 48.1 us
    all_to_all x1, waiting for transfers between devices: 0.01 us -> 14.6 us  [local(): lax.all_to_all(plain, 'space', split_axis=0, concat_axis=0, tiled=True)]
    reshape x7, local copies, waits for them, and re-layouts: 21.5 us -> 9.81 us  [the longest x1 5.83 us: weighted_dense_chunks(): footprint.reshape(time_count * lat_count, lon_count)]
    transpose x3 -> x0, local copies, waits for them, and re-layouts: 4.1 us -> none  [the longest x1 4.07 us: dense_chunks(): main = main.transpose(1, 2, 0, 3).reshape(chunks, per * time_count, LANE)]
    dot_general x3 -> x5, matrix products: 9.84 us -> 7.47 us  [the longest x1 2.33 us: weighted_dense_chunks(): jnp.einsum('ts,tjl->jsl', time_cov[:, :full_rows], main, preferred_elemen...]
    all_to_all x1, waiting for transfers between devices: 31.2 us -> 28.9 us  [local(): lax.all_to_all(weighted, 'space', split_axis=0, concat_axis=0, tiled=True)]
    concatenate x2 -> x4, other arithmetic: 5.14 us -> 5.07 us  [the longest x2 5.02 us: assemble(): return jnp.concatenate(pieces, axis=1)]
  transfers between devices with their start and end apart: 3 -> 3, of which waited for: 2 -> 3; matrix products, arithmetic and copies ran while one was open for 37% -> 20% of each run, Pallas kernels for 0% -> 0%
where the time goes in v5:
time: 177 us; the launch traced here: 176 us
  local copies, waits for them, and re-layouts  72.1 us (41%)
  waiting for transfers between devices  48 us (27%)
  starting transfers between devices  18.1 us (10%)
  blocking collectives  16.5 us (9%)
  matrix products  10.8 us (6%)
  other arithmetic  10.3 us (6%)
    unnamed x71, local copies, waits for them, and re-layouts  48.1 us
    all_to_all x1, waiting for transfers between devices, local(): lax.all_to_all(weighted, 'space', split_axis=0, concat_axis=0, tiled=True)  28.9 us
    all_to_all x1, blocking collectives, local(): lax.all_to_all(partial_value, 'space', split_axis=0, concat_axis=0, tiled...  16.5 us
    all_to_all x1, waiting for transfers between devices, local(): lax.all_to_all(plain, 'space', split_axis=0, concat_axis=0, tiled=True)  14.6 us
    all_to_all x1, starting transfers between devices, local(): lax.all_to_all(weighted, 'space', split_axis=0, concat_axis=0, tiled=True)  9.71 us
    all_to_all x1, starting transfers between devices, local(): lax.all_to_all(plain, 'space', split_axis=0, concat_axis=0, tiled=True)  8.36 us
    reshape x1, local copies, waits for them, and re-layouts, weighted_dense_chunks(): footprint.reshape(time_count * lat_count, lon_count)  5.83 us
    concatenate x2, other arithmetic, assemble(): return jnp.concatenate(pieces, axis=1)  5.02 us
  transfers between devices with their start and end apart: 3, of which 3 were waited for; matrix products, arithmetic and copies ran while one was open for 20% of the time, Pallas kernels for 0%

profile of v5, /device:TPU:0, one launch (start us, length us, event | category | flops | bytes accessed | tf_op | source)
XLA Modules:
  0.0 175.9 jit_solution(15604843069733904616)
XLA Ops:
  4.7 1.4 constant_dynamic-update-slice_fusion.61
  6.1 1.4 constant_dynamic-update-slice_fusion.60
  7.4 1.4 constant_dynamic-update-slice_fusion.59
  8.8 1.4 constant_dynamic-update-slice_fusion.58
  10.2 1.4 constant_dynamic-update-slice_fusion.57
  50.8 3.2 %maximum_maximum_fusion = bf16[16,496,128]{2,1,0:T(8,128)(2,1)} fusion(bf16[16,47,128]{2,1,0:T(8,128)(2,1)S(1)} %reshape.55, bf16[16,448,128]{2,1,0:T(8,128)(2,1)} %bitcast.383, bf16[496]{0:T(512)(128)(2,1)S(1)} %pad.18.clone), kind=kLoop, calls=%fused_computation.7 | loop fusion | flops 6094848 | bytes 4060128 | tf_op jit(solution)/shard_map/concatenate | solution.py:42
  54.0 8.4 %all-to-all-start.1 = ((bf16[16,496,128]{2,1,0:T(8,128)(2,1)}), bf16[16,496,128]{2,1,0:T(8,128)(2,1)}, u32[]{:S(2)}, u32[]{:S(2)}) async-start(bf16[16,496,128]{2,1,0:T(8,128)(2,1)} %maximum_maximum_fusion), calls=%async_computation.1 | async-start | bytes 4063232 | tf_op jit(solution)/shard_map/all_to_all | solution.py:86
  62.4 5.8 %reshape.56 = bf16[8400,120]{1,0:T(8,128)(2,1)S(1)} reshape(bf16[120,8400]{1,0:T(8,128)(2,1)} %bitcast.330) | data formatting | bytes 4032000 | tf_op jit(solution)/shard_map/reshape | solution.py:60
  68.2 2.1 %convolution_convert_fusion = bf16[8400,120]{0,1:T(8,128)(2,1)} fusion(bf16[8400,120]{1,0:T(8,128)(2,1)S(1)} %reshape.56, bf16[120,120]{1,0:T(8,128)(2,1)S(1)} %copy-done), kind=kOutput, calls=%fused_computation | convolution fusion | flops 242928000 | bytes 4060800 | tf_op jit(solution)/shard_map/dot_general | solution.py:59
  70.3 4.1 %copy.22 = bf16[8400,120]{1,0:T(8,128)(2,1)} copy(bf16[8400,120]{0,1:T(8,128)(2,1)} %convolution_convert_fusion) | data formatting | bytes 4032000 | tf_op jit(solution)/shard_map/convert_element_type | solution.py:63
  74.4 2.8 %reshape.57 = bf16[120,70,120]{2,1,0:T(8,128)(2,1)S(1)} reshape(bf16[8400,120]{1,0:T(8,128)(2,1)} %copy.22) | data formatting | bytes 4032000 | tf_op jit(solution)/shard_map/reshape | solution.py:66
  77.2 2.1 %convert_bitcast_fusion = bf16[120,70,120]{2,1,0:T(8,128)(2,1)} fusion(bf16[120,70,120]{2,1,0:T(8,128)(2,1)S(1)} %reshape.57, bf16[70,70]{1,0:T(8,128)(2,1)S(1)} %copy-done.3), kind=kOutput, calls=%fused_computation.6 | convolution fusion | flops 142128000 | bytes 4041800 | tf_op jit(solution)/shard_map/tab,ac->tcb/dot_general | solution.py:64
  79.4 3.6 %copy.24 = bf16[120,70,120]{0,2,1:T(8,128)(2,1)S(1)} copy(bf16[120,70,120]{2,1,0:T(8,128)(2,1)} %convert_bitcast_fusion) | data formatting | bytes 4032000 | tf_op jit(solution)/shard_map/convert_element_type | solution.py:69
  83.0 1.5 slice.347
  85.6 2.3 %convolution_convert_fusion.2 = bf16[64,128,112]{1,2,0:T(8,128)(2,1)S(1)} fusion(bf16[120,64,128]{0,2,1:T(8,128)(2,1)} %bitcast.314, bf16[120,120]{1,0:T(8,128)(2,1)S(1)} %copy-done.2), kind=kOutput, calls=%fused_computation.12 | convolution fusion | flops 221118464 | bytes 3829888 | tf_op jit(solution)/shard_map/ts,tjl->jsl/dot_general | solution.py:72
  88.0 1.8 %maximum_maximum_fusion.1 = bf16[16,496,128]{2,1,0:T(8,128)(2,1)} fusion(bf16[16,47,128]{2,1,0:T(8,128)(2,1)S(1)} %reshape.65, bf16[16,448,128]{2,1,0:T(8,128)(2,1)S(1)} %bitcast.382, bf16[496]{0:T(512)(128)(2,1)S(1)} %pad.18.clone), kind=kLoop, calls=%fused_computation.8 | loop fusion | flops 6094848 | bytes 4060128 | tf_op jit(solution)/shard_map/concatenate | solution.py:42
  89.7 14.6 %all-to-all-done.1 = bf16[16,496,128]{2,1,0:T(8,128)(2,1)} async-done(((bf16[16,496,128]{2,1,0:T(8,128)(2,1)}), bf16[16,496,128]{2,1,0:T(8,128)(2,1)}, u32[]{:S(2)}, u32[]{:S(2)}) %all-to-all-start.1) | async-done | bytes 2031648 | tf_op jit(solution)/shard_map/all_to_all | solution.py:86
  104.4 9.7 %all-to-all-start = ((bf16[16,496,128]{2,1,0:T(8,128)(2,1)}), bf16[16,496,128]{2,1,0:T(8,128)(2,1)S(1)}, u32[]{:S(2)}, u32[]{:S(2)}) async-start(bf16[16,496,128]{2,1,0:T(8,128)(2,1)} %maximum_maximum_fusion.1), calls=%async_computation | async-start | bytes 4063232 | tf_op jit(solution)/shard_map/all_to_all | solution.py:88
  114.1 3.4 %copy.29 = bf16[16,496,128]{2,0,1:T(8,128)(2,1)} copy(bf16[16,496,128]{2,1,0:T(8,128)(2,1)} %all-to-all-done.1) | data formatting | bytes 4063232 | tf_op jit(solution)/shard_map/all_to_all | solution.py:86
  117.5 4.4 %collective-permute-done = bf16[16,496,128]{2,0,1:T(8,128)(2,1)} collective-permute-done((bf16[16,496,128]{2,0,1:T(8,128)(2,1)}, bf16[16,496,128]{2,0,1:T(8,128)(2,1)}, u32[]{:S(2)}, u32[]{:S(2)}) %collective-permute-start) | collective-permute-done | bytes 2031648 | tf_op jit(solution)/shard_map/ppermute | solution.py:94
  121.9 4.6 %broadcast_select_fusion.1 = (bf16[16,496,128]{2,0,1:T(8,128)(2,1)}, bf16[16,496,128]{2,0,1:T(8,128)(2,1)}) fusion(bf16[16,496,128]{2,0,1:T(8,128)(2,1)} %collective-permute-done, pred[]{:T(512)S(6)} %eq.9, bf16[16,496,128]{2,1,0:T(8,128)(2,1)} %all-to-all-done.1, pred[]{:T(512)S(6)} %eq.10), kind=kLoop, calls=%fused_computation.11 | loop fusion | flops 2031616 | bytes 8126466 | tf_op jit(solution)/shard_map/jit(_where)/select_n | solution.py:99
  126.5 28.9 %all-to-all-done = bf16[16,496,128]{2,1,0:T(8,128)(2,1)S(1)} async-done(((bf16[16,496,128]{2,1,0:T(8,128)(2,1)}), bf16[16,496,128]{2,1,0:T(8,128)(2,1)S(1)}, u32[]{:S(2)}, u32[]{:S(2)}) %all-to-all-start) | async-done | bytes 2031648 | tf_op jit(solution)/shard_map/all_to_all | solution.py:88
  155.5 3.3 %fusion = f32[16,32,1]{1,0,2:T(8,128)S(1)} fusion(bf16[16,496,128]{2,0,1:T(8,128)(2,1)} %get-tuple-element.10, bf16[16,496,128]{2,0,1:T(8,128)(2,1)} %get-tuple-element.9, bf16[16,496,128]{2,1,0:T(8,128)(2,1)S(1)} %all-to-all-done), kind=kOutput, calls=%fused_computation.2 | convolution fusion | flops 73138176 | bytes 6096896 | tf_op jit(solution)/shard_map/dot_general | solution.py:102
  158.8 16.5 %all_to_all.19 = f32[16,1,32]{2,1,0:T(1,128)S(1)} all-to-all(f32[16,1,32]{2,1,0:T(1,128)S(1)} %bitcast.387), channel_id=1, replica_groups=mesh['rec'=2,'space'=16] {'space'}, dimensions={0} | all-to-all | bytes 4096 | tf_op jit(solution)/shard_map/all_to_all | solution.py:103
  (81 shorter events, 45.6 us)
Async XLA Ops:
  0.0 68.2 %copy-start = (bf16[120,120]{1,0:T(8,128)(2,1)S(1)}, bf16[120,120]{1,0:T(8,128)(2,1)}, u32[]{:S(2)}) copy-start(bf16[120,120]{1,0:T(8,128)(2,1)} %param.7) | copy-start | bytes 86404
  0.0 19.6 %copy-start.1 = (bf16[1,120,8400]{2,1,0:T(8,128)(2,1)S(1)}, bf16[1,120,8400]{2,1,0:T(8,128)(2,1)}, u32[]{:S(2)}) copy-start(bf16[1,120,8400]{2,1,0:T(8,128)(2,1)} %param.4) | copy-start | bytes 6048004
  54.0 50.4 %all-to-all-start.1 = ((bf16[16,496,128]{2,1,0:T(8,128)(2,1)}), bf16[16,496,128]{2,1,0:T(8,128)(2,1)}, u32[]{:S(2)}, u32[]{:S(2)}) async-start(bf16[16,496,128]{2,1,0:T(8,128)(2,1)} %maximum_maximum_fusion), calls=%async_computation.1 | async-start | bytes 4063232 | tf_op jit(solution)/shard_map/all_to_all | solution.py:86
  74.4 2.8 %copy-start.3 = (bf16[70,70]{1,0:T(8,128)(2,1)S(1)}, bf16[70,70]{1,0:T(8,128)(2,1)}, u32[]{:S(2)}) copy-start(bf16[70,70]{1,0:T(8,128)(2,1)} %param.6) | copy-start | bytes 29404
  83.0 1.5 copy-start.2
  104.4 51.1 %all-to-all-start = ((bf16[16,496,128]{2,1,0:T(8,128)(2,1)}), bf16[16,496,128]{2,1,0:T(8,128)(2,1)S(1)}, u32[]{:S(2)}, u32[]{:S(2)}) async-start(bf16[16,496,128]{2,1,0:T(8,128)(2,1)} %maximum_maximum_fusion.1), calls=%async_computation | async-start | bytes 4063232 | tf_op jit(solution)/shard_map/all_to_all | solution.py:88
  117.5 4.4 %collective-permute-start = (bf16[16,496,128]{2,0,1:T(8,128)(2,1)}, bf16[16,496,128]{2,0,1:T(8,128)(2,1)}, u32[]{:S(2)}, u32[]{:S(2)}) collective-permute-start(bf16[16,496,128]{2,0,1:T(8,128)(2,1)} %copy.29), channel_id=1, source_target_pairs={{0,16},{16,0},{1,17},{17,1},{2,18},{18,2},{3,19},{19,3},{4,20},{20... | collective-permute-start | bytes 6094856 | tf_op jit(solution)/shard_map/ppermute | solution.py:94

commit v6 on v5

--- a/solution.py
+++ b/solution.py
@@ -1,7 +1,10 @@
+import functools
 import jax
 import jax.numpy as jnp
 from jax import lax
 from jax.sharding import PartitionSpec as P
+from jax.experimental import pallas as pl
+from jax.experimental.pallas import tpu as pltpu
 
 ROW_TILE = 16
 LANE = 128
@@ -42,13 +45,29 @@
     return jnp.concatenate(pieces, axis=1)
 
 
+def pack_kernel(full_rows, per, values_ref, rest_ref, out_ref):
+    chunks = out_ref.shape[0]
+    for k in range(chunks):
+        for q in range(per):
+            j = k * per + q
+            out_ref[k, q * full_rows:(q + 1) * full_rows, :] = values_ref[0:full_rows, j * LANE:(j + 1) * LANE]
+        out_ref[k, per * full_rows:, :] = rest_ref[k]
+
+
 def dense_chunks(values, chunks):
     time_count, cell_count = values.shape
     per, main_cols, full_rows, share, extra = layout_of(time_count, cell_count, chunks)
-    main = jnp.stack([values[:full_rows, j * LANE:(j + 1) * LANE] for j in range(chunks * per)])
-    main = main.reshape(chunks, per * full_rows, LANE)
     rest = rest_chunks(values[full_rows:, :main_cols], values[:, main_cols:], chunks, share)
-    return assemble(main, rest, extra, chunks, values.dtype)
+    if extra:
+        rest = jnp.pad(rest, ((0, 0), (0, extra), (0, 0)))
+    rows = per * full_rows + share + extra
+    return pl.pallas_call(
+        functools.partial(pack_kernel, full_rows, per),
+        out_shape=jax.ShapeDtypeStruct((chunks, rows, LANE), values.dtype),
+        in_specs=[pl.BlockSpec(memory_space=pltpu.VMEM)] * 2,
+        out_specs=pl.BlockSpec(memory_space=pltpu.VMEM),
+        cost_estimate=pl.CostEstimate(flops=0, transcendentals=0, bytes_accessed=4 * chunks * rows * LANE),
+    )(values, rest)
 
 
 def weighted_dense_chunks(footprint, time_cov, lat_cov, lon_cov, chunks):

time: 177 us -> 128 us (0.72)
  local copies, waits for them, and re-layouts: 72.1 us -> 18.6 us
  waiting for transfers between devices: 48 us -> 52.9 us
  other arithmetic: 10.3 us -> 7.06 us
  Pallas kernels: 0 us -> 3.17 us
    unnamed x71 -> x8, local copies, waits for them, and re-layouts: 48.1 us -> 0.02 us
    all_to_all x1 -> x0, local copies, waits for them, and re-layouts: 3.4 us -> none  [local(): lax.all_to_all(plain, 'space', split_axis=0, concat_axis=0, tiled=True)]
    all_to_all x1, waiting for transfers between devices: 28.9 us -> 32.2 us  [local(): lax.all_to_all(weighted, 'space', split_axis=0, concat_axis=0, tiled=True)]
    concatenate x2 -> x1, other arithmetic: 5.02 us -> 1.79 us  [assemble(): return jnp.concatenate(pieces, axis=1)]
    pallas_call x0 -> x1, Pallas kernels: none -> 3.17 us  [dense_chunks(): pl.pallas_call(functools.partial(pack_kernel, full_rows, per), out_shape=...]
    concatenate x0 -> x1, other arithmetic: none -> 2.24 us  [local(): everyone = jnp.concatenate(ordered, axis=0)]
    select_n x1, other arithmetic: 4.64 us -> 2.44 us  [local(): jnp.where((rec_index + rec_count - shift) % rec_count == g, received[shif...]
  transfers between devices with their start and end apart: 3 -> 3, of which waited for: 3 -> 3; matrix products, arithmetic and copies ran while one was open for 20% -> 24% of each run, Pallas kernels for 0% -> 0%
where the time goes in v6:
time: 128 us
  waiting for transfers between devices  52.9 us (41%)
  local copies, waits for them, and re-layouts  18.6 us (15%)
  starting transfers between devices  18.3 us (14%)
  blocking collectives  16.5 us (13%)
  matrix products  11.1 us (9%)
  other arithmetic  7.06 us (6%)
  Pallas kernels  3.17 us (2%)
    all_to_all x1, waiting for transfers between devices, local(): lax.all_to_all(weighted, 'space', split_axis=0, concat_axis=0, tiled=True)  32.2 us
    all_to_all x1, blocking collectives, local(): lax.all_to_all(partial_value, 'space', split_axis=0, concat_axis=0, tiled...  16.5 us
    all_to_all x1, waiting for transfers between devices, local(): lax.all_to_all(plain, 'space', split_axis=0, concat_axis=0, tiled=True)  16.3 us
    all_to_all x1, starting transfers between devices, local(): lax.all_to_all(weighted, 'space', split_axis=0, concat_axis=0, tiled=True)  9.71 us
    all_to_all x1, starting transfers between devices, local(): lax.all_to_all(plain, 'space', split_axis=0, concat_axis=0, tiled=True)  8.49 us
    reshape x1, local copies, waits for them, and re-layouts, weighted_dense_chunks(): footprint.reshape(time_count * lat_count, lon_count)  5.5 us
    ppermute x1, waiting for transfers between devices, local(): received.append(lax.ppermute(plain_here, 'rec', perm))  4.38 us
    convert_element_type x1, local copies, waits for them, and re-layouts, weighted_dense_chunks(): along_lat = jnp.einsum('tab,ac->tcb', along_lon.reshape(time_count, lat_c...  3.59 us
  transfers between devices with their start and end apart: 3, of which 3 were waited for; matrix products, arithmetic and copies ran while one was open for 24% of the time, Pallas kernels for 0%

profile of v6, /device:TPU:0, one launch (start us, length us, event | category | flops | bytes accessed | tf_op | source)
XLA Modules:
  0.0 127.8 jit_solution(11662499953913864045)
XLA Ops:
  0.0 0.8 slice.26
  0.8 0.9 slice_bitcast_fusion
  1.9 0.7 pad.12.rest_ref
  2.6 3.2 %shard_map.46 = bf16[16,496,128]{2,1,0:T(8,128)(2,1)} custom-call(bf16[120,8400]{1,0:T(8,128)(2,1)} %bitcast.53, bf16[16,48,128]{2,1,0:T(8,128)(2,1)} %pad.12.rest_ref), custom_call_target="tpu_custom_call" | custom-call | bytes 4063232 | tf_op jit(solution)/shard_map/pallas_call | solution.py:64
  5.8 8.5 %all-to-all-start.1 = ((bf16[16,496,128]{2,1,0:T(8,128)(2,1)}), bf16[16,496,128]{2,1,0:T(8,128)(2,1)}, u32[]{:S(2)}, u32[]{:S(2)}) async-start(bf16[16,496,128]{2,1,0:T(8,128)(2,1)} %shard_map.46), calls=%async_computation.1 | async-start | bytes 4063232 | tf_op jit(solution)/shard_map/all_to_all | solution.py:105
  14.3 5.5 %reshape.52 = bf16[8400,120]{1,0:T(8,128)(2,1)} reshape(bf16[120,8400]{1,0:T(8,128)(2,1)S(1)} %bitcast.54) | data formatting | bytes 4032000 | tf_op jit(solution)/shard_map/reshape | solution.py:79
  19.8 2.4 %convolution_convert_fusion = bf16[8400,120]{0,1:T(8,128)(2,1)S(1)} fusion(bf16[8400,120]{1,0:T(8,128)(2,1)} %reshape.52, bf16[120,120]{1,0:T(8,128)(2,1)S(1)} %copy-done), kind=kOutput, calls=%fused_computation | convolution fusion | flops 242928000 | bytes 4060800 | tf_op jit(solution)/shard_map/dot_general | solution.py:78
  22.2 2.4 %copy.23 = bf16[8400,120]{1,0:T(8,128)(2,1)} copy(bf16[8400,120]{0,1:T(8,128)(2,1)S(1)} %convolution_convert_fusion) | data formatting | bytes 4032000 | tf_op jit(solution)/shard_map/convert_element_type | solution.py:82
  24.6 2.8 %reshape.53 = bf16[120,70,120]{2,1,0:T(8,128)(2,1)S(1)} reshape(bf16[8400,120]{1,0:T(8,128)(2,1)} %copy.23) | data formatting | bytes 4032000 | tf_op jit(solution)/shard_map/reshape | solution.py:85
  27.4 2.1 %convert_bitcast_fusion = bf16[120,70,120]{2,1,0:T(8,128)(2,1)} fusion(bf16[120,70,120]{2,1,0:T(8,128)(2,1)S(1)} %reshape.53, bf16[70,70]{1,0:T(8,128)(2,1)S(1)} %copy-done.3), kind=kOutput, calls=%fused_computation.5 | convolution fusion | flops 142128000 | bytes 4041800 | tf_op jit(solution)/shard_map/tab,ac->tcb/dot_general | solution.py:83
  29.5 3.6 %copy.25 = bf16[120,70,120]{0,2,1:T(8,128)(2,1)S(1)} copy(bf16[120,70,120]{2,1,0:T(8,128)(2,1)} %convert_bitcast_fusion) | data formatting | bytes 4032000 | tf_op jit(solution)/shard_map/convert_element_type | solution.py:88
  33.1 1.5 %slice.27 = bf16[120,8192]{0,1:T(8,128)(2,1)} slice(bf16[120,8400]{0,1:T(8,128)(2,1)S(1)} %bitcast.48), slice={[0:120], [0:8192]} | slice | bytes 3932160 | tf_op jit(solution)/shard_map/slice | solution.py:90
  34.9 0.7 fusion.3
  35.9 2.3 %convolution_convert_fusion.2 = bf16[64,128,112]{1,2,0:T(8,128)(2,1)S(1)} fusion(bf16[120,64,128]{0,2,1:T(8,128)(2,1)} %bitcast.55, bf16[120,120]{1,0:T(8,128)(2,1)S(1)} %copy-done.2), kind=kOutput, calls=%fused_computation.10 | convolution fusion | flops 221118464 | bytes 3829888 | tf_op jit(solution)/shard_map/ts,tjl->jsl/dot_general | solution.py:91
  38.2 1.8 %maximum_maximum_fusion = bf16[16,496,128]{2,1,0:T(8,128)(2,1)} fusion(bf16[16,47,128]{2,1,0:T(8,128)(2,1)S(1)} %reshape.61, bf16[16,448,128]{2,1,0:T(8,128)(2,1)S(1)} %bitcast.56, bf16[496]{0:T(512)(128)(2,1)S(1)} %pad.18.clone), kind=kLoop, calls=%fused_computation.6 | loop fusion | flops 6094848 | bytes 4060128 | tf_op jit(solution)/shard_map/concatenate | solution.py:45
  40.0 16.3 %all-to-all-done.1 = bf16[16,496,128]{2,1,0:T(8,128)(2,1)} async-done(((bf16[16,496,128]{2,1,0:T(8,128)(2,1)}), bf16[16,496,128]{2,1,0:T(8,128)(2,1)}, u32[]{:S(2)}, u32[]{:S(2)}) %all-to-all-start.1) | async-done | bytes 2031648 | tf_op jit(solution)/shard_map/all_to_all | solution.py:105
  56.3 9.7 %all-to-all-start = ((bf16[16,496,128]{2,1,0:T(8,128)(2,1)}), bf16[16,496,128]{2,1,0:T(8,128)(2,1)S(1)}, u32[]{:S(2)}, u32[]{:S(2)}) async-start(bf16[16,496,128]{2,1,0:T(8,128)(2,1)} %maximum_maximum_fusion), calls=%async_computation | async-start | bytes 4063232 | tf_op jit(solution)/shard_map/all_to_all | solution.py:107
  66.1 4.4 %collective-permute-done = bf16[16,496,128]{2,1,0:T(8,128)(2,1)} collective-permute-done((bf16[16,496,128]{2,1,0:T(8,128)(2,1)}, bf16[16,496,128]{2,1,0:T(8,128)(2,1)}, u32[]{:S(2)}, u32[]{:S(2)}) %collective-permute-start) | collective-permute-done | bytes 2031648 | tf_op jit(solution)/shard_map/ppermute | solution.py:113
  70.5 2.4 %broadcast_select_fusion.1 = (bf16[16,496,128]{2,1,0:T(8,128)(2,1)S(1)}, bf16[16,496,128]{2,1,0:T(8,128)(2,1)S(1)}) fusion(bf16[16,496,128]{2,1,0:T(8,128)(2,1)} %collective-permute-done, bf16[16,496,128]{2,1,0:T(8,128)(2,1)} %all-to-all-done.1, pred[]{:T(512)S(6)} %eq.9, pred[]{:T(512)S(6)} %eq.10), kind=kLoop, calls=%fused_computation.9 | loop fusion | flops 2031616 | bytes 8126466 | tf_op jit(solution)/shard_map/jit(_where)/select_n | solution.py:118
  72.9 2.2 %pad_maximum_fusion = bf16[32,496,128]{2,1,0:T(8,128)(2,1)} fusion(bf16[16,496,128]{2,1,0:T(8,128)(2,1)S(1)} %get-tuple-element.10, bf16[16,496,128]{2,1,0:T(8,128)(2,1)S(1)} %get-tuple-element.9), kind=kLoop, calls=%fused_computation.2 | loop fusion | flops 2031616 | bytes 8126464 | tf_op jit(solution)/shard_map/concatenate | solution.py:120
  75.2 32.2 %all-to-all-done = bf16[16,496,128]{2,1,0:T(8,128)(2,1)S(1)} async-done(((bf16[16,496,128]{2,1,0:T(8,128)(2,1)}), bf16[16,496,128]{2,1,0:T(8,128)(2,1)S(1)}, u32[]{:S(2)}, u32[]{:S(2)}) %all-to-all-start) | async-done | bytes 2031648 | tf_op jit(solution)/shard_map/all_to_all | solution.py:107
  107.4 3.3 %fusion = f32[16,32,1]{1,0,2:T(8,128)S(1)} fusion(bf16[32,496,128]{2,1,0:T(8,128)(2,1)} %pad_maximum_fusion, bf16[16,496,128]{2,1,0:T(8,128)(2,1)S(1)} %all-to-all-done), kind=kOutput, calls=%fused_computation.3 | convolution fusion | flops 65011712 | bytes 6096896 | tf_op jit(solution)/shard_map/dot_general | solution.py:121
  110.7 16.5 %all_to_all.19 = f32[16,1,32]{2,1,0:T(1,128)S(1)} all-to-all(f32[16,1,32]{2,1,0:T(1,128)S(1)} %bitcast.61), channel_id=1, replica_groups=mesh['rec'=2,'space'=16] {'space'}, dimensions={0} | all-to-all | bytes 4096 | tf_op jit(solution)/shard_map/all_to_all | solution.py:122
  127.2 0.5 reduce_sum.9
  (20 shorter events, 0.7 us)
Async XLA Ops:
  0.0 19.8 %copy-start = (bf16[120,120]{1,0:T(8,128)(2,1)S(1)}, bf16[120,120]{1,0:T(8,128)(2,1)}, u32[]{:S(2)}) copy-start(bf16[120,120]{1,0:T(8,128)(2,1)} %param.7) | copy-start | bytes 86404
  5.8 8.5 %copy-start.1 = (bf16[1,120,8400]{2,1,0:T(8,128)(2,1)S(1)}, bf16[1,120,8400]{2,1,0:T(8,128)(2,1)}, u32[]{:S(2)}) copy-start(bf16[1,120,8400]{2,1,0:T(8,128)(2,1)} %param.4) | copy-start | bytes 6048004
  5.8 50.5 %all-to-all-start.1 = ((bf16[16,496,128]{2,1,0:T(8,128)(2,1)}), bf16[16,496,128]{2,1,0:T(8,128)(2,1)}, u32[]{:S(2)}, u32[]{:S(2)}) async-start(bf16[16,496,128]{2,1,0:T(8,128)(2,1)} %shard_map.46), calls=%async_computation.1 | async-start | bytes 4063232 | tf_op jit(solution)/shard_map/all_to_all | solution.py:105
  24.6 2.8 %copy-start.3 = (bf16[70,70]{1,0:T(8,128)(2,1)S(1)}, bf16[70,70]{1,0:T(8,128)(2,1)}, u32[]{:S(2)}) copy-start(bf16[70,70]{1,0:T(8,128)(2,1)} %param.6) | copy-start | bytes 29404
  33.1 1.5 %copy-start.2 = (bf16[120,120]{1,0:T(8,128)(2,1)S(1)}, bf16[120,120]{1,0:T(8,128)(2,1)}, u32[]{:S(2)}) copy-start(bf16[120,120]{1,0:T(8,128)(2,1)} %param.5) | copy-start | bytes 86404
  56.3 51.1 %all-to-all-start = ((bf16[16,496,128]{2,1,0:T(8,128)(2,1)}), bf16[16,496,128]{2,1,0:T(8,128)(2,1)S(1)}, u32[]{:S(2)}, u32[]{:S(2)}) async-start(bf16[16,496,128]{2,1,0:T(8,128)(2,1)} %maximum_maximum_fusion), calls=%async_computation | async-start | bytes 4063232 | tf_op jit(solution)/shard_map/all_to_all | solution.py:107
  66.0 4.5 %collective-permute-start = (bf16[16,496,128]{2,1,0:T(8,128)(2,1)}, bf16[16,496,128]{2,1,0:T(8,128)(2,1)}, u32[]{:S(2)}, u32[]{:S(2)}) collective-permute-start(bf16[16,496,128]{2,1,0:T(8,128)(2,1)} %all-to-all-done.1), channel_id=1, source_target_pairs={{0,16},{16,0},{1,17},{17,1},{2,18},{18,2},{3,19},{19,3},{4,20},{20... | collective-permute-start | bytes 6094856 | tf_op jit(solution)/shard_map/ppermute | solution.py:113

commit v7 on v6

--- a/solution.py
+++ b/solution.py
@@ -45,29 +45,44 @@
     return jnp.concatenate(pieces, axis=1)
 
 
-def pack_kernel(full_rows, per, values_ref, rest_ref, out_ref):
-    chunks = out_ref.shape[0]
+def pack_kernel(full_rows, per, share, values_ref, out_ref, rest_ref):
+    time_count, cell_count = values_ref.shape
+    chunks, rows, _ = out_ref.shape
+    main_tiles = chunks * per
+    main_cols = main_tiles * LANE
     for k in range(chunks):
         for q in range(per):
             j = k * per + q
             out_ref[k, q * full_rows:(q + 1) * full_rows, :] = values_ref[0:full_rows, j * LANE:(j + 1) * LANE]
-        out_ref[k, per * full_rows:, :] = rest_ref[k]
+    rest_ref[...] = jnp.zeros(rest_ref.shape, rest_ref.dtype)
+    low = time_count - full_rows
+    at = 0
+    if low:
+        for j in range(main_tiles):
+            rest_ref[at:at + low, :] = values_ref[full_rows:time_count, j * LANE:(j + 1) * LANE].astype(jnp.float32)
+            at += low
+    for lo in range(main_cols, cell_count, LANE):
+        width = min(LANE, cell_count - lo)
+        rest_ref[at:at + time_count, 0:width] = values_ref[:, lo:lo + width].astype(jnp.float32)
+        at += time_count
+    for k in range(chunks):
+        out_ref[k, per * full_rows:per * full_rows + share, :] = rest_ref[k * share:(k + 1) * share, :].astype(out_ref.dtype)
+        if rows > per * full_rows + share:
+            out_ref[k, per * full_rows + share:, :] = jnp.zeros((rows - per * full_rows - share, LANE), out_ref.dtype)
 
 
 def dense_chunks(values, chunks):
     time_count, cell_count = values.shape
     per, main_cols, full_rows, share, extra = layout_of(time_count, cell_count, chunks)
-    rest = rest_chunks(values[full_rows:, :main_cols], values[:, main_cols:], chunks, share)
-    if extra:
-        rest = jnp.pad(rest, ((0, 0), (0, extra), (0, 0)))
     rows = per * full_rows + share + extra
     return pl.pallas_call(
-        functools.partial(pack_kernel, full_rows, per),
+        functools.partial(pack_kernel, full_rows, per, share),
         out_shape=jax.ShapeDtypeStruct((chunks, rows, LANE), values.dtype),
-        in_specs=[pl.BlockSpec(memory_space=pltpu.VMEM)] * 2,
+        in_specs=[pl.BlockSpec(memory_space=pltpu.VMEM)],
         out_specs=pl.BlockSpec(memory_space=pltpu.VMEM),
+        scratch_shapes=[pltpu.VMEM((share * chunks, LANE), jnp.float32)],
         cost_estimate=pl.CostEstimate(flops=0, transcendentals=0, bytes_accessed=4 * chunks * rows * LANE),
-    )(values, rest)
+    )(values)
 
 
 def weighted_dense_chunks(footprint, time_cov, lat_cov, lon_cov, chunks):

time: 128 us -> 126 us (0.984)
  waiting for transfers between devices: 52.9 us -> 51.1 us
    all_to_all x1, waiting for transfers between devices: 16.3 us -> 14.5 us  [local(): lax.all_to_all(plain, 'space', split_axis=0, concat_axis=0, tiled=True)]
    convert_element_type x1, local copies, waits for them, and re-layouts: 2.39 us -> 4.09 us  [weighted_dense_chunks(): along_lon = jnp.dot(footprint.reshape(time_count * lat_count, lon_count),...]
  transfers between devices with their start and end apart: 3 -> 3, of which waited for: 3 -> 3; matrix products, arithmetic and copies ran while one was open for 24% -> 26% of each run, Pallas kernels for 0% -> 0%
where the time goes in v7:
time: 126 us; the launch traced here: 125 us
  waiting for transfers between devices  51.1 us (41%)
  local copies, waits for them, and re-layouts  18.1 us (14%)
  starting transfers between devices  18.1 us (14%)
  blocking collectives  16.5 us (13%)
  matrix products  10.8 us (9%)
  other arithmetic  7.05 us (6%)
  Pallas kernels  3.23 us (3%)
    all_to_all x1, waiting for transfers between devices, local(): lax.all_to_all(weighted, 'space', split_axis=0, concat_axis=0, tiled=True)  32.2 us
    all_to_all x1, blocking collectives, local(): lax.all_to_all(partial_value, 'space', split_axis=0, concat_axis=0, tiled...  16.5 us
    all_to_all x1, waiting for transfers between devices, local(): lax.all_to_all(plain, 'space', split_axis=0, concat_axis=0, tiled=True)  14.5 us
    all_to_all x1, starting transfers between devices, local(): lax.all_to_all(weighted, 'space', split_axis=0, concat_axis=0, tiled=True)  9.71 us
    all_to_all x1, starting transfers between devices, local(): lax.all_to_all(plain, 'space', split_axis=0, concat_axis=0, tiled=True)  8.36 us
    reshape x1, local copies, waits for them, and re-layouts, weighted_dense_chunks(): footprint.reshape(time_count * lat_count, lon_count)  5.83 us
    ppermute x1, waiting for transfers between devices, local(): received.append(lax.ppermute(plain_here, 'rec', perm))  4.38 us
    convert_element_type x1, local copies, waits for them, and re-layouts, weighted_dense_chunks(): along_lon = jnp.dot(footprint.reshape(time_count * lat_count, lon_count),...  4.09 us
  transfers between devices with their start and end apart: 3, of which 3 were waited for; matrix products, arithmetic and copies ran while one was open for 26% of the time, Pallas kernels for 0%

profile of v7, /device:TPU:0, one launch (start us, length us, event | category | flops | bytes accessed | tf_op | source)
XLA Modules:
  0.0 125.1 jit_solution(1870173833794302011)
XLA Ops:
  0.0 3.2 %shard_map.46 = bf16[16,496,128]{2,1,0:T(8,128)(2,1)} custom-call(bf16[120,8400]{1,0:T(8,128)(2,1)} %bitcast.44), custom_call_target="tpu_custom_call" | custom-call | bytes 4063232 | tf_op jit(solution)/shard_map/pallas_call | solution.py:78
  3.2 8.4 %all-to-all-start.1 = ((bf16[16,496,128]{2,1,0:T(8,128)(2,1)}), bf16[16,496,128]{2,1,0:T(8,128)(2,1)}, u32[]{:S(2)}, u32[]{:S(2)}) async-start(bf16[16,496,128]{2,1,0:T(8,128)(2,1)} %shard_map.46), calls=%async_computation.1 | async-start | bytes 4063232 | tf_op jit(solution)/shard_map/all_to_all | solution.py:120
  11.6 5.8 %reshape.32 = bf16[8400,120]{1,0:T(8,128)(2,1)S(1)} reshape(bf16[120,8400]{1,0:T(8,128)(2,1)} %bitcast.45) | data formatting | bytes 4032000 | tf_op jit(solution)/shard_map/reshape | solution.py:94
  17.4 2.1 %convolution_convert_fusion = bf16[8400,120]{0,1:T(8,128)(2,1)} fusion(bf16[8400,120]{1,0:T(8,128)(2,1)S(1)} %reshape.32, bf16[120,120]{1,0:T(8,128)(2,1)S(1)} %copy-done), kind=kOutput, calls=%fused_computation | convolution fusion | flops 242928000 | bytes 4060800 | tf_op jit(solution)/shard_map/dot_general | solution.py:93
  19.6 4.1 %copy.20 = bf16[8400,120]{1,0:T(8,128)(2,1)} copy(bf16[8400,120]{0,1:T(8,128)(2,1)} %convolution_convert_fusion) | data formatting | bytes 4032000 | tf_op jit(solution)/shard_map/convert_element_type | solution.py:97
  23.7 2.8 %reshape.33 = bf16[120,70,120]{2,1,0:T(8,128)(2,1)S(1)} reshape(bf16[8400,120]{1,0:T(8,128)(2,1)} %copy.20) | data formatting | bytes 4032000 | tf_op jit(solution)/shard_map/reshape | solution.py:100
  26.5 2.1 %convert_bitcast_fusion = bf16[120,70,120]{2,1,0:T(8,128)(2,1)} fusion(bf16[120,70,120]{2,1,0:T(8,128)(2,1)S(1)} %reshape.33, bf16[70,70]{1,0:T(8,128)(2,1)S(1)} %copy-done.2), kind=kOutput, calls=%fused_computation.5 | convolution fusion | flops 142128000 | bytes 4041800 | tf_op jit(solution)/shard_map/tab,ac->tcb/dot_general | solution.py:98
  28.6 3.6 %copy.22 = bf16[120,70,120]{0,2,1:T(8,128)(2,1)S(1)} copy(bf16[120,70,120]{2,1,0:T(8,128)(2,1)} %convert_bitcast_fusion) | data formatting | bytes 4032000 | tf_op jit(solution)/shard_map/convert_element_type | solution.py:103
  32.2 1.5 %slice.17 = bf16[120,8192]{0,1:T(8,128)(2,1)} slice(bf16[120,8400]{0,1:T(8,128)(2,1)S(1)} %bitcast.40), slice={[0:120], [0:8192]} | slice | bytes 3932160 | tf_op jit(solution)/shard_map/slice | solution.py:105
  33.7 0.2 fusion.4
  33.9 0.1 copy.26
  34.0 0.7 fusion.3
  34.9 0.1 pad.9.clone
  34.9 2.4 %convolution_convert_fusion.2 = bf16[64,128,112]{1,2,0:T(8,128)(2,1)S(1)} fusion(bf16[120,64,128]{0,2,1:T(8,128)(2,1)} %bitcast.43, bf16[120,120]{1,0:T(8,128)(2,1)S(1)} %copy-done.1), kind=kOutput, calls=%fused_computation.10 | convolution fusion | flops 221118464 | bytes 3829888 | tf_op jit(solution)/shard_map/ts,tjl->jsl/dot_general | solution.py:106
  37.3 1.8 %maximum_maximum_fusion = bf16[16,496,128]{2,1,0:T(8,128)(2,1)} fusion(bf16[16,47,128]{2,1,0:T(8,128)(2,1)S(1)} %reshape.41, bf16[16,448,128]{2,1,0:T(8,128)(2,1)S(1)} %bitcast.46, bf16[496]{0:T(512)(128)(2,1)S(1)} %pad.9.clone), kind=kLoop, calls=%fused_computation.6 | loop fusion | flops 6094848 | bytes 4060128 | tf_op jit(solution)/shard_map/concatenate | solution.py:45
  39.1 14.5 %all-to-all-done.1 = bf16[16,496,128]{2,1,0:T(8,128)(2,1)} async-done(((bf16[16,496,128]{2,1,0:T(8,128)(2,1)}), bf16[16,496,128]{2,1,0:T(8,128)(2,1)}, u32[]{:S(2)}, u32[]{:S(2)}) %all-to-all-start.1) | async-done | bytes 2031648 | tf_op jit(solution)/shard_map/all_to_all | solution.py:120
  53.6 9.7 %all-to-all-start = ((bf16[16,496,128]{2,1,0:T(8,128)(2,1)}), bf16[16,496,128]{2,1,0:T(8,128)(2,1)S(1)}, u32[]{:S(2)}, u32[]{:S(2)}) async-start(bf16[16,496,128]{2,1,0:T(8,128)(2,1)} %maximum_maximum_fusion), calls=%async_computation | async-start | bytes 4063232 | tf_op jit(solution)/shard_map/all_to_all | solution.py:122
  63.4 4.4 %collective-permute-done = bf16[16,496,128]{2,1,0:T(8,128)(2,1)} collective-permute-done((bf16[16,496,128]{2,1,0:T(8,128)(2,1)}, bf16[16,496,128]{2,1,0:T(8,128)(2,1)}, u32[]{:S(2)}, u32[]{:S(2)}) %collective-permute-start) | collective-permute-done | bytes 2031648 | tf_op jit(solution)/shard_map/ppermute | solution.py:128
  67.8 2.4 %broadcast_select_fusion.1 = (bf16[16,496,128]{2,1,0:T(8,128)(2,1)S(1)}, bf16[16,496,128]{2,1,0:T(8,128)(2,1)S(1)}) fusion(bf16[16,496,128]{2,1,0:T(8,128)(2,1)} %collective-permute-done, bf16[16,496,128]{2,1,0:T(8,128)(2,1)} %all-to-all-done.1, pred[]{:T(512)S(6)} %eq.9, pred[]{:T(512)S(6)} %eq.10), kind=kLoop, calls=%fused_computation.9 | loop fusion | flops 2031616 | bytes 8126466 | tf_op jit(solution)/shard_map/jit(_where)/select_n | solution.py:133
  70.2 2.2 %pad_maximum_fusion = bf16[32,496,128]{2,1,0:T(8,128)(2,1)} fusion(bf16[16,496,128]{2,1,0:T(8,128)(2,1)S(1)} %get-tuple-element.10, bf16[16,496,128]{2,1,0:T(8,128)(2,1)S(1)} %get-tuple-element.9), kind=kLoop, calls=%fused_computation.2 | loop fusion | flops 2031616 | bytes 8126464 | tf_op jit(solution)/shard_map/concatenate | solution.py:135
  72.5 32.2 %all-to-all-done = bf16[16,496,128]{2,1,0:T(8,128)(2,1)S(1)} async-done(((bf16[16,496,128]{2,1,0:T(8,128)(2,1)}), bf16[16,496,128]{2,1,0:T(8,128)(2,1)S(1)}, u32[]{:S(2)}, u32[]{:S(2)}) %all-to-all-start) | async-done | bytes 2031648 | tf_op jit(solution)/shard_map/all_to_all | solution.py:122
  104.7 3.3 %fusion = f32[16,32,1]{1,0,2:T(8,128)S(1)} fusion(bf16[32,496,128]{2,1,0:T(8,128)(2,1)} %pad_maximum_fusion, bf16[16,496,128]{2,1,0:T(8,128)(2,1)S(1)} %all-to-all-done), kind=kOutput, calls=%fused_computation.3 | convolution fusion | flops 65011712 | bytes 6096896 | tf_op jit(solution)/shard_map/dot_general | solution.py:136
  108.0 16.5 %all_to_all.19 = f32[16,1,32]{2,1,0:T(1,128)S(1)} all-to-all(f32[16,1,32]{2,1,0:T(1,128)S(1)} %bitcast.49), channel_id=1, replica_groups=mesh['rec'=2,'space'=16] {'space'}, dimensions={0} | all-to-all | bytes 4096 | tf_op jit(solution)/shard_map/all_to_all | solution.py:137
  124.5 0.5 reduce_sum.9
  (10 shorter events, 0.2 us)
Async XLA Ops:
  0.0 17.4 %copy-start = (bf16[120,120]{1,0:T(8,128)(2,1)S(1)}, bf16[120,120]{1,0:T(8,128)(2,1)}, u32[]{:S(2)}) copy-start(bf16[120,120]{1,0:T(8,128)(2,1)} %param.7) | copy-start | bytes 86404
  3.2 50.4 %all-to-all-start.1 = ((bf16[16,496,128]{2,1,0:T(8,128)(2,1)}), bf16[16,496,128]{2,1,0:T(8,128)(2,1)}, u32[]{:S(2)}, u32[]{:S(2)}) async-start(bf16[16,496,128]{2,1,0:T(8,128)(2,1)} %shard_map.46), calls=%async_computation.1 | async-start | bytes 4063232 | tf_op jit(solution)/shard_map/all_to_all | solution.py:120
  23.7 2.8 %copy-start.2 = (bf16[70,70]{1,0:T(8,128)(2,1)S(1)}, bf16[70,70]{1,0:T(8,128)(2,1)}, u32[]{:S(2)}) copy-start(bf16[70,70]{1,0:T(8,128)(2,1)} %param.6) | copy-start | bytes 29404
  32.2 1.5 %copy-start.1 = (bf16[120,120]{1,0:T(8,128)(2,1)S(1)}, bf16[120,120]{1,0:T(8,128)(2,1)}, u32[]{:S(2)}) copy-start(bf16[120,120]{1,0:T(8,128)(2,1)} %param.5) | copy-start | bytes 86404
  53.6 51.1 %all-to-all-start = ((bf16[16,496,128]{2,1,0:T(8,128)(2,1)}), bf16[16,496,128]{2,1,0:T(8,128)(2,1)S(1)}, u32[]{:S(2)}, u32[]{:S(2)}) async-start(bf16[16,496,128]{2,1,0:T(8,128)(2,1)} %maximum_maximum_fusion), calls=%async_computation | async-start | bytes 4063232 | tf_op jit(solution)/shard_map/all_to_all | solution.py:122
  63.3 4.5 %collective-permute-start = (bf16[16,496,128]{2,1,0:T(8,128)(2,1)}, bf16[16,496,128]{2,1,0:T(8,128)(2,1)}, u32[]{:S(2)}, u32[]{:S(2)}) collective-permute-start(bf16[16,496,128]{2,1,0:T(8,128)(2,1)} %all-to-all-done.1), channel_id=1, source_target_pairs={{0,16},{16,0},{1,17},{17,1},{2,18},{18,2},{3,19},{19,3},{4,20},{20... | collective-permute-start | bytes 6094856 | tf_op jit(solution)/shard_map/ppermute | solution.py:128

commit v8 on v7

--- a/solution.py
+++ b/solution.py
@@ -117,7 +117,13 @@
     rec_index = lax.axis_index("rec")
     plain = dense_chunks(footprints[0], space_count)
     plain, footprint = lax.optimization_barrier((plain, footprints[0]))
-    plain_here = lax.all_to_all(plain, "space", split_axis=0, concat_axis=0, tiled=True)
+    space_index = lax.axis_index("space")
+    shifted = [lax.dynamic_index_in_dim(plain, space_index, 0, keepdims=True)]
+    for shift in range(1, space_count):
+        perm = [(i, (i + shift) % space_count) for i in range(space_count)]
+        piece = lax.dynamic_index_in_dim(plain, (space_index + shift) % space_count, 0, keepdims=True)
+        shifted.append(lax.ppermute(piece, "space", perm))
+    plain_here = jnp.concatenate(shifted, axis=0)
     weighted = weighted_dense_chunks(footprint, time_cov, lat_cov, lon_cov, space_count)
     weighted_here = lax.all_to_all(weighted, "space", split_axis=0, concat_axis=0, tiled=True)
     contract = (((1, 2), (1, 2)), ((), ()))
@@ -134,6 +140,8 @@
         ordered.append(choice)
     everyone = jnp.concatenate(ordered, axis=0)
     partial_value = lax.dot_general(weighted_here, everyone, contract, preferred_element_type=jnp.float32)
+    source = (space_index - jnp.arange(group)) % group
+    partial_value = jnp.take(partial_value.reshape(group, rec_count, group), source, axis=2).reshape(group, rec_count * group)
     spread = lax.all_to_all(partial_value, "space", split_axis=0, concat_axis=0, tiled=True)
     return jnp.sum(spread, axis=0, keepdims=True)
 

time: 126 us -> 160 us (1.27)
  starting transfers between devices: 18.1 us -> 41.9 us
  local copies, waits for them, and re-layouts: 18.1 us -> 26.6 us
  waiting for transfers between devices: 51.1 us -> 55 us
  blocking collectives: 16.5 us -> 13.9 us
    ppermute x0 -> x15, waiting for transfers between devices: none -> 51 us  [local(): shifted.append(lax.ppermute(piece, 'space', perm))]
    ppermute x0 -> x15, starting transfers between devices: none -> 36.1 us  [local(): shifted.append(lax.ppermute(piece, 'space', perm))]
    all_to_all x1, waiting for transfers between devices: 32.2 us -> 0.01 us  [local(): lax.all_to_all(weighted, 'space', split_axis=0, concat_axis=0, tiled=True)]
    all_to_all x1 -> x0, waiting for transfers between devices: 14.5 us -> none  [local(): lax.all_to_all(plain, 'space', split_axis=0, concat_axis=0, tiled=True)]
    all_to_all x1 -> x0, starting transfers between devices: 8.36 us -> none  [local(): lax.all_to_all(plain, 'space', split_axis=0, concat_axis=0, tiled=True)]
    unnamed x6 -> x24, local copies, waits for them, and re-layouts: 0.01 us -> 4.77 us
    all_to_all x1, starting transfers between devices: 9.71 us -> 5.73 us  [local(): lax.all_to_all(weighted, 'space', split_axis=0, concat_axis=0, tiled=True)]
    dynamic_slice x0 -> x1, local copies, waits for them, and re-layouts: none -> 2.73 us  [local(): lax.dynamic_index_in_dim(plain, (space_index + shift) % space_count, 0, k...]
  transfers between devices with their start and end apart: 3 -> 17, of which waited for: 3 -> 5; matrix products, arithmetic and copies ran while one was open for 26% -> 23% of each run, Pallas kernels for 0% -> 0%
where the time goes in v8:
time: 160 us; the launch traced here: 159 us
  waiting for transfers between devices  55 us (34%)
  starting transfers between devices  41.9 us (26%)
  local copies, waits for them, and re-layouts  26.6 us (17%)
  blocking collectives  13.9 us (9%)
  matrix products  11.5 us (7%)
  other arithmetic  6.5 us (4%)
  Pallas kernels  3.27 us (2%)
    ppermute x15, waiting for transfers between devices, local(): shifted.append(lax.ppermute(piece, 'space', perm))  51 us
    ppermute x15, starting transfers between devices, local(): shifted.append(lax.ppermute(piece, 'space', perm))  36.1 us
    all_to_all x1, blocking collectives, local(): lax.all_to_all(partial_value, 'space', split_axis=0, concat_axis=0, tiled...  13.9 us
    reshape x1, local copies, waits for them, and re-layouts, weighted_dense_chunks(): footprint.reshape(time_count * lat_count, lon_count)  5.82 us
    all_to_all x1, starting transfers between devices, local(): lax.all_to_all(weighted, 'space', split_axis=0, concat_axis=0, tiled=True)  5.73 us
    unnamed x24, local copies, waits for them, and re-layouts  4.77 us
    convert_element_type x1, local copies, waits for them, and re-layouts, weighted_dense_chunks(): along_lon = jnp.dot(footprint.reshape(time_count * lat_count, lon_count),...  4.07 us
    ppermute x1, waiting for transfers between devices, local(): received.append(lax.ppermute(plain_here, 'rec', perm))  4.03 us
  transfers between devices with their start and end apart: 17, of which 5 were waited for; matrix products, arithmetic and copies ran while one was open for 23% of the time, Pallas kernels for 0%

profile of v8, /device:TPU:0, one launch (start us, length us, event | category | flops | bytes accessed | tf_op | source)
XLA Modules:
  0.0 158.9 jit_solution(15025906664498766892)
XLA Ops:
  0.0 3.3 %shard_map.46 = bf16[16,496,128]{2,1,0:T(8,128)(2,1)} custom-call(bf16[120,8400]{1,0:T(8,128)(2,1)} %bitcast.46), custom_call_target="tpu_custom_call" | custom-call | bytes 4063232 | tf_op jit(solution)/shard_map/pallas_call | solution.py:78
  3.3 2.7 %constant_dynamic-slice_fusion = (bf16[1,496,128]{2,1,0:T(8,128)(2,1)S(1)}, bf16[1,496,128]{2,1,0:T(8,128)(2,1)S(1)}, bf16[1,496,128]{2,1,0:T(8,128)(2,1)S(1)}, ...) fusion(bf16[16,496,128]{2,1,0:T(8,128)(2,1)} %shard_map.46, ...), kind=kLoop, calls=%fused_computation.40 | loop fusion | bytes 4063296 | tf_op jit(solution)/shard_map/jit(dynamic_index_in_dim)/dynamic_slice | solution.py:124
  6.0 3.0 %collective-permute-start = (bf16[1,496,128]{2,1,0:T(8,128)(2,1)}, bf16[1,496,128]{2,1,0:T(8,128)(2,1)}, u32[]{:S(2)}, u32[]{:S(2)}) collective-permute-start(bf16[1,496,128]{2,1,0:T(8,128)(2,1)} %get-tuple-element.25), channel_id=1, source_target_pairs={{0,1},{1,2},{2,3},{3,4},{4,5},{5,6},{6,7},{7,8},{8,9},{9,10},{10,1... | collective-permute-start | bytes 380936 | tf_op jit(solution)/shard_map/ppermute | solution.py:125
  10.5 2.4 %collective-permute-start.2 = (bf16[1,496,128]{2,1,0:T(8,128)(2,1)}, bf16[1,496,128]{2,1,0:T(8,128)(2,1)}, u32[]{:S(2)}, u32[]{:S(2)}) collective-permute-start(bf16[1,496,128]{2,1,0:T(8,128)(2,1)} %get-tuple-element.23), channel_id=1, source_target_pairs={{0,3},{1,4},{2,5},{3,6},{4,7},{5,8},{6,9},{7,10},{8,11},{9,12},{10... | collective-permute-start | bytes 380936 | tf_op jit(solution)/shard_map/ppermute | solution.py:125
  16.1 5.8 %reshape.130 = bf16[8400,120]{1,0:T(8,128)(2,1)S(1)} reshape(bf16[120,8400]{1,0:T(8,128)(2,1)} %bitcast.47) | data formatting | bytes 4032000 | tf_op jit(solution)/shard_map/reshape | solution.py:94
  21.9 2.1 %convolution_convert_fusion = bf16[8400,120]{0,1:T(8,128)(2,1)} fusion(bf16[8400,120]{1,0:T(8,128)(2,1)S(1)} %reshape.130, bf16[120,120]{1,0:T(8,128)(2,1)S(1)} %copy-done), kind=kOutput, calls=%fused_computation.1 | convolution fusion | flops 242928000 | bytes 4060800 | tf_op jit(solution)/shard_map/dot_general | solution.py:93
  24.1 4.1 %copy.33 = bf16[8400,120]{1,0:T(8,128)(2,1)} copy(bf16[8400,120]{0,1:T(8,128)(2,1)} %convolution_convert_fusion) | data formatting | bytes 4032000 | tf_op jit(solution)/shard_map/convert_element_type | solution.py:97
  28.1 2.8 %reshape.131 = bf16[120,70,120]{2,1,0:T(8,128)(2,1)S(1)} reshape(bf16[8400,120]{1,0:T(8,128)(2,1)} %copy.33) | data formatting | bytes 4032000 | tf_op jit(solution)/shard_map/reshape | solution.py:100
  31.0 2.1 %convert_bitcast_fusion = bf16[120,70,120]{2,1,0:T(8,128)(2,1)} fusion(bf16[120,70,120]{2,1,0:T(8,128)(2,1)S(1)} %reshape.131, bf16[70,70]{1,0:T(8,128)(2,1)S(1)} %copy-done.4), kind=kOutput, calls=%fused_computation.6 | convolution fusion | flops 142128000 | bytes 4041800 | tf_op jit(solution)/shard_map/tab,ac->tcb/dot_general | solution.py:98
  33.1 3.6 %copy.35 = bf16[120,70,120]{0,2,1:T(8,128)(2,1)S(1)} copy(bf16[120,70,120]{2,1,0:T(8,128)(2,1)} %convert_bitcast_fusion) | data formatting | bytes 4032000 | tf_op jit(solution)/shard_map/convert_element_type | solution.py:103
  39.4 2.3 %convolution_convert_fusion.2 = bf16[64,128,112]{1,2,0:T(8,128)(2,1)S(1)} fusion(bf16[120,64,128]{0,2,1:T(8,128)(2,1)} %bitcast.45, bf16[120,120]{1,0:T(8,128)(2,1)S(1)} %copy-done.2), kind=kOutput, calls=%fused_computation.11 | convolution fusion | flops 221118464 | bytes 3829888 | tf_op jit(solution)/shard_map/ts,tjl->jsl/dot_general | solution.py:106
  43.6 5.7 %all-to-all-start = ((bf16[16,496,128]{2,1,0:T(8,128)(2,1)}), bf16[16,496,128]{2,1,0:T(8,128)(2,1)}, u32[]{:S(2)}, u32[]{:S(2)}) async-start(bf16[16,496,128]{2,1,0:T(8,128)(2,1)} %maximum_maximum_fusion), calls=%async_computation | async-start | bytes 4063232 | tf_op jit(solution)/shard_map/all_to_all | solution.py:128
  49.4 2.8 %collective-permute-start.5 = (bf16[1,496,128]{2,1,0:T(8,128)(2,1)S(1)}, bf16[1,496,128]{2,1,0:T(8,128)(2,1)S(1)}, u32[]{:S(2)}, u32[]{:S(2)}) collective-permute-start(bf16[1,496,128]{2,1,0:T(8,128)(2,1)S(1)} %copy-done.3), channel_id=1, source_target_pairs={{0,6},{1,7},{2,8},{3,9},{4,10},{5,11},{6,12},{7,13},{8,14},{9,15},... | collective-permute-start | bytes 380936 | tf_op jit(solution)/shard_map/ppermute | solution.py:125
  53.1 3.3 %collective-permute-start.6 = (bf16[1,496,128]{2,1,0:T(8,128)(2,1)S(1)}, bf16[1,496,128]{2,1,0:T(8,128)(2,1)S(1)}, u32[]{:S(2)}, u32[]{:S(2)}) collective-permute-start(bf16[1,496,128]{2,1,0:T(8,128)(2,1)S(1)} %get-tuple-element.19), channel_id=1, source_target_pairs={{0,7},{1,8},{2,9},{3,10},{4,11},{5,12},{6,13},{7,14},{8,15},{9,0},... | collective-permute-start | bytes 380936 | tf_op jit(solution)/shard_map/ppermute | solution.py:125
  58.9 2.4 %collective-permute-start.8 = (bf16[1,496,128]{2,1,0:T(8,128)(2,1)S(1)}, bf16[1,496,128]{2,1,0:T(8,128)(2,1)S(1)}, u32[]{:S(2)}, u32[]{:S(2)}) collective-permute-start(bf16[1,496,128]{2,1,0:T(8,128)(2,1)S(1)} %get-tuple-element.17), channel_id=1, source_target_pairs={{0,9},{1,10},{2,11},{3,12},{4,13},{5,14},{6,15},{7,0},{8,1},{9,2},... | collective-permute-start | bytes 380936 | tf_op jit(solution)/shard_map/ppermute | solution.py:125
  64.7 46.6 %collective-permute-done.5 = bf16[1,496,128]{2,1,0:T(8,128)(2,1)S(1)} collective-permute-done((bf16[1,496,128]{2,1,0:T(8,128)(2,1)S(1)}, bf16[1,496,128]{2,1,0:T(8,128)(2,1)S(1)}, u32[]{:S(2)}, u32[]{:S(2)}) %collective-permute-start.5) | collective-permute-done | bytes 127008 | tf_op jit(solution)/shard_map/ppermute | solution.py:125
  111.3 2.2 %collective-permute-start.10 = (bf16[1,496,128]{2,1,0:T(8,128)(2,1)S(1)}, bf16[1,496,128]{2,1,0:T(8,128)(2,1)S(1)}, u32[]{:S(2)}, u32[]{:S(2)}) collective-permute-start(bf16[1,496,128]{2,1,0:T(8,128)(2,1)S(1)} %get-tuple-element.15), channel_id=1, source_target_pairs={{0,11},{1,12},{2,13},{3,14},{4,15},{5,0},{6,1},{7,2},{8,3},{9,4},{... | collective-permute-start | bytes 380936 | tf_op jit(solution)/shard_map/ppermute | solution.py:125
  113.5 7.6 %collective-permute-start.11 = (bf16[1,496,128]{2,1,0:T(8,128)(2,1)S(1)}, bf16[1,496,128]{2,1,0:T(8,128)(2,1)S(1)}, u32[]{:S(2)}, u32[]{:S(2)}) collective-permute-start(bf16[1,496,128]{2,1,0:T(8,128)(2,1)S(1)} %get-tuple-element.14), channel_id=1, source_target_pairs={{0,12},{1,13},{2,14},{3,15},{4,0},{5,1},{6,2},{7,3},{8,4},{9,5},{1... | collective-permute-start | bytes 380936 | tf_op jit(solution)/shard_map/ppermute | solution.py:125
  123.0 3.2 %collective-permute-start.13 = (bf16[1,496,128]{2,1,0:T(8,128)(2,1)S(1)}, bf16[1,496,128]{2,1,0:T(8,128)(2,1)S(1)}, u32[]{:S(2)}, u32[]{:S(2)}) collective-permute-start(bf16[1,496,128]{2,1,0:T(8,128)(2,1)S(1)} %get-tuple-element.12), channel_id=1, source_target_pairs={{0,14},{1,15},{2,0},{3,1},{4,2},{5,3},{6,4},{7,5},{8,6},{9,7},{10,... | collective-permute-start | bytes 380936 | tf_op jit(solution)/shard_map/ppermute | solution.py:125
  129.1 2.1 %collective-permute-done.14 = bf16[1,496,128]{2,1,0:T(8,128)(2,1)S(1)} collective-permute-done((bf16[1,496,128]{2,1,0:T(8,128)(2,1)S(1)}, bf16[1,496,128]{2,1,0:T(8,128)(2,1)S(1)}, u32[]{:S(2)}, u32[]{:S(2)}) %collective-permute-start.14) | collective-permute-done | bytes 127008 | tf_op jit(solution)/shard_map/ppermute | solution.py:125
  131.5 4.0 %collective-permute-done.15 = bf16[16,496,128]{2,1,0:T(8,128)(2,1)} collective-permute-done((bf16[16,496,128]{2,1,0:T(8,128)(2,1)S(1)}, bf16[16,496,128]{2,1,0:T(8,128)(2,1)}, u32[]{:S(2)}, u32[]{:S(2)}) %collective-permute-start.15) | collective-permute-done | bytes 2031648 | tf_op jit(solution)/shard_map/ppermute | solution.py:134
  137.3 2.3 %pad_maximum_fusion = bf16[32,496,128]{2,1,0:T(8,128)(2,1)} fusion(bf16[16,496,128]{2,1,0:T(8,128)(2,1)S(1)} %get-tuple-element.10, bf16[16,496,128]{2,1,0:T(8,128)(2,1)S(1)} %get-tuple-element.9), kind=kLoop, calls=%fused_computation.3 | loop fusion | flops 2031616 | bytes 8126464 | tf_op jit(solution)/shard_map/concatenate | solution.py:141
  139.6 3.9 %fusion.5 = f32[16,32]{1,0:T(8,128)S(1)} fusion(bf16[32,496,128]{2,1,0:T(8,128)(2,1)} %pad_maximum_fusion, bf16[16,496,128]{2,1,0:T(8,128)(2,1)} %all-to-all-done), kind=kOutput, calls=%fused_computation.15 | convolution fusion | flops 65011712 | bytes 6096896 | tf_op jit(solution)/shard_map/dot_general | solution.py:142
  144.5 13.9 %all_to_all.11 = f32[16,1,32]{2,1,0:T(1,128)S(1)} all-to-all(f32[16,1,32]{2,1,0:T(1,128)S(1)} %bitcast.52), channel_id=1, replica_groups=mesh['rec'=2,'space'=16] {'space'}, dimensions={0} | all-to-all | bytes 4096 | tf_op jit(solution)/shard_map/all_to_all | solution.py:145
  (69 shorter events, 24.2 us)
Async XLA Ops:
  0.0 21.9 %copy-start = (bf16[120,120]{1,0:T(8,128)(2,1)S(1)}, bf16[120,120]{1,0:T(8,128)(2,1)}, u32[]{:S(2)}) copy-start(bf16[120,120]{1,0:T(8,128)(2,1)} %param.7) | copy-start | bytes 86404
  6.0 43.3 %collective-permute-start = (bf16[1,496,128]{2,1,0:T(8,128)(2,1)}, bf16[1,496,128]{2,1,0:T(8,128)(2,1)}, u32[]{:S(2)}, u32[]{:S(2)}) collective-permute-start(bf16[1,496,128]{2,1,0:T(8,128)(2,1)} %get-tuple-element.25), channel_id=1, source_target_pairs={{0,1},{1,2},{2,3},{3,4},{4,5},{5,6},{6,7},{7,8},{8,9},{9,10},{10,1... | collective-permute-start | bytes 380936 | tf_op jit(solution)/shard_map/ppermute | solution.py:125
  9.0 44.2 %collective-permute-start.1 = (bf16[1,496,128]{2,1,0:T(8,128)(2,1)}, bf16[1,496,128]{2,1,0:T(8,128)(2,1)}, u32[]{:S(2)}, u32[]{:S(2)}) collective-permute-start(bf16[1,496,128]{2,1,0:T(8,128)(2,1)} %get-tuple-element.24), channel_id=1, source_target_pairs={{0,2},{1,3},{2,4},{3,5},{4,6},{5,7},{6,8},{7,9},{8,10},{9,11},{10,... | collective-permute-start | bytes 380936 | tf_op jit(solution)/shard_map/ppermute | solution.py:125
  10.5 46.9 %collective-permute-start.2 = (bf16[1,496,128]{2,1,0:T(8,128)(2,1)}, bf16[1,496,128]{2,1,0:T(8,128)(2,1)}, u32[]{:S(2)}, u32[]{:S(2)}) collective-permute-start(bf16[1,496,128]{2,1,0:T(8,128)(2,1)} %get-tuple-element.23), channel_id=1, source_target_pairs={{0,3},{1,4},{2,5},{3,6},{4,7},{5,8},{6,9},{7,10},{8,11},{9,12},{10... | collective-permute-start | bytes 380936 | tf_op jit(solution)/shard_map/ppermute | solution.py:125
  12.9 46.0 %collective-permute-start.3 = (bf16[1,496,128]{2,1,0:T(8,128)(2,1)}, bf16[1,496,128]{2,1,0:T(8,128)(2,1)}, u32[]{:S(2)}, u32[]{:S(2)}) collective-permute-start(bf16[1,496,128]{2,1,0:T(8,128)(2,1)} %get-tuple-element.22), channel_id=1, source_target_pairs={{0,4},{1,5},{2,6},{3,7},{4,8},{5,9},{6,10},{7,11},{8,12},{9,13},{1... | collective-permute-start | bytes 380936 | tf_op jit(solution)/shard_map/ppermute | solution.py:125
  14.5 47.8 %collective-permute-start.4 = (bf16[1,496,128]{2,1,0:T(8,128)(2,1)}, bf16[1,496,128]{2,1,0:T(8,128)(2,1)}, u32[]{:S(2)}, u32[]{:S(2)}) collective-permute-start(bf16[1,496,128]{2,1,0:T(8,128)(2,1)} %get-tuple-element.21), channel_id=1, source_target_pairs={{0,5},{1,6},{2,7},{3,8},{4,9},{5,10},{6,11},{7,12},{8,13},{9,14},{... | collective-permute-start | bytes 380936 | tf_op jit(solution)/shard_map/ppermute | solution.py:125
  28.1 2.8 %copy-start.4 = (bf16[70,70]{1,0:T(8,128)(2,1)S(1)}, bf16[70,70]{1,0:T(8,128)(2,1)}, u32[]{:S(2)}) copy-start(bf16[70,70]{1,0:T(8,128)(2,1)} %param.6) | copy-start | bytes 29404
  33.1 3.6 %copy-start.2 = (bf16[120,120]{1,0:T(8,128)(2,1)S(1)}, bf16[120,120]{1,0:T(8,128)(2,1)}, u32[]{:S(2)}) copy-start(bf16[120,120]{1,0:T(8,128)(2,1)} %param.5) | copy-start | bytes 86404
  43.6 5.8 %copy-start.3 = (bf16[1,496,128]{2,1,0:T(8,128)(2,1)S(1)}, bf16[1,496,128]{2,1,0:T(8,128)(2,1)}, u32[]{:S(2)}) copy-start(bf16[1,496,128]{2,1,0:T(8,128)(2,1)} %get-tuple-element.20) | copy-start | bytes 380932
  43.6 8.6 %copy-start.1 = (bf16[16,496,128]{2,1,0:T(8,128)(2,1)S(1)}, bf16[16,496,128]{2,1,0:T(8,128)(2,1)}, u32[]{:S(2)}) copy-start(bf16[16,496,128]{2,1,0:T(8,128)(2,1)} %get-tuple-element.26) | copy-start | bytes 6094852
  43.6 96.0 %all-to-all-start = ((bf16[16,496,128]{2,1,0:T(8,128)(2,1)}), bf16[16,496,128]{2,1,0:T(8,128)(2,1)}, u32[]{:S(2)}, u32[]{:S(2)}) async-start(bf16[16,496,128]{2,1,0:T(8,128)(2,1)} %maximum_maximum_fusion), calls=%async_computation | async-start | bytes 4063232 | tf_op jit(solution)/shard_map/all_to_all | solution.py:128
  49.4 62.0 %collective-permute-start.5 = (bf16[1,496,128]{2,1,0:T(8,128)(2,1)S(1)}, bf16[1,496,128]{2,1,0:T(8,128)(2,1)S(1)}, u32[]{:S(2)}, u32[]{:S(2)}) collective-permute-start(bf16[1,496,128]{2,1,0:T(8,128)(2,1)S(1)} %copy-done.3), channel_id=1, source_target_pairs={{0,6},{1,7},{2,8},{3,9},{4,10},{5,11},{6,12},{7,13},{8,14},{9,15},... | collective-permute-start | bytes 380936 | tf_op jit(solution)/shard_map/ppermute | solution.py:125
  53.1 60.4 %collective-permute-start.6 = (bf16[1,496,128]{2,1,0:T(8,128)(2,1)S(1)}, bf16[1,496,128]{2,1,0:T(8,128)(2,1)S(1)}, u32[]{:S(2)}, u32[]{:S(2)}) collective-permute-start(bf16[1,496,128]{2,1,0:T(8,128)(2,1)S(1)} %get-tuple-element.19), channel_id=1, source_target_pairs={{0,7},{1,8},{2,9},{3,10},{4,11},{5,12},{6,13},{7,14},{8,15},{9,0},... | collective-permute-start | bytes 380936 | tf_op jit(solution)/shard_map/ppermute | solution.py:125
  57.4 63.8 %collective-permute-start.7 = (bf16[1,496,128]{2,1,0:T(8,128)(2,1)S(1)}, bf16[1,496,128]{2,1,0:T(8,128)(2,1)S(1)}, u32[]{:S(2)}, u32[]{:S(2)}) collective-permute-start(bf16[1,496,128]{2,1,0:T(8,128)(2,1)S(1)} %get-tuple-element.18), channel_id=1, source_target_pairs={{0,8},{1,9},{2,10},{3,11},{4,12},{5,13},{6,14},{7,15},{8,0},{9,1},... | collective-permute-start | bytes 380936 | tf_op jit(solution)/shard_map/ppermute | solution.py:125
  58.9 64.1 %collective-permute-start.8 = (bf16[1,496,128]{2,1,0:T(8,128)(2,1)S(1)}, bf16[1,496,128]{2,1,0:T(8,128)(2,1)S(1)}, u32[]{:S(2)}, u32[]{:S(2)}) collective-permute-start(bf16[1,496,128]{2,1,0:T(8,128)(2,1)S(1)} %get-tuple-element.17), channel_id=1, source_target_pairs={{0,9},{1,10},{2,11},{3,12},{4,13},{5,14},{6,15},{7,0},{8,1},{9,2},... | collective-permute-start | bytes 380936 | tf_op jit(solution)/shard_map/ppermute | solution.py:125
  62.3 63.9 %collective-permute-start.9 = (bf16[1,496,128]{2,1,0:T(8,128)(2,1)S(1)}, bf16[1,496,128]{2,1,0:T(8,128)(2,1)S(1)}, u32[]{:S(2)}, u32[]{:S(2)}) collective-permute-start(bf16[1,496,128]{2,1,0:T(8,128)(2,1)S(1)} %get-tuple-element.16), channel_id=1, source_target_pairs={{0,10},{1,11},{2,12},{3,13},{4,14},{5,15},{6,0},{7,1},{8,2},{9,3},... | collective-permute-start | bytes 380936 | tf_op jit(solution)/shard_map/ppermute | solution.py:125
  111.3 15.4 %collective-permute-start.10 = (bf16[1,496,128]{2,1,0:T(8,128)(2,1)S(1)}, bf16[1,496,128]{2,1,0:T(8,128)(2,1)S(1)}, u32[]{:S(2)}, u32[]{:S(2)}) collective-permute-start(bf16[1,496,128]{2,1,0:T(8,128)(2,1)S(1)} %get-tuple-element.15), channel_id=1, source_target_pairs={{0,11},{1,12},{2,13},{3,14},{4,15},{5,0},{6,1},{7,2},{8,3},{9,4},{... | collective-permute-start | bytes 380936 | tf_op jit(solution)/shard_map/ppermute | solution.py:125
  113.5 13.3 %collective-permute-start.11 = (bf16[1,496,128]{2,1,0:T(8,128)(2,1)S(1)}, bf16[1,496,128]{2,1,0:T(8,128)(2,1)S(1)}, u32[]{:S(2)}, u32[]{:S(2)}) collective-permute-start(bf16[1,496,128]{2,1,0:T(8,128)(2,1)S(1)} %get-tuple-element.14), channel_id=1, source_target_pairs={{0,12},{1,13},{2,14},{3,15},{4,0},{5,1},{6,2},{7,3},{8,4},{9,5},{1... | collective-permute-start | bytes 380936 | tf_op jit(solution)/shard_map/ppermute | solution.py:125
  121.2 6.8 %collective-permute-start.12 = (bf16[1,496,128]{2,1,0:T(8,128)(2,1)S(1)}, bf16[1,496,128]{2,1,0:T(8,128)(2,1)S(1)}, u32[]{:S(2)}, u32[]{:S(2)}) collective-permute-start(bf16[1,496,128]{2,1,0:T(8,128)(2,1)S(1)} %get-tuple-element.13), channel_id=1, source_target_pairs={{0,13},{1,14},{2,15},{3,0},{4,1},{5,2},{6,3},{7,4},{8,5},{9,6},{10... | collective-permute-start | bytes 380936 | tf_op jit(solution)/shard_map/ppermute | solution.py:125
  123.0 6.1 %collective-permute-start.13 = (bf16[1,496,128]{2,1,0:T(8,128)(2,1)S(1)}, bf16[1,496,128]{2,1,0:T(8,128)(2,1)S(1)}, u32[]{:S(2)}, u32[]{:S(2)}) collective-permute-start(bf16[1,496,128]{2,1,0:T(8,128)(2,1)S(1)} %get-tuple-element.12), channel_id=1, source_target_pairs={{0,14},{1,15},{2,0},{3,1},{4,2},{5,3},{6,4},{7,5},{8,6},{9,7},{10,... | collective-permute-start | bytes 380936 | tf_op jit(solution)/shard_map/ppermute | solution.py:125
  126.2 5.0 %collective-permute-start.14 = (bf16[1,496,128]{2,1,0:T(8,128)(2,1)S(1)}, bf16[1,496,128]{2,1,0:T(8,128)(2,1)S(1)}, u32[]{:S(2)}, u32[]{:S(2)}) collective-permute-start(bf16[1,496,128]{2,1,0:T(8,128)(2,1)S(1)} %get-tuple-element.11), channel_id=1, source_target_pairs={{0,15},{1,0},{2,1},{3,2},{4,3},{5,4},{6,5},{7,6},{8,7},{9,8},{10,9... | collective-permute-start | bytes 380936 | tf_op jit(solution)/shard_map/ppermute | solution.py:125
  131.2 4.3 %collective-permute-start.15 = (bf16[16,496,128]{2,1,0:T(8,128)(2,1)S(1)}, bf16[16,496,128]{2,1,0:T(8,128)(2,1)}, u32[]{:S(2)}, u32[]{:S(2)}) collective-permute-start(bf16[16,496,128]{2,1,0:T(8,128)(2,1)S(1)} %constant_dynamic-update-slice_fusion), channel_id=1, source_target_pairs={{0,16},{16,0},{1,17},{17,1},{2,18},{18,2},{3,19},{19,3},{4,20},{20... | collective-permute-start | bytes 6094856 | tf_op jit(solution)/shard_map/ppermute | solution.py:134

commit v9 on v7

--- a/solution.py
+++ b/solution.py
@@ -45,15 +45,22 @@
     return jnp.concatenate(pieces, axis=1)
 
 
-def pack_kernel(full_rows, per, share, values_ref, out_ref, rest_ref):
+def pack_kernel(full_rows, per, share, values_ref, out_ref, rest_ref, sems):
     time_count, cell_count = values_ref.shape
     chunks, rows, _ = out_ref.shape
     main_tiles = chunks * per
     main_cols = main_tiles * LANE
+    copies = []
     for k in range(chunks):
         for q in range(per):
             j = k * per + q
-            out_ref[k, q * full_rows:(q + 1) * full_rows, :] = values_ref[0:full_rows, j * LANE:(j + 1) * LANE]
+            copy = pltpu.make_async_copy(
+                values_ref.at[0:full_rows, j * LANE:(j + 1) * LANE],
+                out_ref.at[k, q * full_rows:(q + 1) * full_rows, :],
+                sems.at[j],
+            )
+            copy.start()
+            copies.append(copy)
     rest_ref[...] = jnp.zeros(rest_ref.shape, rest_ref.dtype)
     low = time_count - full_rows
     at = 0
@@ -69,6 +76,8 @@
         out_ref[k, per * full_rows:per * full_rows + share, :] = rest_ref[k * share:(k + 1) * share, :].astype(out_ref.dtype)
         if rows > per * full_rows + share:
             out_ref[k, per * full_rows + share:, :] = jnp.zeros((rows - per * full_rows - share, LANE), out_ref.dtype)
+    for copy in copies:
+        copy.wait()
 
 
 def dense_chunks(values, chunks):
@@ -80,7 +89,7 @@
         out_shape=jax.ShapeDtypeStruct((chunks, rows, LANE), values.dtype),
         in_specs=[pl.BlockSpec(memory_space=pltpu.VMEM)],
         out_specs=pl.BlockSpec(memory_space=pltpu.VMEM),
-        scratch_shapes=[pltpu.VMEM((share * chunks, LANE), jnp.float32)],
+        scratch_shapes=[pltpu.VMEM((share * chunks, LANE), jnp.float32), pltpu.SemaphoreType.DMA((chunks * per,))],
         cost_estimate=pl.CostEstimate(flops=0, transcendentals=0, bytes_accessed=4 * chunks * rows * LANE),
     )(values)
 

time: 126 us -> 126 us (level)
  transfers between devices with their start and end apart: 3 -> 3, of which waited for: 3 -> 3; matrix products, arithmetic and copies ran while one was open for 26% -> 25% of each run, Pallas kernels for 0% -> 0%
where the time goes in v9:
time: 126 us
  waiting for transfers between devices  51.1 us (41%)
  local copies, waits for them, and re-layouts  18.1 us (14%)
  starting transfers between devices  18.1 us (14%)
  blocking collectives  16.5 us (13%)
  matrix products  10.8 us (9%)
  other arithmetic  7.05 us (6%)
  Pallas kernels  3.92 us (3%)
    all_to_all x1, waiting for transfers between devices, local(): lax.all_to_all(weighted, 'space', split_axis=0, concat_axis=0, tiled=True)  32.2 us
    all_to_all x1, blocking collectives, local(): lax.all_to_all(partial_value, 'space', split_axis=0, concat_axis=0, tiled...  16.5 us
    all_to_all x1, waiting for transfers between devices, local(): lax.all_to_all(plain, 'space', split_axis=0, concat_axis=0, tiled=True)  14.5 us
    all_to_all x1, starting transfers between devices, local(): lax.all_to_all(weighted, 'space', split_axis=0, concat_axis=0, tiled=True)  9.71 us
    all_to_all x1, starting transfers between devices, local(): lax.all_to_all(plain, 'space', split_axis=0, concat_axis=0, tiled=True)  8.37 us
    reshape x1, local copies, waits for them, and re-layouts, weighted_dense_chunks(): footprint.reshape(time_count * lat_count, lon_count)  5.83 us
    ppermute x1, waiting for transfers between devices, local(): received.append(lax.ppermute(plain_here, 'rec', perm))  4.38 us
    convert_element_type x1, local copies, waits for them, and re-layouts, weighted_dense_chunks(): along_lon = jnp.dot(footprint.reshape(time_count * lat_count, lon_count),...  4.09 us
  transfers between devices with their start and end apart: 3, of which 3 were waited for; matrix products, arithmetic and copies ran while one was open for 25% of the time, Pallas kernels for 0%

profile of v9, /device:TPU:0, one launch (start us, length us, event | category | flops | bytes accessed | tf_op | source)
XLA Modules:
  0.0 125.8 jit_solution(14385671624017345194)
XLA Ops:
  0.0 3.9 %shard_map.46 = bf16[16,496,128]{2,1,0:T(8,128)(2,1)} custom-call(bf16[120,8400]{1,0:T(8,128)(2,1)} %bitcast.44), custom_call_target="tpu_custom_call" | custom-call | bytes 4063232 | tf_op jit(solution)/shard_map/pallas_call | solution.py:87
  3.9 8.4 %all-to-all-start.1 = ((bf16[16,496,128]{2,1,0:T(8,128)(2,1)}), bf16[16,496,128]{2,1,0:T(8,128)(2,1)}, u32[]{:S(2)}, u32[]{:S(2)}) async-start(bf16[16,496,128]{2,1,0:T(8,128)(2,1)} %shard_map.46), calls=%async_computation.1 | async-start | bytes 4063232 | tf_op jit(solution)/shard_map/all_to_all | solution.py:129
  12.3 5.8 %reshape.32 = bf16[8400,120]{1,0:T(8,128)(2,1)S(1)} reshape(bf16[120,8400]{1,0:T(8,128)(2,1)} %bitcast.45) | data formatting | bytes 4032000 | tf_op jit(solution)/shard_map/reshape | solution.py:103
  18.2 2.1 %convolution_convert_fusion = bf16[8400,120]{0,1:T(8,128)(2,1)} fusion(bf16[8400,120]{1,0:T(8,128)(2,1)S(1)} %reshape.32, bf16[120,120]{1,0:T(8,128)(2,1)S(1)} %copy-done), kind=kOutput, calls=%fused_computation | convolution fusion | flops 242928000 | bytes 4060800 | tf_op jit(solution)/shard_map/dot_general | solution.py:102
  20.3 4.1 %copy.20 = bf16[8400,120]{1,0:T(8,128)(2,1)} copy(bf16[8400,120]{0,1:T(8,128)(2,1)} %convolution_convert_fusion) | data formatting | bytes 4032000 | tf_op jit(solution)/shard_map/convert_element_type | solution.py:106
  24.4 2.8 %reshape.33 = bf16[120,70,120]{2,1,0:T(8,128)(2,1)S(1)} reshape(bf16[8400,120]{1,0:T(8,128)(2,1)} %copy.20) | data formatting | bytes 4032000 | tf_op jit(solution)/shard_map/reshape | solution.py:109
  27.2 2.1 %convert_bitcast_fusion = bf16[120,70,120]{2,1,0:T(8,128)(2,1)} fusion(bf16[120,70,120]{2,1,0:T(8,128)(2,1)S(1)} %reshape.33, bf16[70,70]{1,0:T(8,128)(2,1)S(1)} %copy-done.2), kind=kOutput, calls=%fused_computation.5 | convolution fusion | flops 142128000 | bytes 4041800 | tf_op jit(solution)/shard_map/tab,ac->tcb/dot_general | solution.py:107
  29.3 3.6 %copy.22 = bf16[120,70,120]{0,2,1:T(8,128)(2,1)S(1)} copy(bf16[120,70,120]{2,1,0:T(8,128)(2,1)} %convert_bitcast_fusion) | data formatting | bytes 4032000 | tf_op jit(solution)/shard_map/convert_element_type | solution.py:112
  32.9 1.5 %slice.17 = bf16[120,8192]{0,1:T(8,128)(2,1)} slice(bf16[120,8400]{0,1:T(8,128)(2,1)S(1)} %bitcast.40), slice={[0:120], [0:8192]} | slice | bytes 3932160 | tf_op jit(solution)/shard_map/slice | solution.py:114
  34.4 0.2 fusion.4
  34.6 0.1 copy.26
  34.7 0.7 fusion.3
  35.6 0.1 pad.9.clone
  35.6 2.3 %convolution_convert_fusion.2 = bf16[64,128,112]{1,2,0:T(8,128)(2,1)S(1)} fusion(bf16[120,64,128]{0,2,1:T(8,128)(2,1)} %bitcast.43, bf16[120,120]{1,0:T(8,128)(2,1)S(1)} %copy-done.1), kind=kOutput, calls=%fused_computation.10 | convolution fusion | flops 221118464 | bytes 3829888 | tf_op jit(solution)/shard_map/ts,tjl->jsl/dot_general | solution.py:115
  38.0 1.8 %maximum_maximum_fusion = bf16[16,496,128]{2,1,0:T(8,128)(2,1)} fusion(bf16[16,47,128]{2,1,0:T(8,128)(2,1)S(1)} %reshape.41, bf16[16,448,128]{2,1,0:T(8,128)(2,1)S(1)} %bitcast.46, bf16[496]{0:T(512)(128)(2,1)S(1)} %pad.9.clone), kind=kLoop, calls=%fused_computation.6 | loop fusion | flops 6094848 | bytes 4060128 | tf_op jit(solution)/shard_map/concatenate | solution.py:45
  39.8 14.5 %all-to-all-done.1 = bf16[16,496,128]{2,1,0:T(8,128)(2,1)} async-done(((bf16[16,496,128]{2,1,0:T(8,128)(2,1)}), bf16[16,496,128]{2,1,0:T(8,128)(2,1)}, u32[]{:S(2)}, u32[]{:S(2)}) %all-to-all-start.1) | async-done | bytes 2031648 | tf_op jit(solution)/shard_map/all_to_all | solution.py:129
  54.3 9.7 %all-to-all-start = ((bf16[16,496,128]{2,1,0:T(8,128)(2,1)}), bf16[16,496,128]{2,1,0:T(8,128)(2,1)S(1)}, u32[]{:S(2)}, u32[]{:S(2)}) async-start(bf16[16,496,128]{2,1,0:T(8,128)(2,1)} %maximum_maximum_fusion), calls=%async_computation | async-start | bytes 4063232 | tf_op jit(solution)/shard_map/all_to_all | solution.py:131
  64.1 4.4 %collective-permute-done = bf16[16,496,128]{2,1,0:T(8,128)(2,1)} collective-permute-done((bf16[16,496,128]{2,1,0:T(8,128)(2,1)}, bf16[16,496,128]{2,1,0:T(8,128)(2,1)}, u32[]{:S(2)}, u32[]{:S(2)}) %collective-permute-start) | collective-permute-done | bytes 2031648 | tf_op jit(solution)/shard_map/ppermute | solution.py:137
  68.5 2.4 %broadcast_select_fusion.1 = (bf16[16,496,128]{2,1,0:T(8,128)(2,1)S(1)}, bf16[16,496,128]{2,1,0:T(8,128)(2,1)S(1)}) fusion(bf16[16,496,128]{2,1,0:T(8,128)(2,1)} %collective-permute-done, bf16[16,496,128]{2,1,0:T(8,128)(2,1)} %all-to-all-done.1, pred[]{:T(512)S(6)} %eq.9, pred[]{:T(512)S(6)} %eq.10), kind=kLoop, calls=%fused_computation.9 | loop fusion | flops 2031616 | bytes 8126466 | tf_op jit(solution)/shard_map/jit(_where)/select_n | solution.py:142
  71.0 2.2 %pad_maximum_fusion = bf16[32,496,128]{2,1,0:T(8,128)(2,1)} fusion(bf16[16,496,128]{2,1,0:T(8,128)(2,1)S(1)} %get-tuple-element.10, bf16[16,496,128]{2,1,0:T(8,128)(2,1)S(1)} %get-tuple-element.9), kind=kLoop, calls=%fused_computation.2 | loop fusion | flops 2031616 | bytes 8126464 | tf_op jit(solution)/shard_map/concatenate | solution.py:144
  73.2 32.2 %all-to-all-done = bf16[16,496,128]{2,1,0:T(8,128)(2,1)S(1)} async-done(((bf16[16,496,128]{2,1,0:T(8,128)(2,1)}), bf16[16,496,128]{2,1,0:T(8,128)(2,1)S(1)}, u32[]{:S(2)}, u32[]{:S(2)}) %all-to-all-start) | async-done | bytes 2031648 | tf_op jit(solution)/shard_map/all_to_all | solution.py:131
  105.4 3.3 %fusion = f32[16,32,1]{1,0,2:T(8,128)S(1)} fusion(bf16[32,496,128]{2,1,0:T(8,128)(2,1)} %pad_maximum_fusion, bf16[16,496,128]{2,1,0:T(8,128)(2,1)S(1)} %all-to-all-done), kind=kOutput, calls=%fused_computation.3 | convolution fusion | flops 65011712 | bytes 6096896 | tf_op jit(solution)/shard_map/dot_general | solution.py:145
  108.7 16.5 %all_to_all.19 = f32[16,1,32]{2,1,0:T(1,128)S(1)} all-to-all(f32[16,1,32]{2,1,0:T(1,128)S(1)} %bitcast.49), channel_id=1, replica_groups=mesh['rec'=2,'space'=16] {'space'}, dimensions={0} | all-to-all | bytes 4096 | tf_op jit(solution)/shard_map/all_to_all | solution.py:146
  125.3 0.5 reduce_sum.9
  (10 shorter events, 0.2 us)
Async XLA Ops:
  0.0 18.2 %copy-start = (bf16[120,120]{1,0:T(8,128)(2,1)S(1)}, bf16[120,120]{1,0:T(8,128)(2,1)}, u32[]{:S(2)}) copy-start(bf16[120,120]{1,0:T(8,128)(2,1)} %param.7) | copy-start | bytes 86404
  3.9 50.4 %all-to-all-start.1 = ((bf16[16,496,128]{2,1,0:T(8,128)(2,1)}), bf16[16,496,128]{2,1,0:T(8,128)(2,1)}, u32[]{:S(2)}, u32[]{:S(2)}) async-start(bf16[16,496,128]{2,1,0:T(8,128)(2,1)} %shard_map.46), calls=%async_computation.1 | async-start | bytes 4063232 | tf_op jit(solution)/shard_map/all_to_all | solution.py:129
  24.4 2.8 %copy-start.2 = (bf16[70,70]{1,0:T(8,128)(2,1)S(1)}, bf16[70,70]{1,0:T(8,128)(2,1)}, u32[]{:S(2)}) copy-start(bf16[70,70]{1,0:T(8,128)(2,1)} %param.6) | copy-start | bytes 29404
  32.9 1.5 %copy-start.1 = (bf16[120,120]{1,0:T(8,128)(2,1)S(1)}, bf16[120,120]{1,0:T(8,128)(2,1)}, u32[]{:S(2)}) copy-start(bf16[120,120]{1,0:T(8,128)(2,1)} %param.5) | copy-start | bytes 86404
  54.3 51.1 %all-to-all-start = ((bf16[16,496,128]{2,1,0:T(8,128)(2,1)}), bf16[16,496,128]{2,1,0:T(8,128)(2,1)S(1)}, u32[]{:S(2)}, u32[]{:S(2)}) async-start(bf16[16,496,128]{2,1,0:T(8,128)(2,1)} %maximum_maximum_fusion), calls=%async_computation | async-start | bytes 4063232 | tf_op jit(solution)/shard_map/all_to_all | solution.py:131
  64.0 4.5 %collective-permute-start = (bf16[16,496,128]{2,1,0:T(8,128)(2,1)}, bf16[16,496,128]{2,1,0:T(8,128)(2,1)}, u32[]{:S(2)}, u32[]{:S(2)}) collective-permute-start(bf16[16,496,128]{2,1,0:T(8,128)(2,1)} %all-to-all-done.1), channel_id=1, source_target_pairs={{0,16},{16,0},{1,17},{17,1},{2,18},{18,2},{3,19},{19,3},{4,20},{20... | collective-permute-start | bytes 6094856 | tf_op jit(solution)/shard_map/ppermute | solution.py:137

commit v10 on v7

--- a/solution.py
+++ b/solution.py
@@ -45,30 +45,64 @@
     return jnp.concatenate(pieces, axis=1)
 
 
-def pack_kernel(full_rows, per, share, values_ref, out_ref, rest_ref):
-    time_count, cell_count = values_ref.shape
-    chunks, rows, _ = out_ref.shape
+def pack_kernel(full_rows, per, share, values_hbm, out_hbm, values, main_out, rest_out, rest_ref, in_sems, out_sems):
+    time_count, cell_count = values.shape
+    chunks, rows, _ = out_hbm.shape
     main_tiles = chunks * per
     main_cols = main_tiles * LANE
-    for k in range(chunks):
-        for q in range(per):
-            j = k * per + q
-            out_ref[k, q * full_rows:(q + 1) * full_rows, :] = values_ref[0:full_rows, j * LANE:(j + 1) * LANE]
+    groups = 4 if chunks % 4 == 0 else 1
+    width = main_cols // groups
+    loads = []
+    for g in range(groups):
+        load = pltpu.make_async_copy(
+            values_hbm.at[:, g * width:(g + 1) * width], values.at[:, g * width:(g + 1) * width], in_sems.at[g]
+        )
+        load.start()
+        loads.append(load)
+    if cell_count > main_cols:
+        tail = pltpu.make_async_copy(
+            values_hbm.at[:, main_cols:cell_count], values.at[:, main_cols:cell_count], in_sems.at[groups]
+        )
+        tail.start()
+        loads.append(tail)
+    stores = []
+    per_group = chunks // groups
+    for g in range(groups):
+        loads[g].wait()
+        for k in range(g * per_group, (g + 1) * per_group):
+            for q in range(per):
+                j = k * per + q
+                main_out[k, q * full_rows:(q + 1) * full_rows, :] = values[0:full_rows, j * LANE:(j + 1) * LANE]
+        store = pltpu.make_async_copy(
+            main_out.at[g * per_group:(g + 1) * per_group],
+            out_hbm.at[g * per_group:(g + 1) * per_group, 0:per * full_rows, :],
+            out_sems.at[g],
+        )
+        store.start()
+        stores.append(store)
+    if cell_count > main_cols:
+        loads[groups].wait()
     rest_ref[...] = jnp.zeros(rest_ref.shape, rest_ref.dtype)
     low = time_count - full_rows
     at = 0
     if low:
         for j in range(main_tiles):
-            rest_ref[at:at + low, :] = values_ref[full_rows:time_count, j * LANE:(j + 1) * LANE].astype(jnp.float32)
+            rest_ref[at:at + low, :] = values[full_rows:time_count, j * LANE:(j + 1) * LANE].astype(jnp.float32)
             at += low
     for lo in range(main_cols, cell_count, LANE):
-        width = min(LANE, cell_count - lo)
-        rest_ref[at:at + time_count, 0:width] = values_ref[:, lo:lo + width].astype(jnp.float32)
+        span = min(LANE, cell_count - lo)
+        rest_ref[at:at + time_count, 0:span] = values[:, lo:lo + span].astype(jnp.float32)
         at += time_count
+    tail_rows = rows - per * full_rows
     for k in range(chunks):
-        out_ref[k, per * full_rows:per * full_rows + share, :] = rest_ref[k * share:(k + 1) * share, :].astype(out_ref.dtype)
-        if rows > per * full_rows + share:
-            out_ref[k, per * full_rows + share:, :] = jnp.zeros((rows - per * full_rows - share, LANE), out_ref.dtype)
+        rest_out[k, 0:share, :] = rest_ref[k * share:(k + 1) * share, :].astype(rest_out.dtype)
+        if tail_rows > share:
+            rest_out[k, share:, :] = jnp.zeros((tail_rows - share, LANE), rest_out.dtype)
+    last = pltpu.make_async_copy(rest_out, out_hbm.at[:, per * full_rows:rows, :], out_sems.at[groups])
+    last.start()
+    for store in stores:
+        store.wait()
+    last.wait()
 
 
 def dense_chunks(values, chunks):
@@ -78,9 +112,16 @@
     return pl.pallas_call(
         functools.partial(pack_kernel, full_rows, per, share),
         out_shape=jax.ShapeDtypeStruct((chunks, rows, LANE), values.dtype),
-        in_specs=[pl.BlockSpec(memory_space=pltpu.VMEM)],
-        out_specs=pl.BlockSpec(memory_space=pltpu.VMEM),
-        scratch_shapes=[pltpu.VMEM((share * chunks, LANE), jnp.float32)],
+        in_specs=[pl.BlockSpec(memory_space=pl.ANY)],
+        out_specs=pl.BlockSpec(memory_space=pl.ANY),
+        scratch_shapes=[
+            pltpu.VMEM((time_count, cell_count), values.dtype),
+            pltpu.VMEM((chunks, per * full_rows, LANE), values.dtype),
+            pltpu.VMEM((chunks, rows - per * full_rows, LANE), values.dtype),
+            pltpu.VMEM((share * chunks, LANE), jnp.float32),
+            pltpu.SemaphoreType.DMA((5,)),
+            pltpu.SemaphoreType.DMA((5,)),
+        ],
         cost_estimate=pl.CostEstimate(flops=0, transcendentals=0, bytes_accessed=4 * chunks * rows * LANE),
     )(values)
 

time: 126 us -> 125 us (level)
  no operation moved by 1% of the time
where the time goes in v10:
time: 125 us; the launch traced here: 124 us
  waiting for transfers between devices  51.1 us (41%)
  local copies, waits for them, and re-layouts  18.1 us (14%)
  starting transfers between devices  18.1 us (14%)
  blocking collectives  16.5 us (13%)
  matrix products  10.9 us (9%)
  other arithmetic  7.05 us (6%)
  Pallas kernels  2.52 us (2%)
    all_to_all x1, waiting for transfers between devices, local(): lax.all_to_all(weighted, 'space', split_axis=0, concat_axis=0, tiled=True)  32.2 us
    all_to_all x1, blocking collectives, local(): lax.all_to_all(partial_value, 'space', split_axis=0, concat_axis=0, tiled...  16.5 us
    all_to_all x1, waiting for transfers between devices, local(): lax.all_to_all(plain, 'space', split_axis=0, concat_axis=0, tiled=True)  14.5 us
    all_to_all x1, starting transfers between devices, local(): lax.all_to_all(weighted, 'space', split_axis=0, concat_axis=0, tiled=True)  9.71 us
    all_to_all x1, starting transfers between devices, local(): lax.all_to_all(plain, 'space', split_axis=0, concat_axis=0, tiled=True)  8.37 us
    reshape x1, local copies, waits for them, and re-layouts, weighted_dense_chunks(): footprint.reshape(time_count * lat_count, lon_count)  5.83 us
    ppermute x1, waiting for transfers between devices, local(): received.append(lax.ppermute(plain_here, 'rec', perm))  4.38 us
    convert_element_type x1, local copies, waits for them, and re-layouts, weighted_dense_chunks(): along_lon = jnp.dot(footprint.reshape(time_count * lat_count, lon_count),...  4.09 us
  transfers between devices with their start and end apart: 3, of which 3 were waited for; matrix products, arithmetic and copies ran while one was open for 26% of the time, Pallas kernels for 0%

profile of v10, /device:TPU:0, one launch (start us, length us, event | category | flops | bytes accessed | tf_op | source)
XLA Modules:
  0.0 124.4 jit_solution(15515102380921042443)
XLA Ops:
  0.0 2.5 %shard_map.46 = bf16[16,496,128]{2,1,0:T(8,128)(2,1)} custom-call(bf16[120,8400]{1,0:T(8,128)(2,1)} %bitcast.44), custom_call_target="tpu_custom_call" | custom-call | bytes 4063232 | tf_op jit(solution)/shard_map/pallas_call | solution.py:112
  2.5 8.4 %all-to-all-start.1 = ((bf16[16,496,128]{2,1,0:T(8,128)(2,1)}), bf16[16,496,128]{2,1,0:T(8,128)(2,1)}, u32[]{:S(2)}, u32[]{:S(2)}) async-start(bf16[16,496,128]{2,1,0:T(8,128)(2,1)} %shard_map.46), calls=%async_computation.1 | async-start | bytes 4063232 | tf_op jit(solution)/shard_map/all_to_all | solution.py:161
  10.9 5.8 %reshape.32 = bf16[8400,120]{1,0:T(8,128)(2,1)S(1)} reshape(bf16[120,8400]{1,0:T(8,128)(2,1)} %bitcast.45) | data formatting | bytes 4032000 | tf_op jit(solution)/shard_map/reshape | solution.py:135
  16.8 2.1 %convolution_convert_fusion = bf16[8400,120]{0,1:T(8,128)(2,1)} fusion(bf16[8400,120]{1,0:T(8,128)(2,1)S(1)} %reshape.32, bf16[120,120]{1,0:T(8,128)(2,1)S(1)} %copy-done), kind=kOutput, calls=%fused_computation | convolution fusion | flops 242928000 | bytes 4060800 | tf_op jit(solution)/shard_map/dot_general | solution.py:134
  18.9 4.1 %copy.20 = bf16[8400,120]{1,0:T(8,128)(2,1)} copy(bf16[8400,120]{0,1:T(8,128)(2,1)} %convolution_convert_fusion) | data formatting | bytes 4032000 | tf_op jit(solution)/shard_map/convert_element_type | solution.py:138
  23.0 2.8 %reshape.33 = bf16[120,70,120]{2,1,0:T(8,128)(2,1)S(1)} reshape(bf16[8400,120]{1,0:T(8,128)(2,1)} %copy.20) | data formatting | bytes 4032000 | tf_op jit(solution)/shard_map/reshape | solution.py:141
  25.8 2.1 %convert_bitcast_fusion = bf16[120,70,120]{2,1,0:T(8,128)(2,1)} fusion(bf16[120,70,120]{2,1,0:T(8,128)(2,1)S(1)} %reshape.33, bf16[70,70]{1,0:T(8,128)(2,1)S(1)} %copy-done.2), kind=kOutput, calls=%fused_computation.5 | convolution fusion | flops 142128000 | bytes 4041800 | tf_op jit(solution)/shard_map/tab,ac->tcb/dot_general | solution.py:139
  27.9 3.6 %copy.22 = bf16[120,70,120]{0,2,1:T(8,128)(2,1)S(1)} copy(bf16[120,70,120]{2,1,0:T(8,128)(2,1)} %convert_bitcast_fusion) | data formatting | bytes 4032000 | tf_op jit(solution)/shard_map/convert_element_type | solution.py:144
  31.5 1.5 %slice.17 = bf16[120,8192]{0,1:T(8,128)(2,1)} slice(bf16[120,8400]{0,1:T(8,128)(2,1)S(1)} %bitcast.40), slice={[0:120], [0:8192]} | slice | bytes 3932160 | tf_op jit(solution)/shard_map/slice | solution.py:146
  33.0 0.2 fusion.4
  33.2 0.1 copy.26
  33.3 0.7 fusion.3
  34.2 0.1 pad.9.clone
  34.2 2.4 %convolution_convert_fusion.2 = bf16[64,128,112]{1,2,0:T(8,128)(2,1)S(1)} fusion(bf16[120,64,128]{0,2,1:T(8,128)(2,1)} %bitcast.43, bf16[120,120]{1,0:T(8,128)(2,1)S(1)} %copy-done.1), kind=kOutput, calls=%fused_computation.10 | convolution fusion | flops 221118464 | bytes 3829888 | tf_op jit(solution)/shard_map/ts,tjl->jsl/dot_general | solution.py:147
  36.6 1.8 %maximum_maximum_fusion = bf16[16,496,128]{2,1,0:T(8,128)(2,1)} fusion(bf16[16,47,128]{2,1,0:T(8,128)(2,1)S(1)} %reshape.41, bf16[16,448,128]{2,1,0:T(8,128)(2,1)S(1)} %bitcast.46, bf16[496]{0:T(512)(128)(2,1)S(1)} %pad.9.clone), kind=kLoop, calls=%fused_computation.6 | loop fusion | flops 6094848 | bytes 4060128 | tf_op jit(solution)/shard_map/concatenate | solution.py:45
  38.4 14.5 %all-to-all-done.1 = bf16[16,496,128]{2,1,0:T(8,128)(2,1)} async-done(((bf16[16,496,128]{2,1,0:T(8,128)(2,1)}), bf16[16,496,128]{2,1,0:T(8,128)(2,1)}, u32[]{:S(2)}, u32[]{:S(2)}) %all-to-all-start.1) | async-done | bytes 2031648 | tf_op jit(solution)/shard_map/all_to_all | solution.py:161
  52.9 9.7 %all-to-all-start = ((bf16[16,496,128]{2,1,0:T(8,128)(2,1)}), bf16[16,496,128]{2,1,0:T(8,128)(2,1)S(1)}, u32[]{:S(2)}, u32[]{:S(2)}) async-start(bf16[16,496,128]{2,1,0:T(8,128)(2,1)} %maximum_maximum_fusion), calls=%async_computation | async-start | bytes 4063232 | tf_op jit(solution)/shard_map/all_to_all | solution.py:163
  62.7 4.4 %collective-permute-done = bf16[16,496,128]{2,1,0:T(8,128)(2,1)} collective-permute-done((bf16[16,496,128]{2,1,0:T(8,128)(2,1)}, bf16[16,496,128]{2,1,0:T(8,128)(2,1)}, u32[]{:S(2)}, u32[]{:S(2)}) %collective-permute-start) | collective-permute-done | bytes 2031648 | tf_op jit(solution)/shard_map/ppermute | solution.py:169
  67.1 2.4 %broadcast_select_fusion.1 = (bf16[16,496,128]{2,1,0:T(8,128)(2,1)S(1)}, bf16[16,496,128]{2,1,0:T(8,128)(2,1)S(1)}) fusion(bf16[16,496,128]{2,1,0:T(8,128)(2,1)} %collective-permute-done, bf16[16,496,128]{2,1,0:T(8,128)(2,1)} %all-to-all-done.1, pred[]{:T(512)S(6)} %eq.9, pred[]{:T(512)S(6)} %eq.10), kind=kLoop, calls=%fused_computation.9 | loop fusion | flops 2031616 | bytes 8126466 | tf_op jit(solution)/shard_map/jit(_where)/select_n | solution.py:174
  69.5 2.2 %pad_maximum_fusion = bf16[32,496,128]{2,1,0:T(8,128)(2,1)} fusion(bf16[16,496,128]{2,1,0:T(8,128)(2,1)S(1)} %get-tuple-element.10, bf16[16,496,128]{2,1,0:T(8,128)(2,1)S(1)} %get-tuple-element.9), kind=kLoop, calls=%fused_computation.2 | loop fusion | flops 2031616 | bytes 8126464 | tf_op jit(solution)/shard_map/concatenate | solution.py:176
  71.8 32.2 %all-to-all-done = bf16[16,496,128]{2,1,0:T(8,128)(2,1)S(1)} async-done(((bf16[16,496,128]{2,1,0:T(8,128)(2,1)}), bf16[16,496,128]{2,1,0:T(8,128)(2,1)S(1)}, u32[]{:S(2)}, u32[]{:S(2)}) %all-to-all-start) | async-done | bytes 2031648 | tf_op jit(solution)/shard_map/all_to_all | solution.py:163
  104.0 3.3 %fusion = f32[16,32,1]{1,0,2:T(8,128)S(1)} fusion(bf16[32,496,128]{2,1,0:T(8,128)(2,1)} %pad_maximum_fusion, bf16[16,496,128]{2,1,0:T(8,128)(2,1)S(1)} %all-to-all-done), kind=kOutput, calls=%fused_computation.3 | convolution fusion | flops 65011712 | bytes 6096896 | tf_op jit(solution)/shard_map/dot_general | solution.py:177
  107.3 16.5 %all_to_all.19 = f32[16,1,32]{2,1,0:T(1,128)S(1)} all-to-all(f32[16,1,32]{2,1,0:T(1,128)S(1)} %bitcast.49), channel_id=1, replica_groups=mesh['rec'=2,'space'=16] {'space'}, dimensions={0} | all-to-all | bytes 4096 | tf_op jit(solution)/shard_map/all_to_all | solution.py:178
  123.9 0.5 reduce_sum.9
  (10 shorter events, 0.2 us)
Async XLA Ops:
  0.0 16.8 %copy-start = (bf16[120,120]{1,0:T(8,128)(2,1)S(1)}, bf16[120,120]{1,0:T(8,128)(2,1)}, u32[]{:S(2)}) copy-start(bf16[120,120]{1,0:T(8,128)(2,1)} %param.7) | copy-start | bytes 86404
  2.5 50.4 %all-to-all-start.1 = ((bf16[16,496,128]{2,1,0:T(8,128)(2,1)}), bf16[16,496,128]{2,1,0:T(8,128)(2,1)}, u32[]{:S(2)}, u32[]{:S(2)}) async-start(bf16[16,496,128]{2,1,0:T(8,128)(2,1)} %shard_map.46), calls=%async_computation.1 | async-start | bytes 4063232 | tf_op jit(solution)/shard_map/all_to_all | solution.py:161
  23.0 2.8 %copy-start.2 = (bf16[70,70]{1,0:T(8,128)(2,1)S(1)}, bf16[70,70]{1,0:T(8,128)(2,1)}, u32[]{:S(2)}) copy-start(bf16[70,70]{1,0:T(8,128)(2,1)} %param.6) | copy-start | bytes 29404
  31.5 1.5 %copy-start.1 = (bf16[120,120]{1,0:T(8,128)(2,1)S(1)}, bf16[120,120]{1,0:T(8,128)(2,1)}, u32[]{:S(2)}) copy-start(bf16[120,120]{1,0:T(8,128)(2,1)} %param.5) | copy-start | bytes 86404
  52.9 51.1 %all-to-all-start = ((bf16[16,496,128]{2,1,0:T(8,128)(2,1)}), bf16[16,496,128]{2,1,0:T(8,128)(2,1)S(1)}, u32[]{:S(2)}, u32[]{:S(2)}) async-start(bf16[16,496,128]{2,1,0:T(8,128)(2,1)} %maximum_maximum_fusion), calls=%async_computation | async-start | bytes 4063232 | tf_op jit(solution)/shard_map/all_to_all | solution.py:163
  62.6 4.5 %collective-permute-start = (bf16[16,496,128]{2,1,0:T(8,128)(2,1)}, bf16[16,496,128]{2,1,0:T(8,128)(2,1)}, u32[]{:S(2)}, u32[]{:S(2)}) collective-permute-start(bf16[16,496,128]{2,1,0:T(8,128)(2,1)} %all-to-all-done.1), channel_id=1, source_target_pairs={{0,16},{16,0},{1,17},{17,1},{2,18},{18,2},{3,19},{19,3},{4,20},{20... | collective-permute-start | bytes 6094856 | tf_op jit(solution)/shard_map/ppermute | solution.py:169

commit v11 on v10

--- a/solution.py
+++ b/solution.py
@@ -50,7 +50,7 @@
     chunks, rows, _ = out_hbm.shape
     main_tiles = chunks * per
     main_cols = main_tiles * LANE
-    groups = 4 if chunks % 4 == 0 else 1
+    groups = 8 if chunks % 8 == 0 else 1
     width = main_cols // groups
     loads = []
     for g in range(groups):
@@ -67,12 +67,16 @@
         loads.append(tail)
     stores = []
     per_group = chunks // groups
+    rest_ref[...] = jnp.zeros(rest_ref.shape, rest_ref.dtype)
+    low = time_count - full_rows
     for g in range(groups):
         loads[g].wait()
         for k in range(g * per_group, (g + 1) * per_group):
             for q in range(per):
                 j = k * per + q
                 main_out[k, q * full_rows:(q + 1) * full_rows, :] = values[0:full_rows, j * LANE:(j + 1) * LANE]
+                if low:
+                    rest_ref[j * low:(j + 1) * low, :] = values[full_rows:time_count, j * LANE:(j + 1) * LANE].astype(jnp.float32)
         store = pltpu.make_async_copy(
             main_out.at[g * per_group:(g + 1) * per_group],
             out_hbm.at[g * per_group:(g + 1) * per_group, 0:per * full_rows, :],
@@ -82,13 +86,7 @@
         stores.append(store)
     if cell_count > main_cols:
         loads[groups].wait()
-    rest_ref[...] = jnp.zeros(rest_ref.shape, rest_ref.dtype)
-    low = time_count - full_rows
-    at = 0
-    if low:
-        for j in range(main_tiles):
-            rest_ref[at:at + low, :] = values[full_rows:time_count, j * LANE:(j + 1) * LANE].astype(jnp.float32)
-            at += low
+    at = low * main_tiles
     for lo in range(main_cols, cell_count, LANE):
         span = min(LANE, cell_count - lo)
         rest_ref[at:at + time_count, 0:span] = values[:, lo:lo + span].astype(jnp.float32)
@@ -119,8 +117,8 @@
             pltpu.VMEM((chunks, per * full_rows, LANE), values.dtype),
             pltpu.VMEM((chunks, rows - per * full_rows, LANE), values.dtype),
             pltpu.VMEM((share * chunks, LANE), jnp.float32),
-            pltpu.SemaphoreType.DMA((5,)),
-            pltpu.SemaphoreType.DMA((5,)),
+            pltpu.SemaphoreType.DMA((9,)),
+            pltpu.SemaphoreType.DMA((9,)),
         ],
         cost_estimate=pl.CostEstimate(flops=0, transcendentals=0, bytes_accessed=4 * chunks * rows * LANE),
     )(values)

time: 125 us -> 125 us (level)
  no operation moved by 1% of the time
where the time goes in v11:
time: 125 us; the launch traced here: 124 us
  waiting for transfers between devices  51.1 us (41%)
  local copies, waits for them, and re-layouts  18.1 us (14%)
  starting transfers between devices  18.1 us (14%)
  blocking collectives  16.5 us (13%)
  matrix products  10.8 us (9%)
  other arithmetic  7.05 us (6%)
  Pallas kernels  2.62 us (2%)
    all_to_all x1, waiting for transfers between devices, local(): lax.all_to_all(weighted, 'space', split_axis=0, concat_axis=0, tiled=True)  32.2 us
    all_to_all x1, blocking collectives, local(): lax.all_to_all(partial_value, 'space', split_axis=0, concat_axis=0, tiled...  16.5 us
    all_to_all x1, waiting for transfers between devices, local(): lax.all_to_all(plain, 'space', split_axis=0, concat_axis=0, tiled=True)  14.5 us
    all_to_all x1, starting transfers between devices, local(): lax.all_to_all(weighted, 'space', split_axis=0, concat_axis=0, tiled=True)  9.71 us
    all_to_all x1, starting transfers between devices, local(): lax.all_to_all(plain, 'space', split_axis=0, concat_axis=0, tiled=True)  8.37 us
    reshape x1, local copies, waits for them, and re-layouts, weighted_dense_chunks(): footprint.reshape(time_count * lat_count, lon_count)  5.83 us
    ppermute x1, waiting for transfers between devices, local(): received.append(lax.ppermute(plain_here, 'rec', perm))  4.38 us
    convert_element_type x1, local copies, waits for them, and re-layouts, weighted_dense_chunks(): along_lon = jnp.dot(footprint.reshape(time_count * lat_count, lon_count),...  4.09 us
  transfers between devices with their start and end apart: 3, of which 3 were waited for; matrix products, arithmetic and copies ran while one was open for 26% of the time, Pallas kernels for 0%

profile of v11, /device:TPU:0, one launch (start us, length us, event | category | flops | bytes accessed | tf_op | source)
XLA Modules:
  0.0 124.5 jit_solution(17413959768615339723)
XLA Ops:
  0.0 2.6 %shard_map.46 = bf16[16,496,128]{2,1,0:T(8,128)(2,1)} custom-call(bf16[120,8400]{1,0:T(8,128)(2,1)} %bitcast.44), custom_call_target="tpu_custom_call" | custom-call | bytes 4063232 | tf_op jit(solution)/shard_map/pallas_call | solution.py:110
  2.6 8.4 %all-to-all-start.1 = ((bf16[16,496,128]{2,1,0:T(8,128)(2,1)}), bf16[16,496,128]{2,1,0:T(8,128)(2,1)}, u32[]{:S(2)}, u32[]{:S(2)}) async-start(bf16[16,496,128]{2,1,0:T(8,128)(2,1)} %shard_map.46), calls=%async_computation.1 | async-start | bytes 4063232 | tf_op jit(solution)/shard_map/all_to_all | solution.py:159
  11.0 5.8 %reshape.32 = bf16[8400,120]{1,0:T(8,128)(2,1)S(1)} reshape(bf16[120,8400]{1,0:T(8,128)(2,1)} %bitcast.45) | data formatting | bytes 4032000 | tf_op jit(solution)/shard_map/reshape | solution.py:133
  16.9 2.1 %convolution_convert_fusion = bf16[8400,120]{0,1:T(8,128)(2,1)} fusion(bf16[8400,120]{1,0:T(8,128)(2,1)S(1)} %reshape.32, bf16[120,120]{1,0:T(8,128)(2,1)S(1)} %copy-done), kind=kOutput, calls=%fused_computation | convolution fusion | flops 242928000 | bytes 4060800 | tf_op jit(solution)/shard_map/dot_general | solution.py:132
  19.0 4.1 %copy.20 = bf16[8400,120]{1,0:T(8,128)(2,1)} copy(bf16[8400,120]{0,1:T(8,128)(2,1)} %convolution_convert_fusion) | data formatting | bytes 4032000 | tf_op jit(solution)/shard_map/convert_element_type | solution.py:136
  23.1 2.8 %reshape.33 = bf16[120,70,120]{2,1,0:T(8,128)(2,1)S(1)} reshape(bf16[8400,120]{1,0:T(8,128)(2,1)} %copy.20) | data formatting | bytes 4032000 | tf_op jit(solution)/shard_map/reshape | solution.py:139
  25.9 2.1 %convert_bitcast_fusion = bf16[120,70,120]{2,1,0:T(8,128)(2,1)} fusion(bf16[120,70,120]{2,1,0:T(8,128)(2,1)S(1)} %reshape.33, bf16[70,70]{1,0:T(8,128)(2,1)S(1)} %copy-done.2), kind=kOutput, calls=%fused_computation.5 | convolution fusion | flops 142128000 | bytes 4041800 | tf_op jit(solution)/shard_map/tab,ac->tcb/dot_general | solution.py:137
  28.0 3.6 %copy.22 = bf16[120,70,120]{0,2,1:T(8,128)(2,1)S(1)} copy(bf16[120,70,120]{2,1,0:T(8,128)(2,1)} %convert_bitcast_fusion) | data formatting | bytes 4032000 | tf_op jit(solution)/shard_map/convert_element_type | solution.py:142
  31.6 1.5 %slice.17 = bf16[120,8192]{0,1:T(8,128)(2,1)} slice(bf16[120,8400]{0,1:T(8,128)(2,1)S(1)} %bitcast.40), slice={[0:120], [0:8192]} | slice | bytes 3932160 | tf_op jit(solution)/shard_map/slice | solution.py:144
  33.1 0.2 fusion.4
  33.3 0.1 copy.26
  33.4 0.7 fusion.3
  34.3 0.1 pad.9.clone
  34.3 2.4 %convolution_convert_fusion.2 = bf16[64,128,112]{1,2,0:T(8,128)(2,1)S(1)} fusion(bf16[120,64,128]{0,2,1:T(8,128)(2,1)} %bitcast.43, bf16[120,120]{1,0:T(8,128)(2,1)S(1)} %copy-done.1), kind=kOutput, calls=%fused_computation.10 | convolution fusion | flops 221118464 | bytes 3829888 | tf_op jit(solution)/shard_map/ts,tjl->jsl/dot_general | solution.py:145
  36.7 1.8 %maximum_maximum_fusion = bf16[16,496,128]{2,1,0:T(8,128)(2,1)} fusion(bf16[16,47,128]{2,1,0:T(8,128)(2,1)S(1)} %reshape.41, bf16[16,448,128]{2,1,0:T(8,128)(2,1)S(1)} %bitcast.46, bf16[496]{0:T(512)(128)(2,1)S(1)} %pad.9.clone), kind=kLoop, calls=%fused_computation.6 | loop fusion | flops 6094848 | bytes 4060128 | tf_op jit(solution)/shard_map/concatenate | solution.py:45
  38.5 14.5 %all-to-all-done.1 = bf16[16,496,128]{2,1,0:T(8,128)(2,1)} async-done(((bf16[16,496,128]{2,1,0:T(8,128)(2,1)}), bf16[16,496,128]{2,1,0:T(8,128)(2,1)}, u32[]{:S(2)}, u32[]{:S(2)}) %all-to-all-start.1) | async-done | bytes 2031648 | tf_op jit(solution)/shard_map/all_to_all | solution.py:159
  53.0 9.7 %all-to-all-start = ((bf16[16,496,128]{2,1,0:T(8,128)(2,1)}), bf16[16,496,128]{2,1,0:T(8,128)(2,1)S(1)}, u32[]{:S(2)}, u32[]{:S(2)}) async-start(bf16[16,496,128]{2,1,0:T(8,128)(2,1)} %maximum_maximum_fusion), calls=%async_computation | async-start | bytes 4063232 | tf_op jit(solution)/shard_map/all_to_all | solution.py:161
  62.8 4.4 %collective-permute-done = bf16[16,496,128]{2,1,0:T(8,128)(2,1)} collective-permute-done((bf16[16,496,128]{2,1,0:T(8,128)(2,1)}, bf16[16,496,128]{2,1,0:T(8,128)(2,1)}, u32[]{:S(2)}, u32[]{:S(2)}) %collective-permute-start) | collective-permute-done | bytes 2031648 | tf_op jit(solution)/shard_map/ppermute | solution.py:167
  67.2 2.4 %broadcast_select_fusion.1 = (bf16[16,496,128]{2,1,0:T(8,128)(2,1)S(1)}, bf16[16,496,128]{2,1,0:T(8,128)(2,1)S(1)}) fusion(bf16[16,496,128]{2,1,0:T(8,128)(2,1)} %collective-permute-done, bf16[16,496,128]{2,1,0:T(8,128)(2,1)} %all-to-all-done.1, pred[]{:T(512)S(6)} %eq.9, pred[]{:T(512)S(6)} %eq.10), kind=kLoop, calls=%fused_computation.9 | loop fusion | flops 2031616 | bytes 8126466 | tf_op jit(solution)/shard_map/jit(_where)/select_n | solution.py:172
  69.6 2.2 %pad_maximum_fusion = bf16[32,496,128]{2,1,0:T(8,128)(2,1)} fusion(bf16[16,496,128]{2,1,0:T(8,128)(2,1)S(1)} %get-tuple-element.10, bf16[16,496,128]{2,1,0:T(8,128)(2,1)S(1)} %get-tuple-element.9), kind=kLoop, calls=%fused_computation.2 | loop fusion | flops 2031616 | bytes 8126464 | tf_op jit(solution)/shard_map/concatenate | solution.py:174
  71.9 32.2 %all-to-all-done = bf16[16,496,128]{2,1,0:T(8,128)(2,1)S(1)} async-done(((bf16[16,496,128]{2,1,0:T(8,128)(2,1)}), bf16[16,496,128]{2,1,0:T(8,128)(2,1)S(1)}, u32[]{:S(2)}, u32[]{:S(2)}) %all-to-all-start) | async-done | bytes 2031648 | tf_op jit(solution)/shard_map/all_to_all | solution.py:161
  104.1 3.3 %fusion = f32[16,32,1]{1,0,2:T(8,128)S(1)} fusion(bf16[32,496,128]{2,1,0:T(8,128)(2,1)} %pad_maximum_fusion, bf16[16,496,128]{2,1,0:T(8,128)(2,1)S(1)} %all-to-all-done), kind=kOutput, calls=%fused_computation.3 | convolution fusion | flops 65011712 | bytes 6096896 | tf_op jit(solution)/shard_map/dot_general | solution.py:175
  107.4 16.5 %all_to_all.19 = f32[16,1,32]{2,1,0:T(1,128)S(1)} all-to-all(f32[16,1,32]{2,1,0:T(1,128)S(1)} %bitcast.49), channel_id=1, replica_groups=mesh['rec'=2,'space'=16] {'space'}, dimensions={0} | all-to-all | bytes 4096 | tf_op jit(solution)/shard_map/all_to_all | solution.py:176
  124.0 0.5 reduce_sum.9
  (10 shorter events, 0.2 us)
Async XLA Ops:
  0.0 16.8 %copy-start = (bf16[120,120]{1,0:T(8,128)(2,1)S(1)}, bf16[120,120]{1,0:T(8,128)(2,1)}, u32[]{:S(2)}) copy-start(bf16[120,120]{1,0:T(8,128)(2,1)} %param.7) | copy-start | bytes 86404
  2.6 50.4 %all-to-all-start.1 = ((bf16[16,496,128]{2,1,0:T(8,128)(2,1)}), bf16[16,496,128]{2,1,0:T(8,128)(2,1)}, u32[]{:S(2)}, u32[]{:S(2)}) async-start(bf16[16,496,128]{2,1,0:T(8,128)(2,1)} %shard_map.46), calls=%async_computation.1 | async-start | bytes 4063232 | tf_op jit(solution)/shard_map/all_to_all | solution.py:159
  23.1 2.8 %copy-start.2 = (bf16[70,70]{1,0:T(8,128)(2,1)S(1)}, bf16[70,70]{1,0:T(8,128)(2,1)}, u32[]{:S(2)}) copy-start(bf16[70,70]{1,0:T(8,128)(2,1)} %param.6) | copy-start | bytes 29404
  31.6 1.5 %copy-start.1 = (bf16[120,120]{1,0:T(8,128)(2,1)S(1)}, bf16[120,120]{1,0:T(8,128)(2,1)}, u32[]{:S(2)}) copy-start(bf16[120,120]{1,0:T(8,128)(2,1)} %param.5) | copy-start | bytes 86404
  53.0 51.1 %all-to-all-start = ((bf16[16,496,128]{2,1,0:T(8,128)(2,1)}), bf16[16,496,128]{2,1,0:T(8,128)(2,1)S(1)}, u32[]{:S(2)}, u32[]{:S(2)}) async-start(bf16[16,496,128]{2,1,0:T(8,128)(2,1)} %maximum_maximum_fusion), calls=%async_computation | async-start | bytes 4063232 | tf_op jit(solution)/shard_map/all_to_all | solution.py:161
  62.7 4.5 %collective-permute-start = (bf16[16,496,128]{2,1,0:T(8,128)(2,1)}, bf16[16,496,128]{2,1,0:T(8,128)(2,1)}, u32[]{:S(2)}, u32[]{:S(2)}) collective-permute-start(bf16[16,496,128]{2,1,0:T(8,128)(2,1)} %all-to-all-done.1), channel_id=1, source_target_pairs={{0,16},{16,0},{1,17},{17,1},{2,18},{18,2},{3,19},{19,3},{4,20},{20... | collective-permute-start | bytes 6094856 | tf_op jit(solution)/shard_map/ppermute | solution.py:167

commit v12 on v10

--- a/solution.py
+++ b/solution.py
@@ -167,14 +167,14 @@
     for shift in range(1, rec_count):
         perm = [(i, (i + shift) % rec_count) for i in range(rec_count)]
         received.append(lax.ppermute(plain_here, "rec", perm))
+    blocks = [lax.dot_general(weighted_here, part, contract, preferred_element_type=jnp.float32) for part in received]
     ordered = []
     for g in range(rec_count):
-        choice = received[0]
+        choice = blocks[0]
         for shift in range(1, rec_count):
-            choice = jnp.where((rec_index + rec_count - shift) % rec_count == g, received[shift], choice)
+            choice = jnp.where((rec_index + rec_count - shift) % rec_count == g, blocks[shift], choice)
         ordered.append(choice)
-    everyone = jnp.concatenate(ordered, axis=0)
-    partial_value = lax.dot_general(weighted_here, everyone, contract, preferred_element_type=jnp.float32)
+    partial_value = jnp.concatenate(ordered, axis=1)
     spread = lax.all_to_all(partial_value, "space", split_axis=0, concat_axis=0, tiled=True)
     return jnp.sum(spread, axis=0, keepdims=True)
 

time: 125 us -> 127 us (1.016)
  waiting for transfers between devices: 51.1 us -> 55.8 us
  other arithmetic: 7.05 us -> 2.45 us
  matrix products: 10.9 us -> 12.8 us
    all_to_all x1, waiting for transfers between devices: 32.2 us -> 41.3 us  [local(): lax.all_to_all(weighted, 'space', split_axis=0, concat_axis=0, tiled=True)]
    ppermute x1, waiting for transfers between devices: 4.38 us -> 0.01 us  [local(): received.append(lax.ppermute(plain_here, 'rec', perm))]
    select_n x1 -> x0, other arithmetic: 2.44 us -> none  [local(): jnp.where((rec_index + rec_count - shift) % rec_count == g, received[shif...]
    concatenate x1, other arithmetic: 2.24 us -> 0.09 us  [local(): partial_value = jnp.concatenate(ordered, axis=1)]
    dot_general x1 -> x2, matrix products: 3.31 us -> 5.29 us  [local(): lax.dot_general(weighted_here, part, contract, preferred_element_type=jnp...]
  transfers between devices with their start and end apart: 3 -> 3, of which waited for: 3 -> 2; matrix products, arithmetic and copies ran while one was open for 26% -> 24% of each run, Pallas kernels for 0% -> 0%
where the time goes in v12:
time: 127 us; the launch traced here: 126 us
  waiting for transfers between devices  55.8 us (44%)
  local copies, waits for them, and re-layouts  18.1 us (14%)
  starting transfers between devices  18.1 us (14%)
  blocking collectives  16.5 us (13%)
  matrix products  12.8 us (10%)
  Pallas kernels  2.52 us (2%)
  other arithmetic  2.45 us (2%)
    all_to_all x1, waiting for transfers between devices, local(): lax.all_to_all(weighted, 'space', split_axis=0, concat_axis=0, tiled=True)  41.3 us
    all_to_all x1, blocking collectives, local(): lax.all_to_all(partial_value, 'space', split_axis=0, concat_axis=0, tiled...  16.5 us
    all_to_all x1, waiting for transfers between devices, local(): lax.all_to_all(plain, 'space', split_axis=0, concat_axis=0, tiled=True)  14.5 us
    all_to_all x1, starting transfers between devices, local(): lax.all_to_all(weighted, 'space', split_axis=0, concat_axis=0, tiled=True)  9.71 us
    all_to_all x1, starting transfers between devices, local(): lax.all_to_all(plain, 'space', split_axis=0, concat_axis=0, tiled=True)  8.37 us
    reshape x1, local copies, waits for them, and re-layouts, weighted_dense_chunks(): footprint.reshape(time_count * lat_count, lon_count)  5.83 us
    dot_general x2, matrix products, local(): lax.dot_general(weighted_here, part, contract, preferred_element_type=jnp...  5.29 us
    convert_element_type x1, local copies, waits for them, and re-layouts, weighted_dense_chunks(): along_lon = jnp.dot(footprint.reshape(time_count * lat_count, lon_count),...  4.09 us
  transfers between devices with their start and end apart: 3, of which 2 were waited for; matrix products, arithmetic and copies ran while one was open for 24% of the time, Pallas kernels for 0%

profile of v12, /device:TPU:0, one launch (start us, length us, event | category | flops | bytes accessed | tf_op | source)
XLA Modules:
  0.0 126.5 jit_solution(15714801982449466890)
XLA Ops:
  0.0 2.5 %shard_map.46 = bf16[16,496,128]{2,1,0:T(8,128)(2,1)} custom-call(bf16[120,8400]{1,0:T(8,128)(2,1)} %bitcast.47), custom_call_target="tpu_custom_call" | custom-call | bytes 4063232 | tf_op jit(solution)/shard_map/pallas_call | solution.py:112
  2.5 8.4 %all-to-all-start.1 = ((bf16[16,496,128]{2,1,0:T(8,128)(2,1)}), bf16[16,496,128]{2,1,0:T(8,128)(2,1)}, u32[]{:S(2)}, u32[]{:S(2)}) async-start(bf16[16,496,128]{2,1,0:T(8,128)(2,1)} %shard_map.46), calls=%async_computation.1 | async-start | bytes 4063232 | tf_op jit(solution)/shard_map/all_to_all | solution.py:161
  10.9 5.8 %reshape.32 = bf16[8400,120]{1,0:T(8,128)(2,1)S(1)} reshape(bf16[120,8400]{1,0:T(8,128)(2,1)} %bitcast.48) | data formatting | bytes 4032000 | tf_op jit(solution)/shard_map/reshape | solution.py:135
  16.8 2.1 %convolution_convert_fusion = bf16[8400,120]{0,1:T(8,128)(2,1)} fusion(bf16[8400,120]{1,0:T(8,128)(2,1)S(1)} %reshape.32, bf16[120,120]{1,0:T(8,128)(2,1)S(1)} %copy-done), kind=kOutput, calls=%fused_computation | convolution fusion | flops 242928000 | bytes 4060800 | tf_op jit(solution)/shard_map/dot_general | solution.py:134
  18.9 4.1 %copy.22 = bf16[8400,120]{1,0:T(8,128)(2,1)} copy(bf16[8400,120]{0,1:T(8,128)(2,1)} %convolution_convert_fusion) | data formatting | bytes 4032000 | tf_op jit(solution)/shard_map/convert_element_type | solution.py:138
  23.0 2.8 %reshape.33 = bf16[120,70,120]{2,1,0:T(8,128)(2,1)S(1)} reshape(bf16[8400,120]{1,0:T(8,128)(2,1)} %copy.22) | data formatting | bytes 4032000 | tf_op jit(solution)/shard_map/reshape | solution.py:141
  25.8 2.1 %convert_bitcast_fusion = bf16[120,70,120]{2,1,0:T(8,128)(2,1)} fusion(bf16[120,70,120]{2,1,0:T(8,128)(2,1)S(1)} %reshape.33, bf16[70,70]{1,0:T(8,128)(2,1)S(1)} %copy-done.2), kind=kOutput, calls=%fused_computation.2 | convolution fusion | flops 142128000 | bytes 4041800 | tf_op jit(solution)/shard_map/tab,ac->tcb/dot_general | solution.py:139
  27.9 3.6 %copy.24 = bf16[120,70,120]{0,2,1:T(8,128)(2,1)S(1)} copy(bf16[120,70,120]{2,1,0:T(8,128)(2,1)} %convert_bitcast_fusion) | data formatting | bytes 4032000 | tf_op jit(solution)/shard_map/convert_element_type | solution.py:144
  31.5 1.5 %slice.17 = bf16[120,8192]{0,1:T(8,128)(2,1)} slice(bf16[120,8400]{0,1:T(8,128)(2,1)S(1)} %bitcast.43), slice={[0:120], [0:8192]} | slice | bytes 3932160 | tf_op jit(solution)/shard_map/slice | solution.py:146
  33.0 0.2 fusion.7
  33.2 0.1 copy.28
  33.3 0.7 fusion.6
  34.2 0.1 pad.9.clone
  34.2 2.4 %convolution_convert_fusion.2 = bf16[64,128,112]{1,2,0:T(8,128)(2,1)S(1)} fusion(bf16[120,64,128]{0,2,1:T(8,128)(2,1)} %bitcast.46, bf16[120,120]{1,0:T(8,128)(2,1)S(1)} %copy-done.1), kind=kOutput, calls=%fused_computation.8 | convolution fusion | flops 221118464 | bytes 3829888 | tf_op jit(solution)/shard_map/ts,tjl->jsl/dot_general | solution.py:147
  36.6 1.8 %maximum_maximum_fusion = bf16[16,496,128]{2,1,0:T(8,128)(2,1)} fusion(bf16[16,47,128]{2,1,0:T(8,128)(2,1)S(1)} %reshape.41, bf16[16,448,128]{2,1,0:T(8,128)(2,1)S(1)} %bitcast.49, bf16[496]{0:T(512)(128)(2,1)S(1)} %pad.9.clone), kind=kLoop, calls=%fused_computation.3 | loop fusion | flops 6094848 | bytes 4060128 | tf_op jit(solution)/shard_map/concatenate | solution.py:45
  38.4 14.5 %all-to-all-done.1 = bf16[16,496,128]{2,1,0:T(8,128)(2,1)} async-done(((bf16[16,496,128]{2,1,0:T(8,128)(2,1)}), bf16[16,496,128]{2,1,0:T(8,128)(2,1)}, u32[]{:S(2)}, u32[]{:S(2)}) %all-to-all-start.1) | async-done | bytes 2031648 | tf_op jit(solution)/shard_map/all_to_all | solution.py:161
  52.9 9.7 %all-to-all-start = ((bf16[16,496,128]{2,1,0:T(8,128)(2,1)}), bf16[16,496,128]{2,1,0:T(8,128)(2,1)S(1)}, u32[]{:S(2)}, u32[]{:S(2)}) async-start(bf16[16,496,128]{2,1,0:T(8,128)(2,1)} %maximum_maximum_fusion), calls=%async_computation | async-start | bytes 4063232 | tf_op jit(solution)/shard_map/all_to_all | solution.py:163
  62.6 0.1 collective-permute-start
  62.7 41.3 %all-to-all-done = bf16[16,496,128]{2,1,0:T(8,128)(2,1)S(1)} async-done(((bf16[16,496,128]{2,1,0:T(8,128)(2,1)}), bf16[16,496,128]{2,1,0:T(8,128)(2,1)S(1)}, u32[]{:S(2)}, u32[]{:S(2)}) %all-to-all-start) | async-done | bytes 2031648 | tf_op jit(solution)/shard_map/all_to_all | solution.py:163
  104.0 2.6 %fusion.13 = f32[16,16]{1,0:T(8,128)S(1)} fusion(bf16[16,496,128]{2,1,0:T(8,128)(2,1)} %all-to-all-done.1, bf16[16,496,128]{2,1,0:T(8,128)(2,1)S(1)} %all-to-all-done), kind=kOutput, calls=%fused_computation.15 | convolution fusion | flops 32505856 | bytes 4064256 | tf_op jit(solution)/shard_map/dot_general | solution.py:170
  106.6 2.7 %broadcast_select_fusion.1 = (f32[16,16]{1,0:T(8,128)S(1)}, f32[16,16]{1,0:T(8,128)S(1)}) fusion(f32[16,16]{1,0:T(8,128)S(1)} %fusion.13, pred[]{:T(512)S(6)} %eq.9, pred[]{:T(512)S(6)} %eq.10, bf16[16,496,128]{2,1,0:T(8,128)(2,1)} %collective-permute-done, bf16[16,496,128]{2,1,0:T(8,128)(2,1)S(1)} %all-to-all-done), kind=kOutput, calls=%fused_computation.24 | convolution fusion | flops 32506368 | bytes 4066306 | tf_op jit(solution)/shard_map/dot_general | solution.py:170
  109.3 0.1 pad_maximum_fusion.1
  109.4 16.5 %all_to_all.19 = f32[16,1,32]{2,1,0:T(1,128)S(1)} all-to-all(f32[16,1,32]{2,1,0:T(1,128)S(1)} %bitcast.52), channel_id=1, replica_groups=mesh['rec'=2,'space'=16] {'space'}, dimensions={0} | all-to-all | bytes 4096 | tf_op jit(solution)/shard_map/all_to_all | solution.py:178
  125.9 0.5 reduce_sum.9
  (10 shorter events, 0.1 us)
Async XLA Ops:
  0.0 16.8 %copy-start = (bf16[120,120]{1,0:T(8,128)(2,1)S(1)}, bf16[120,120]{1,0:T(8,128)(2,1)}, u32[]{:S(2)}) copy-start(bf16[120,120]{1,0:T(8,128)(2,1)} %param.7) | copy-start | bytes 86404
  2.5 50.4 %all-to-all-start.1 = ((bf16[16,496,128]{2,1,0:T(8,128)(2,1)}), bf16[16,496,128]{2,1,0:T(8,128)(2,1)}, u32[]{:S(2)}, u32[]{:S(2)}) async-start(bf16[16,496,128]{2,1,0:T(8,128)(2,1)} %shard_map.46), calls=%async_computation.1 | async-start | bytes 4063232 | tf_op jit(solution)/shard_map/all_to_all | solution.py:161
  23.0 2.8 %copy-start.2 = (bf16[70,70]{1,0:T(8,128)(2,1)S(1)}, bf16[70,70]{1,0:T(8,128)(2,1)}, u32[]{:S(2)}) copy-start(bf16[70,70]{1,0:T(8,128)(2,1)} %param.6) | copy-start | bytes 29404
  31.5 1.5 %copy-start.1 = (bf16[120,120]{1,0:T(8,128)(2,1)S(1)}, bf16[120,120]{1,0:T(8,128)(2,1)}, u32[]{:S(2)}) copy-start(bf16[120,120]{1,0:T(8,128)(2,1)} %param.5) | copy-start | bytes 86404
  52.9 51.1 %all-to-all-start = ((bf16[16,496,128]{2,1,0:T(8,128)(2,1)}), bf16[16,496,128]{2,1,0:T(8,128)(2,1)S(1)}, u32[]{:S(2)}, u32[]{:S(2)}) async-start(bf16[16,496,128]{2,1,0:T(8,128)(2,1)} %maximum_maximum_fusion), calls=%async_computation | async-start | bytes 4063232 | tf_op jit(solution)/shard_map/all_to_all | solution.py:163
  62.6 44.0 %collective-permute-start = (bf16[16,496,128]{2,1,0:T(8,128)(2,1)}, bf16[16,496,128]{2,1,0:T(8,128)(2,1)}, u32[]{:S(2)}, u32[]{:S(2)}) collective-permute-start(bf16[16,496,128]{2,1,0:T(8,128)(2,1)} %all-to-all-done.1), channel_id=1, source_target_pairs={{0,16},{16,0},{1,17},{17,1},{2,18},{18,2},{3,19},{19,3},{4,20},{20... | collective-permute-start | bytes 6094856 | tf_op jit(solution)/shard_map/ppermute | solution.py:169

commit v13 on v10

--- a/solution.py
+++ b/solution.py
@@ -45,7 +45,7 @@
     return jnp.concatenate(pieces, axis=1)
 
 
-def pack_kernel(full_rows, per, share, values_hbm, out_hbm, values, main_out, rest_out, rest_ref, in_sems, out_sems):
+def pack_kernel(full_rows, per, share, values_hbm, out_hbm, values, rest_out, rest_ref, in_sems, out_sems):
     time_count, cell_count = values.shape
     chunks, rows, _ = out_hbm.shape
     main_tiles = chunks * per
@@ -72,14 +72,13 @@
         for k in range(g * per_group, (g + 1) * per_group):
             for q in range(per):
                 j = k * per + q
-                main_out[k, q * full_rows:(q + 1) * full_rows, :] = values[0:full_rows, j * LANE:(j + 1) * LANE]
-        store = pltpu.make_async_copy(
-            main_out.at[g * per_group:(g + 1) * per_group],
-            out_hbm.at[g * per_group:(g + 1) * per_group, 0:per * full_rows, :],
-            out_sems.at[g],
-        )
-        store.start()
-        stores.append(store)
+                store = pltpu.make_async_copy(
+                    values.at[0:full_rows, j * LANE:(j + 1) * LANE],
+                    out_hbm.at[k, q * full_rows:(q + 1) * full_rows, :],
+                    out_sems.at[j],
+                )
+                store.start()
+                stores.append(store)
     if cell_count > main_cols:
         loads[groups].wait()
     rest_ref[...] = jnp.zeros(rest_ref.shape, rest_ref.dtype)
@@ -98,7 +97,7 @@
         rest_out[k, 0:share, :] = rest_ref[k * share:(k + 1) * share, :].astype(rest_out.dtype)
         if tail_rows > share:
             rest_out[k, share:, :] = jnp.zeros((tail_rows - share, LANE), rest_out.dtype)
-    last = pltpu.make_async_copy(rest_out, out_hbm.at[:, per * full_rows:rows, :], out_sems.at[groups])
+    last = pltpu.make_async_copy(rest_out, out_hbm.at[:, per * full_rows:rows, :], out_sems.at[main_tiles])
     last.start()
     for store in stores:
         store.wait()
@@ -116,11 +115,10 @@
         out_specs=pl.BlockSpec(memory_space=pl.ANY),
         scratch_shapes=[
             pltpu.VMEM((time_count, cell_count), values.dtype),
-            pltpu.VMEM((chunks, per * full_rows, LANE), values.dtype),
             pltpu.VMEM((chunks, rows - per * full_rows, LANE), values.dtype),
             pltpu.VMEM((share * chunks, LANE), jnp.float32),
             pltpu.SemaphoreType.DMA((5,)),
-            pltpu.SemaphoreType.DMA((5,)),
+            pltpu.SemaphoreType.DMA((chunks * per + 1,)),
         ],
         cost_estimate=pl.CostEstimate(flops=0, transcendentals=0, bytes_accessed=4 * chunks * rows * LANE),
     )(values)

time: 125 us -> 125 us (level)
  no operation moved by 1% of the time
where the time goes in v13:
time: 125 us
  waiting for transfers between devices  51.1 us (41%)
  local copies, waits for them, and re-layouts  18.1 us (14%)
  starting transfers between devices  18.1 us (14%)
  blocking collectives  16.5 us (13%)
  matrix products  10.8 us (9%)
  other arithmetic  7.05 us (6%)
  Pallas kernels  2.98 us (2%)
    all_to_all x1, waiting for transfers between devices, local(): lax.all_to_all(weighted, 'space', split_axis=0, concat_axis=0, tiled=True)  32.2 us
    all_to_all x1, blocking collectives, local(): lax.all_to_all(partial_value, 'space', split_axis=0, concat_axis=0, tiled...  16.5 us
    all_to_all x1, waiting for transfers between devices, local(): lax.all_to_all(plain, 'space', split_axis=0, concat_axis=0, tiled=True)  14.5 us
    all_to_all x1, starting transfers between devices, local(): lax.all_to_all(weighted, 'space', split_axis=0, concat_axis=0, tiled=True)  9.71 us
    all_to_all x1, starting transfers between devices, local(): lax.all_to_all(plain, 'space', split_axis=0, concat_axis=0, tiled=True)  8.37 us
    reshape x1, local copies, waits for them, and re-layouts, weighted_dense_chunks(): footprint.reshape(time_count * lat_count, lon_count)  5.83 us
    ppermute x1, waiting for transfers between devices, local(): received.append(lax.ppermute(plain_here, 'rec', perm))  4.38 us
    convert_element_type x1, local copies, waits for them, and re-layouts, weighted_dense_chunks(): along_lon = jnp.dot(footprint.reshape(time_count * lat_count, lon_count),...  4.09 us
  transfers between devices with their start and end apart: 3, of which 3 were waited for; matrix products, arithmetic and copies ran while one was open for 26% of the time, Pallas kernels for 0%

profile of v13, /device:TPU:0, one launch (start us, length us, event | category | flops | bytes accessed | tf_op | source)
XLA Modules:
  0.0 124.9 jit_solution(1263259430001577670)
XLA Ops:
  0.0 3.0 %shard_map.46 = bf16[16,496,128]{2,1,0:T(8,128)(2,1)} custom-call(bf16[120,8400]{1,0:T(8,128)(2,1)} %bitcast.44), custom_call_target="tpu_custom_call" | custom-call | bytes 4063232 | tf_op jit(solution)/shard_map/pallas_call | solution.py:111
  3.0 8.4 %all-to-all-start.1 = ((bf16[16,496,128]{2,1,0:T(8,128)(2,1)}), bf16[16,496,128]{2,1,0:T(8,128)(2,1)}, u32[]{:S(2)}, u32[]{:S(2)}) async-start(bf16[16,496,128]{2,1,0:T(8,128)(2,1)} %shard_map.46), calls=%async_computation.1 | async-start | bytes 4063232 | tf_op jit(solution)/shard_map/all_to_all | solution.py:159
  11.4 5.8 %reshape.32 = bf16[8400,120]{1,0:T(8,128)(2,1)S(1)} reshape(bf16[120,8400]{1,0:T(8,128)(2,1)} %bitcast.45) | data formatting | bytes 4032000 | tf_op jit(solution)/shard_map/reshape | solution.py:133
  17.2 2.1 %convolution_convert_fusion = bf16[8400,120]{0,1:T(8,128)(2,1)} fusion(bf16[8400,120]{1,0:T(8,128)(2,1)S(1)} %reshape.32, bf16[120,120]{1,0:T(8,128)(2,1)S(1)} %copy-done), kind=kOutput, calls=%fused_computation | convolution fusion | flops 242928000 | bytes 4060800 | tf_op jit(solution)/shard_map/dot_general | solution.py:132
  19.3 4.1 %copy.20 = bf16[8400,120]{1,0:T(8,128)(2,1)} copy(bf16[8400,120]{0,1:T(8,128)(2,1)} %convolution_convert_fusion) | data formatting | bytes 4032000 | tf_op jit(solution)/shard_map/convert_element_type | solution.py:136
  23.4 2.8 %reshape.33 = bf16[120,70,120]{2,1,0:T(8,128)(2,1)S(1)} reshape(bf16[8400,120]{1,0:T(8,128)(2,1)} %copy.20) | data formatting | bytes 4032000 | tf_op jit(solution)/shard_map/reshape | solution.py:139
  26.2 2.1 %convert_bitcast_fusion = bf16[120,70,120]{2,1,0:T(8,128)(2,1)} fusion(bf16[120,70,120]{2,1,0:T(8,128)(2,1)S(1)} %reshape.33, bf16[70,70]{1,0:T(8,128)(2,1)S(1)} %copy-done.2), kind=kOutput, calls=%fused_computation.5 | convolution fusion | flops 142128000 | bytes 4041800 | tf_op jit(solution)/shard_map/tab,ac->tcb/dot_general | solution.py:137
  28.4 3.6 %copy.22 = bf16[120,70,120]{0,2,1:T(8,128)(2,1)S(1)} copy(bf16[120,70,120]{2,1,0:T(8,128)(2,1)} %convert_bitcast_fusion) | data formatting | bytes 4032000 | tf_op jit(solution)/shard_map/convert_element_type | solution.py:142
  32.0 1.5 %slice.17 = bf16[120,8192]{0,1:T(8,128)(2,1)} slice(bf16[120,8400]{0,1:T(8,128)(2,1)S(1)} %bitcast.40), slice={[0:120], [0:8192]} | slice | bytes 3932160 | tf_op jit(solution)/shard_map/slice | solution.py:144
  33.4 0.2 fusion.4
  33.6 0.1 copy.26
  33.8 0.7 fusion.3
  34.6 0.1 pad.9.clone
  34.7 2.3 %convolution_convert_fusion.2 = bf16[64,128,112]{1,2,0:T(8,128)(2,1)S(1)} fusion(bf16[120,64,128]{0,2,1:T(8,128)(2,1)} %bitcast.43, bf16[120,120]{1,0:T(8,128)(2,1)S(1)} %copy-done.1), kind=kOutput, calls=%fused_computation.10 | convolution fusion | flops 221118464 | bytes 3829888 | tf_op jit(solution)/shard_map/ts,tjl->jsl/dot_general | solution.py:145
  37.0 1.8 %maximum_maximum_fusion = bf16[16,496,128]{2,1,0:T(8,128)(2,1)} fusion(bf16[16,47,128]{2,1,0:T(8,128)(2,1)S(1)} %reshape.41, bf16[16,448,128]{2,1,0:T(8,128)(2,1)S(1)} %bitcast.46, bf16[496]{0:T(512)(128)(2,1)S(1)} %pad.9.clone), kind=kLoop, calls=%fused_computation.6 | loop fusion | flops 6094848 | bytes 4060128 | tf_op jit(solution)/shard_map/concatenate | solution.py:45
  38.8 14.5 %all-to-all-done.1 = bf16[16,496,128]{2,1,0:T(8,128)(2,1)} async-done(((bf16[16,496,128]{2,1,0:T(8,128)(2,1)}), bf16[16,496,128]{2,1,0:T(8,128)(2,1)}, u32[]{:S(2)}, u32[]{:S(2)}) %all-to-all-start.1) | async-done | bytes 2031648 | tf_op jit(solution)/shard_map/all_to_all | solution.py:159
  53.4 9.7 %all-to-all-start = ((bf16[16,496,128]{2,1,0:T(8,128)(2,1)}), bf16[16,496,128]{2,1,0:T(8,128)(2,1)S(1)}, u32[]{:S(2)}, u32[]{:S(2)}) async-start(bf16[16,496,128]{2,1,0:T(8,128)(2,1)} %maximum_maximum_fusion), calls=%async_computation | async-start | bytes 4063232 | tf_op jit(solution)/shard_map/all_to_all | solution.py:161
  63.2 4.4 %collective-permute-done = bf16[16,496,128]{2,1,0:T(8,128)(2,1)} collective-permute-done((bf16[16,496,128]{2,1,0:T(8,128)(2,1)}, bf16[16,496,128]{2,1,0:T(8,128)(2,1)}, u32[]{:S(2)}, u32[]{:S(2)}) %collective-permute-start) | collective-permute-done | bytes 2031648 | tf_op jit(solution)/shard_map/ppermute | solution.py:167
  67.6 2.4 %broadcast_select_fusion.1 = (bf16[16,496,128]{2,1,0:T(8,128)(2,1)S(1)}, bf16[16,496,128]{2,1,0:T(8,128)(2,1)S(1)}) fusion(bf16[16,496,128]{2,1,0:T(8,128)(2,1)} %collective-permute-done, bf16[16,496,128]{2,1,0:T(8,128)(2,1)} %all-to-all-done.1, pred[]{:T(512)S(6)} %eq.9, pred[]{:T(512)S(6)} %eq.10), kind=kLoop, calls=%fused_computation.9 | loop fusion | flops 2031616 | bytes 8126466 | tf_op jit(solution)/shard_map/jit(_where)/select_n | solution.py:172
  70.0 2.2 %pad_maximum_fusion = bf16[32,496,128]{2,1,0:T(8,128)(2,1)} fusion(bf16[16,496,128]{2,1,0:T(8,128)(2,1)S(1)} %get-tuple-element.10, bf16[16,496,128]{2,1,0:T(8,128)(2,1)S(1)} %get-tuple-element.9), kind=kLoop, calls=%fused_computation.2 | loop fusion | flops 2031616 | bytes 8126464 | tf_op jit(solution)/shard_map/concatenate | solution.py:174
  72.2 32.2 %all-to-all-done = bf16[16,496,128]{2,1,0:T(8,128)(2,1)S(1)} async-done(((bf16[16,496,128]{2,1,0:T(8,128)(2,1)}), bf16[16,496,128]{2,1,0:T(8,128)(2,1)S(1)}, u32[]{:S(2)}, u32[]{:S(2)}) %all-to-all-start) | async-done | bytes 2031648 | tf_op jit(solution)/shard_map/all_to_all | solution.py:161
  104.5 3.3 %fusion = f32[16,32,1]{1,0,2:T(8,128)S(1)} fusion(bf16[32,496,128]{2,1,0:T(8,128)(2,1)} %pad_maximum_fusion, bf16[16,496,128]{2,1,0:T(8,128)(2,1)S(1)} %all-to-all-done), kind=kOutput, calls=%fused_computation.3 | convolution fusion | flops 65011712 | bytes 6096896 | tf_op jit(solution)/shard_map/dot_general | solution.py:175
  107.8 16.5 %all_to_all.19 = f32[16,1,32]{2,1,0:T(1,128)S(1)} all-to-all(f32[16,1,32]{2,1,0:T(1,128)S(1)} %bitcast.49), channel_id=1, replica_groups=mesh['rec'=2,'space'=16] {'space'}, dimensions={0} | all-to-all | bytes 4096 | tf_op jit(solution)/shard_map/all_to_all | solution.py:176
  124.3 0.5 reduce_sum.9
  (10 shorter events, 0.2 us)
Async XLA Ops:
  0.0 17.2 %copy-start = (bf16[120,120]{1,0:T(8,128)(2,1)S(1)}, bf16[120,120]{1,0:T(8,128)(2,1)}, u32[]{:S(2)}) copy-start(bf16[120,120]{1,0:T(8,128)(2,1)} %param.7) | copy-start | bytes 86404
  3.0 50.4 %all-to-all-start.1 = ((bf16[16,496,128]{2,1,0:T(8,128)(2,1)}), bf16[16,496,128]{2,1,0:T(8,128)(2,1)}, u32[]{:S(2)}, u32[]{:S(2)}) async-start(bf16[16,496,128]{2,1,0:T(8,128)(2,1)} %shard_map.46), calls=%async_computation.1 | async-start | bytes 4063232 | tf_op jit(solution)/shard_map/all_to_all | solution.py:159
  23.4 2.8 %copy-start.2 = (bf16[70,70]{1,0:T(8,128)(2,1)S(1)}, bf16[70,70]{1,0:T(8,128)(2,1)}, u32[]{:S(2)}) copy-start(bf16[70,70]{1,0:T(8,128)(2,1)} %param.6) | copy-start | bytes 29404
  32.0 1.5 %copy-start.1 = (bf16[120,120]{1,0:T(8,128)(2,1)S(1)}, bf16[120,120]{1,0:T(8,128)(2,1)}, u32[]{:S(2)}) copy-start(bf16[120,120]{1,0:T(8,128)(2,1)} %param.5) | copy-start | bytes 86404
  53.4 51.1 %all-to-all-start = ((bf16[16,496,128]{2,1,0:T(8,128)(2,1)}), bf16[16,496,128]{2,1,0:T(8,128)(2,1)S(1)}, u32[]{:S(2)}, u32[]{:S(2)}) async-start(bf16[16,496,128]{2,1,0:T(8,128)(2,1)} %maximum_maximum_fusion), calls=%async_computation | async-start | bytes 4063232 | tf_op jit(solution)/shard_map/all_to_all | solution.py:161
  63.1 4.5 %collective-permute-start = (bf16[16,496,128]{2,1,0:T(8,128)(2,1)}, bf16[16,496,128]{2,1,0:T(8,128)(2,1)}, u32[]{:S(2)}, u32[]{:S(2)}) collective-permute-start(bf16[16,496,128]{2,1,0:T(8,128)(2,1)} %all-to-all-done.1), channel_id=1, source_target_pairs={{0,16},{16,0},{1,17},{17,1},{2,18},{18,2},{3,19},{19,3},{4,20},{20... | collective-permute-start | bytes 6094856 | tf_op jit(solution)/shard_map/ppermute | solution.py:167

commit v14 on v10

--- a/solution.py
+++ b/solution.py
@@ -176,7 +176,8 @@
     everyone = jnp.concatenate(ordered, axis=0)
     partial_value = lax.dot_general(weighted_here, everyone, contract, preferred_element_type=jnp.float32)
     spread = lax.all_to_all(partial_value, "space", split_axis=0, concat_axis=0, tiled=True)
-    return jnp.sum(spread, axis=0, keepdims=True)
+    ones = jnp.ones((1, spread.shape[0]), jnp.float32)
+    return jnp.dot(ones, spread, precision=lax.Precision.HIGHEST, preferred_element_type=jnp.float32)
 
 
 def solution(mesh):

time: 125 us -> 125 us (level)
  no operation moved by 1% of the time
where the time goes in v14:
time: 125 us; the launch traced here: 124 us
  waiting for transfers between devices  51.1 us (41%)
  local copies, waits for them, and re-layouts  18.1 us (14%)
  starting transfers between devices  18.1 us (14%)
  blocking collectives  16.5 us (13%)
  matrix products  11.4 us (9%)
  other arithmetic  6.51 us (5%)
  Pallas kernels  2.51 us (2%)
    all_to_all x1, waiting for transfers between devices, local(): lax.all_to_all(weighted, 'space', split_axis=0, concat_axis=0, tiled=True)  32.2 us
    all_to_all x1, blocking collectives, local(): lax.all_to_all(partial_value, 'space', split_axis=0, concat_axis=0, tiled...  16.5 us
    all_to_all x1, waiting for transfers between devices, local(): lax.all_to_all(plain, 'space', split_axis=0, concat_axis=0, tiled=True)  14.5 us
    all_to_all x1, starting transfers between devices, local(): lax.all_to_all(weighted, 'space', split_axis=0, concat_axis=0, tiled=True)  9.71 us
    all_to_all x1, starting transfers between devices, local(): lax.all_to_all(plain, 'space', split_axis=0, concat_axis=0, tiled=True)  8.37 us
    reshape x1, local copies, waits for them, and re-layouts, weighted_dense_chunks(): footprint.reshape(time_count * lat_count, lon_count)  5.83 us
    ppermute x1, waiting for transfers between devices, local(): received.append(lax.ppermute(plain_here, 'rec', perm))  4.38 us
    convert_element_type x1, local copies, waits for them, and re-layouts, weighted_dense_chunks(): along_lon = jnp.dot(footprint.reshape(time_count * lat_count, lon_count),...  4.09 us
  transfers between devices with their start and end apart: 3, of which 3 were waited for; matrix products, arithmetic and copies ran while one was open for 26% of the time, Pallas kernels for 0%

profile of v14, /device:TPU:0, one launch (start us, length us, event | category | flops | bytes accessed | tf_op | source)
XLA Modules:
  0.0 124.5 jit_solution(8782646359186655945)
XLA Ops:
  0.0 2.5 %shard_map.46 = bf16[16,496,128]{2,1,0:T(8,128)(2,1)} custom-call(bf16[120,8400]{1,0:T(8,128)(2,1)} %bitcast.46), custom_call_target="tpu_custom_call" | custom-call | bytes 4063232 | tf_op jit(solution)/shard_map/pallas_call | solution.py:112
  2.5 8.4 %all-to-all-start.1 = ((bf16[16,496,128]{2,1,0:T(8,128)(2,1)}), bf16[16,496,128]{2,1,0:T(8,128)(2,1)}, u32[]{:S(2)}, u32[]{:S(2)}) async-start(bf16[16,496,128]{2,1,0:T(8,128)(2,1)} %shard_map.46), calls=%async_computation.1 | async-start | bytes 4063232 | tf_op jit(solution)/shard_map/all_to_all | solution.py:161
  10.9 5.8 %reshape.34 = bf16[8400,120]{1,0:T(8,128)(2,1)S(1)} reshape(bf16[120,8400]{1,0:T(8,128)(2,1)} %bitcast.47) | data formatting | bytes 4032000 | tf_op jit(solution)/shard_map/reshape | solution.py:135
  16.7 2.1 %convolution_convert_fusion = bf16[8400,120]{0,1:T(8,128)(2,1)} fusion(bf16[8400,120]{1,0:T(8,128)(2,1)S(1)} %reshape.34, bf16[120,120]{1,0:T(8,128)(2,1)S(1)} %copy-done), kind=kOutput, calls=%fused_computation | convolution fusion | flops 242928000 | bytes 4060800 | tf_op jit(solution)/shard_map/dot_general | solution.py:134
  18.9 4.1 %copy.20 = bf16[8400,120]{1,0:T(8,128)(2,1)} copy(bf16[8400,120]{0,1:T(8,128)(2,1)} %convolution_convert_fusion) | data formatting | bytes 4032000 | tf_op jit(solution)/shard_map/convert_element_type | solution.py:138
  23.0 2.8 %reshape.35 = bf16[120,70,120]{2,1,0:T(8,128)(2,1)S(1)} reshape(bf16[8400,120]{1,0:T(8,128)(2,1)} %copy.20) | data formatting | bytes 4032000 | tf_op jit(solution)/shard_map/reshape | solution.py:141
  25.8 2.1 %convert_bitcast_fusion = bf16[120,70,120]{2,1,0:T(8,128)(2,1)} fusion(bf16[120,70,120]{2,1,0:T(8,128)(2,1)S(1)} %reshape.35, bf16[70,70]{1,0:T(8,128)(2,1)S(1)} %copy-done.2), kind=kOutput, calls=%fused_computation.5 | convolution fusion | flops 142128000 | bytes 4041800 | tf_op jit(solution)/shard_map/tab,ac->tcb/dot_general | solution.py:139
  27.9 3.6 %copy.22 = bf16[120,70,120]{0,2,1:T(8,128)(2,1)S(1)} copy(bf16[120,70,120]{2,1,0:T(8,128)(2,1)} %convert_bitcast_fusion) | data formatting | bytes 4032000 | tf_op jit(solution)/shard_map/convert_element_type | solution.py:144
  31.5 1.5 %slice.17 = bf16[120,8192]{0,1:T(8,128)(2,1)} slice(bf16[120,8400]{0,1:T(8,128)(2,1)S(1)} %bitcast.42), slice={[0:120], [0:8192]} | slice | bytes 3932160 | tf_op jit(solution)/shard_map/slice | solution.py:146
  33.0 0.2 fusion.4
  33.2 0.1 copy.26
  33.3 0.7 fusion.3
  34.2 0.1 pad.9.clone
  34.2 2.3 %convolution_convert_fusion.2 = bf16[64,128,112]{1,2,0:T(8,128)(2,1)S(1)} fusion(bf16[120,64,128]{0,2,1:T(8,128)(2,1)} %bitcast.45, bf16[120,120]{1,0:T(8,128)(2,1)S(1)} %copy-done.1), kind=kOutput, calls=%fused_computation.10 | convolution fusion | flops 221118464 | bytes 3829888 | tf_op jit(solution)/shard_map/ts,tjl->jsl/dot_general | solution.py:147
  36.6 1.8 %maximum_maximum_fusion = bf16[16,496,128]{2,1,0:T(8,128)(2,1)} fusion(bf16[16,47,128]{2,1,0:T(8,128)(2,1)S(1)} %reshape.43, bf16[16,448,128]{2,1,0:T(8,128)(2,1)S(1)} %bitcast.48, bf16[496]{0:T(512)(128)(2,1)S(1)} %pad.9.clone), kind=kLoop, calls=%fused_computation.6 | loop fusion | flops 6094848 | bytes 4060128 | tf_op jit(solution)/shard_map/concatenate | solution.py:45
  38.4 14.5 %all-to-all-done.1 = bf16[16,496,128]{2,1,0:T(8,128)(2,1)} async-done(((bf16[16,496,128]{2,1,0:T(8,128)(2,1)}), bf16[16,496,128]{2,1,0:T(8,128)(2,1)}, u32[]{:S(2)}, u32[]{:S(2)}) %all-to-all-start.1) | async-done | bytes 2031648 | tf_op jit(solution)/shard_map/all_to_all | solution.py:161
  52.9 9.7 %all-to-all-start = ((bf16[16,496,128]{2,1,0:T(8,128)(2,1)}), bf16[16,496,128]{2,1,0:T(8,128)(2,1)S(1)}, u32[]{:S(2)}, u32[]{:S(2)}) async-start(bf16[16,496,128]{2,1,0:T(8,128)(2,1)} %maximum_maximum_fusion), calls=%async_computation | async-start | bytes 4063232 | tf_op jit(solution)/shard_map/all_to_all | solution.py:163
  62.7 4.4 %collective-permute-done = bf16[16,496,128]{2,1,0:T(8,128)(2,1)} collective-permute-done((bf16[16,496,128]{2,1,0:T(8,128)(2,1)}, bf16[16,496,128]{2,1,0:T(8,128)(2,1)}, u32[]{:S(2)}, u32[]{:S(2)}) %collective-permute-start) | collective-permute-done | bytes 2031648 | tf_op jit(solution)/shard_map/ppermute | solution.py:169
  67.1 2.4 %broadcast_select_fusion.1 = (bf16[16,496,128]{2,1,0:T(8,128)(2,1)S(1)}, bf16[16,496,128]{2,1,0:T(8,128)(2,1)S(1)}) fusion(bf16[16,496,128]{2,1,0:T(8,128)(2,1)} %collective-permute-done, bf16[16,496,128]{2,1,0:T(8,128)(2,1)} %all-to-all-done.1, pred[]{:T(512)S(6)} %eq.9, pred[]{:T(512)S(6)} %eq.10), kind=kLoop, calls=%fused_computation.9 | loop fusion | flops 2031616 | bytes 8126466 | tf_op jit(solution)/shard_map/jit(_where)/select_n | solution.py:174
  69.5 2.3 %pad_maximum_fusion = bf16[32,496,128]{2,1,0:T(8,128)(2,1)} fusion(bf16[16,496,128]{2,1,0:T(8,128)(2,1)S(1)} %get-tuple-element.10, bf16[16,496,128]{2,1,0:T(8,128)(2,1)S(1)} %get-tuple-element.9), kind=kLoop, calls=%fused_computation.2 | loop fusion | flops 2031616 | bytes 8126464 | tf_op jit(solution)/shard_map/concatenate | solution.py:176
  71.8 32.2 %all-to-all-done = bf16[16,496,128]{2,1,0:T(8,128)(2,1)S(1)} async-done(((bf16[16,496,128]{2,1,0:T(8,128)(2,1)}), bf16[16,496,128]{2,1,0:T(8,128)(2,1)S(1)}, u32[]{:S(2)}, u32[]{:S(2)}) %all-to-all-start) | async-done | bytes 2031648 | tf_op jit(solution)/shard_map/all_to_all | solution.py:163
  104.0 3.3 %fusion = f32[16,32,1]{1,0,2:T(8,128)S(1)} fusion(bf16[32,496,128]{2,1,0:T(8,128)(2,1)} %pad_maximum_fusion, bf16[16,496,128]{2,1,0:T(8,128)(2,1)S(1)} %all-to-all-done), kind=kOutput, calls=%fused_computation.3 | convolution fusion | flops 65011712 | bytes 6096896 | tf_op jit(solution)/shard_map/dot_general | solution.py:177
  107.3 16.5 %all_to_all.22 = f32[16,1,32]{2,1,0:T(1,128)S(1)} all-to-all(f32[16,1,32]{2,1,0:T(1,128)S(1)} %bitcast.52), channel_id=1, replica_groups=mesh['rec'=2,'space'=16] {'space'}, dimensions={0} | all-to-all | bytes 4096 | tf_op jit(solution)/shard_map/all_to_all | solution.py:178
  123.8 0.6 fusion.10
  (10 shorter events, 0.2 us)
Async XLA Ops:
  0.0 16.7 %copy-start = (bf16[120,120]{1,0:T(8,128)(2,1)S(1)}, bf16[120,120]{1,0:T(8,128)(2,1)}, u32[]{:S(2)}) copy-start(bf16[120,120]{1,0:T(8,128)(2,1)} %param.7) | copy-start | bytes 86404
  2.5 50.4 %all-to-all-start.1 = ((bf16[16,496,128]{2,1,0:T(8,128)(2,1)}), bf16[16,496,128]{2,1,0:T(8,128)(2,1)}, u32[]{:S(2)}, u32[]{:S(2)}) async-start(bf16[16,496,128]{2,1,0:T(8,128)(2,1)} %shard_map.46), calls=%async_computation.1 | async-start | bytes 4063232 | tf_op jit(solution)/shard_map/all_to_all | solution.py:161
  23.0 2.8 %copy-start.2 = (bf16[70,70]{1,0:T(8,128)(2,1)S(1)}, bf16[70,70]{1,0:T(8,128)(2,1)}, u32[]{:S(2)}) copy-start(bf16[70,70]{1,0:T(8,128)(2,1)} %param.6) | copy-start | bytes 29404
  31.5 1.5 %copy-start.1 = (bf16[120,120]{1,0:T(8,128)(2,1)S(1)}, bf16[120,120]{1,0:T(8,128)(2,1)}, u32[]{:S(2)}) copy-start(bf16[120,120]{1,0:T(8,128)(2,1)} %param.5) | copy-start | bytes 86404
  52.9 51.1 %all-to-all-start = ((bf16[16,496,128]{2,1,0:T(8,128)(2,1)}), bf16[16,496,128]{2,1,0:T(8,128)(2,1)S(1)}, u32[]{:S(2)}, u32[]{:S(2)}) async-start(bf16[16,496,128]{2,1,0:T(8,128)(2,1)} %maximum_maximum_fusion), calls=%async_computation | async-start | bytes 4063232 | tf_op jit(solution)/shard_map/all_to_all | solution.py:163
  62.6 4.5 %collective-permute-start = (bf16[16,496,128]{2,1,0:T(8,128)(2,1)}, bf16[16,496,128]{2,1,0:T(8,128)(2,1)}, u32[]{:S(2)}, u32[]{:S(2)}) collective-permute-start(bf16[16,496,128]{2,1,0:T(8,128)(2,1)} %all-to-all-done.1), channel_id=1, source_target_pairs={{0,16},{16,0},{1,17},{17,1},{2,18},{18,2},{3,19},{19,3},{4,20},{20... | collective-permute-start | bytes 6094856 | tf_op jit(solution)/shard_map/ppermute | solution.py:169

commit v15 on v10

--- a/solution.py
+++ b/solution.py
@@ -50,7 +50,7 @@
     chunks, rows, _ = out_hbm.shape
     main_tiles = chunks * per
     main_cols = main_tiles * LANE
-    groups = 4 if chunks % 4 == 0 else 1
+    groups = 2 if chunks % 2 == 0 else 1
     width = main_cols // groups
     loads = []
     for g in range(groups):

time: 125 us -> 125 us (level)
  no operation moved by 1% of the time
where the time goes in v15:
time: 125 us
  waiting for transfers between devices  51.1 us (41%)
  local copies, waits for them, and re-layouts  18.1 us (14%)
  starting transfers between devices  18.1 us (14%)
  blocking collectives  16.5 us (13%)
  matrix products  10.8 us (9%)
  other arithmetic  7.05 us (6%)
  Pallas kernels  2.76 us (2%)
    all_to_all x1, waiting for transfers between devices, local(): lax.all_to_all(weighted, 'space', split_axis=0, concat_axis=0, tiled=True)  32.2 us
    all_to_all x1, blocking collectives, local(): lax.all_to_all(partial_value, 'space', split_axis=0, concat_axis=0, tiled...  16.5 us
    all_to_all x1, waiting for transfers between devices, local(): lax.all_to_all(plain, 'space', split_axis=0, concat_axis=0, tiled=True)  14.5 us
    all_to_all x1, starting transfers between devices, local(): lax.all_to_all(weighted, 'space', split_axis=0, concat_axis=0, tiled=True)  9.71 us
    all_to_all x1, starting transfers between devices, local(): lax.all_to_all(plain, 'space', split_axis=0, concat_axis=0, tiled=True)  8.37 us
    reshape x1, local copies, waits for them, and re-layouts, weighted_dense_chunks(): footprint.reshape(time_count * lat_count, lon_count)  5.83 us
    ppermute x1, waiting for transfers between devices, local(): received.append(lax.ppermute(plain_here, 'rec', perm))  4.38 us
    convert_element_type x1, local copies, waits for them, and re-layouts, weighted_dense_chunks(): along_lon = jnp.dot(footprint.reshape(time_count * lat_count, lon_count),...  4.09 us
  transfers between devices with their start and end apart: 3, of which 3 were waited for; matrix products, arithmetic and copies ran while one was open for 26% of the time, Pallas kernels for 0%

profile of v15, /device:TPU:0, one launch (start us, length us, event | category | flops | bytes accessed | tf_op | source)
XLA Modules:
  0.0 124.6 jit_solution(11021918220398543874)
XLA Ops:
  0.0 2.8 %shard_map.46 = bf16[16,496,128]{2,1,0:T(8,128)(2,1)} custom-call(bf16[120,8400]{1,0:T(8,128)(2,1)} %bitcast.44), custom_call_target="tpu_custom_call" | custom-call | bytes 4063232 | tf_op jit(solution)/shard_map/pallas_call | solution.py:112
  2.8 8.4 %all-to-all-start.1 = ((bf16[16,496,128]{2,1,0:T(8,128)(2,1)}), bf16[16,496,128]{2,1,0:T(8,128)(2,1)}, u32[]{:S(2)}, u32[]{:S(2)}) async-start(bf16[16,496,128]{2,1,0:T(8,128)(2,1)} %shard_map.46), calls=%async_computation.1 | async-start | bytes 4063232 | tf_op jit(solution)/shard_map/all_to_all | solution.py:161
  11.1 5.8 %reshape.32 = bf16[8400,120]{1,0:T(8,128)(2,1)S(1)} reshape(bf16[120,8400]{1,0:T(8,128)(2,1)} %bitcast.45) | data formatting | bytes 4032000 | tf_op jit(solution)/shard_map/reshape | solution.py:135
  17.0 2.1 %convolution_convert_fusion = bf16[8400,120]{0,1:T(8,128)(2,1)} fusion(bf16[8400,120]{1,0:T(8,128)(2,1)S(1)} %reshape.32, bf16[120,120]{1,0:T(8,128)(2,1)S(1)} %copy-done), kind=kOutput, calls=%fused_computation | convolution fusion | flops 242928000 | bytes 4060800 | tf_op jit(solution)/shard_map/dot_general | solution.py:134
  19.1 4.1 %copy.20 = bf16[8400,120]{1,0:T(8,128)(2,1)} copy(bf16[8400,120]{0,1:T(8,128)(2,1)} %convolution_convert_fusion) | data formatting | bytes 4032000 | tf_op jit(solution)/shard_map/convert_element_type | solution.py:138
  23.2 2.8 %reshape.33 = bf16[120,70,120]{2,1,0:T(8,128)(2,1)S(1)} reshape(bf16[8400,120]{1,0:T(8,128)(2,1)} %copy.20) | data formatting | bytes 4032000 | tf_op jit(solution)/shard_map/reshape | solution.py:141
  26.0 2.1 %convert_bitcast_fusion = bf16[120,70,120]{2,1,0:T(8,128)(2,1)} fusion(bf16[120,70,120]{2,1,0:T(8,128)(2,1)S(1)} %reshape.33, bf16[70,70]{1,0:T(8,128)(2,1)S(1)} %copy-done.2), kind=kOutput, calls=%fused_computation.5 | convolution fusion | flops 142128000 | bytes 4041800 | tf_op jit(solution)/shard_map/tab,ac->tcb/dot_general | solution.py:139
  28.2 3.6 %copy.22 = bf16[120,70,120]{0,2,1:T(8,128)(2,1)S(1)} copy(bf16[120,70,120]{2,1,0:T(8,128)(2,1)} %convert_bitcast_fusion) | data formatting | bytes 4032000 | tf_op jit(solution)/shard_map/convert_element_type | solution.py:144
  31.8 1.5 %slice.17 = bf16[120,8192]{0,1:T(8,128)(2,1)} slice(bf16[120,8400]{0,1:T(8,128)(2,1)S(1)} %bitcast.40), slice={[0:120], [0:8192]} | slice | bytes 3932160 | tf_op jit(solution)/shard_map/slice | solution.py:146
  33.2 0.2 fusion.4
  33.4 0.1 copy.26
  33.5 0.7 fusion.3
  34.4 0.1 pad.9.clone
  34.5 2.3 %convolution_convert_fusion.2 = bf16[64,128,112]{1,2,0:T(8,128)(2,1)S(1)} fusion(bf16[120,64,128]{0,2,1:T(8,128)(2,1)} %bitcast.43, bf16[120,120]{1,0:T(8,128)(2,1)S(1)} %copy-done.1), kind=kOutput, calls=%fused_computation.10 | convolution fusion | flops 221118464 | bytes 3829888 | tf_op jit(solution)/shard_map/ts,tjl->jsl/dot_general | solution.py:147
  36.8 1.8 %maximum_maximum_fusion = bf16[16,496,128]{2,1,0:T(8,128)(2,1)} fusion(bf16[16,47,128]{2,1,0:T(8,128)(2,1)S(1)} %reshape.41, bf16[16,448,128]{2,1,0:T(8,128)(2,1)S(1)} %bitcast.46, bf16[496]{0:T(512)(128)(2,1)S(1)} %pad.9.clone), kind=kLoop, calls=%fused_computation.6 | loop fusion | flops 6094848 | bytes 4060128 | tf_op jit(solution)/shard_map/concatenate | solution.py:45
  38.6 14.5 %all-to-all-done.1 = bf16[16,496,128]{2,1,0:T(8,128)(2,1)} async-done(((bf16[16,496,128]{2,1,0:T(8,128)(2,1)}), bf16[16,496,128]{2,1,0:T(8,128)(2,1)}, u32[]{:S(2)}, u32[]{:S(2)}) %all-to-all-start.1) | async-done | bytes 2031648 | tf_op jit(solution)/shard_map/all_to_all | solution.py:161
  53.2 9.7 %all-to-all-start = ((bf16[16,496,128]{2,1,0:T(8,128)(2,1)}), bf16[16,496,128]{2,1,0:T(8,128)(2,1)S(1)}, u32[]{:S(2)}, u32[]{:S(2)}) async-start(bf16[16,496,128]{2,1,0:T(8,128)(2,1)} %maximum_maximum_fusion), calls=%async_computation | async-start | bytes 4063232 | tf_op jit(solution)/shard_map/all_to_all | solution.py:163
  63.0 4.4 %collective-permute-done = bf16[16,496,128]{2,1,0:T(8,128)(2,1)} collective-permute-done((bf16[16,496,128]{2,1,0:T(8,128)(2,1)}, bf16[16,496,128]{2,1,0:T(8,128)(2,1)}, u32[]{:S(2)}, u32[]{:S(2)}) %collective-permute-start) | collective-permute-done | bytes 2031648 | tf_op jit(solution)/shard_map/ppermute | solution.py:169
  67.3 2.4 %broadcast_select_fusion.1 = (bf16[16,496,128]{2,1,0:T(8,128)(2,1)S(1)}, bf16[16,496,128]{2,1,0:T(8,128)(2,1)S(1)}) fusion(bf16[16,496,128]{2,1,0:T(8,128)(2,1)} %collective-permute-done, bf16[16,496,128]{2,1,0:T(8,128)(2,1)} %all-to-all-done.1, pred[]{:T(512)S(6)} %eq.9, pred[]{:T(512)S(6)} %eq.10), kind=kLoop, calls=%fused_computation.9 | loop fusion | flops 2031616 | bytes 8126466 | tf_op jit(solution)/shard_map/jit(_where)/select_n | solution.py:174
  69.8 2.2 %pad_maximum_fusion = bf16[32,496,128]{2,1,0:T(8,128)(2,1)} fusion(bf16[16,496,128]{2,1,0:T(8,128)(2,1)S(1)} %get-tuple-element.10, bf16[16,496,128]{2,1,0:T(8,128)(2,1)S(1)} %get-tuple-element.9), kind=kLoop, calls=%fused_computation.2 | loop fusion | flops 2031616 | bytes 8126464 | tf_op jit(solution)/shard_map/concatenate | solution.py:176
  72.0 32.2 %all-to-all-done = bf16[16,496,128]{2,1,0:T(8,128)(2,1)S(1)} async-done(((bf16[16,496,128]{2,1,0:T(8,128)(2,1)}), bf16[16,496,128]{2,1,0:T(8,128)(2,1)S(1)}, u32[]{:S(2)}, u32[]{:S(2)}) %all-to-all-start) | async-done | bytes 2031648 | tf_op jit(solution)/shard_map/all_to_all | solution.py:163
  104.2 3.3 %fusion = f32[16,32,1]{1,0,2:T(8,128)S(1)} fusion(bf16[32,496,128]{2,1,0:T(8,128)(2,1)} %pad_maximum_fusion, bf16[16,496,128]{2,1,0:T(8,128)(2,1)S(1)} %all-to-all-done), kind=kOutput, calls=%fused_computation.3 | convolution fusion | flops 65011712 | bytes 6096896 | tf_op jit(solution)/shard_map/dot_general | solution.py:177
  107.5 16.5 %all_to_all.19 = f32[16,1,32]{2,1,0:T(1,128)S(1)} all-to-all(f32[16,1,32]{2,1,0:T(1,128)S(1)} %bitcast.49), channel_id=1, replica_groups=mesh['rec'=2,'space'=16] {'space'}, dimensions={0} | all-to-all | bytes 4096 | tf_op jit(solution)/shard_map/all_to_all | solution.py:178
  124.1 0.5 reduce_sum.9
  (10 shorter events, 0.2 us)
Async XLA Ops:
  0.0 17.0 %copy-start = (bf16[120,120]{1,0:T(8,128)(2,1)S(1)}, bf16[120,120]{1,0:T(8,128)(2,1)}, u32[]{:S(2)}) copy-start(bf16[120,120]{1,0:T(8,128)(2,1)} %param.7) | copy-start | bytes 86404
  2.8 50.4 %all-to-all-start.1 = ((bf16[16,496,128]{2,1,0:T(8,128)(2,1)}), bf16[16,496,128]{2,1,0:T(8,128)(2,1)}, u32[]{:S(2)}, u32[]{:S(2)}) async-start(bf16[16,496,128]{2,1,0:T(8,128)(2,1)} %shard_map.46), calls=%async_computation.1 | async-start | bytes 4063232 | tf_op jit(solution)/shard_map/all_to_all | solution.py:161
  23.2 2.8 %copy-start.2 = (bf16[70,70]{1,0:T(8,128)(2,1)S(1)}, bf16[70,70]{1,0:T(8,128)(2,1)}, u32[]{:S(2)}) copy-start(bf16[70,70]{1,0:T(8,128)(2,1)} %param.6) | copy-start | bytes 29404
  31.8 1.5 %copy-start.1 = (bf16[120,120]{1,0:T(8,128)(2,1)S(1)}, bf16[120,120]{1,0:T(8,128)(2,1)}, u32[]{:S(2)}) copy-start(bf16[120,120]{1,0:T(8,128)(2,1)} %param.5) | copy-start | bytes 86404
  53.2 51.1 %all-to-all-start = ((bf16[16,496,128]{2,1,0:T(8,128)(2,1)}), bf16[16,496,128]{2,1,0:T(8,128)(2,1)S(1)}, u32[]{:S(2)}, u32[]{:S(2)}) async-start(bf16[16,496,128]{2,1,0:T(8,128)(2,1)} %maximum_maximum_fusion), calls=%async_computation | async-start | bytes 4063232 | tf_op jit(solution)/shard_map/all_to_all | solution.py:163
  62.9 4.5 %collective-permute-start = (bf16[16,496,128]{2,1,0:T(8,128)(2,1)}, bf16[16,496,128]{2,1,0:T(8,128)(2,1)}, u32[]{:S(2)}, u32[]{:S(2)}) collective-permute-start(bf16[16,496,128]{2,1,0:T(8,128)(2,1)} %all-to-all-done.1), channel_id=1, source_target_pairs={{0,16},{16,0},{1,17},{17,1},{2,18},{18,2},{3,19},{19,3},{4,20},{20... | collective-permute-start | bytes 6094856 | tf_op jit(solution)/shard_map/ppermute | solution.py:169
